TPU v7x, 256 devices: a whole 4x4x8 slice. The times are simulated.
256 devices in a mesh: req: 32 (over x, z), kv: 8 (over y, core).
Axes of the slice: x: 4, y: 4, z: 8, core: 2. Of those that a mesh axis runs over, the one named last changes fastest.
Arguments:
- states: bfloat16 [256, 2560], P(('req', 'kv')), may hold values from -6 to 6
- norm_gain: bfloat16 [2560], replicated, may hold values from 0.099609375 to 1.8984375
- w_query: bfloat16 [2560, 2560], P(None, 'kv'), may hold values from -0.125 to 0.125
- key_projection_weight: bfloat16 [2560, 640], P(None, 'kv'), may hold values from -0.125 to 0.125
- value_projection_weight: bfloat16 [2560, 640], P(None, 'kv'), may hold values from -0.125 to 0.125
- cache_keys: bfloat16 [256, 8, 80, 4096], P('req', 'kv')
- value_cache_slots: bfloat16 [256, 8, 80, 4096], P('req', 'kv'), may hold values from -6 to 6
- lengths: int32 [256], P('req'), may hold values from 1 to 16383, as said below
- write_pos: int32 [256], P('req'), may hold values from 0 to 4095, as said below
- dealing: int32 [256], replicated, may hold values from 0 to 255, each once
Outputs:
- context: bfloat16 [256, 2560], P(('req', 'kv'))
Inputs may be any that keep to these rules, and one draw needn't show every extreme that they name: `lengths`: largest value is reached by some request in every draw. write_pos equals lengths modulo 4096. `dealing`: A permutation of the requests.
All inputs are finite; a program needn't handle non-finite values.
Results may differ from a plain program's by a relative error of at most 0.022.
The roundings to bfloat16 on the way count: a program that leaves them out, or rounds other values in their place, can miss the bound.
Values may be sent and summed in bfloat16 or wider, within the bound.
No kernel may reach another device: no remote copies, remote signals or barrier semaphores. Data moves between devices by JAX's collectives and lax.ppermute only.
A program may use at most 64 MiB of HBM per device.

v0:
```python
import jax
import jax.numpy as jnp
from jax import lax
from jax.sharding import PartitionSpec as P

HEAD_DIMENSION = 80


def apply_rotary(tensor, positions):
    half_width = tensor.shape[-1] // 2
    frequency = 10000.0 ** (-(jnp.arange(half_width, dtype=jnp.float32) * 2.0 / tensor.shape[-1]))
    angles = positions.astype(jnp.float32)[:, None] * frequency[None, :]
    cosine = jnp.cos(angles)[:, None, :]
    sine_part = jnp.sin(angles)[:, None, :]
    front_half = tensor[..., :half_width]
    back_half = tensor[..., half_width:]
    return jnp.concatenate(
        [front_half * cosine - back_half * sine_part, back_half * cosine + front_half * sine_part],
        axis=-1,
    )


def local(
    states,
    norm_gain,
    w_query,
    key_projection_weight,
    value_projection_weight,
    cache_keys,
    value_cache_slots,
    lengths,
    write_pos,
    dealing,
):
    kv_count = lax.axis_size("kv")
    per_device = states.shape[0]
    group_rows = per_device * kv_count
    group_index = lax.axis_index("req")
    kv_index = lax.axis_index("kv")
    total_rows = dealing.shape[0]
    dealt_ids = lax.dynamic_slice_in_dim(dealing, group_index * group_rows, group_rows)
    all_rows = lax.all_gather(states, ("req", "kv"), axis=0, tiled=True)
    dealt_rows = jnp.take(all_rows, dealt_ids, axis=0)
    wide_rows = dealt_rows.astype(jnp.float32)
    inv_rms = lax.rsqrt(jnp.mean(wide_rows * wide_rows, axis=1, keepdims=True) + 1e-05)
    normalized_input = (wide_rows * inv_rms * norm_gain.astype(jnp.float32)[None, :]).astype(
        jnp.bfloat16
    )
    head_size = HEAD_DIMENSION
    heads_dev = key_projection_weight.shape[1] // head_size
    queries_per_group = w_query.shape[1] // key_projection_weight.shape[1]
    window_size = cache_keys.shape[3]
    query_vectors = jnp.dot(normalized_input, w_query, preferred_element_type=jnp.float32).reshape(
        group_rows, heads_dev * queries_per_group, head_size
    )
    query_vectors = (
        apply_rotary(query_vectors, lengths)
        .astype(jnp.bfloat16)
        .reshape(group_rows, heads_dev, queries_per_group, head_size)
    )
    fresh_key_rows = jnp.dot(
        normalized_input, key_projection_weight, preferred_element_type=jnp.float32
    ).reshape(group_rows, heads_dev, head_size)
    fresh_key_rows = apply_rotary(fresh_key_rows, lengths).astype(jnp.bfloat16)
    fresh_value_rows = (
        jnp.dot(normalized_input, value_projection_weight, preferred_element_type=jnp.float32)
        .astype(jnp.bfloat16)
        .reshape(group_rows, heads_dev, head_size)
    )
    score_scale = 1.0 / head_size**0.5
    scores = (
        jnp.einsum("rkgh,rkhw->rkgw", query_vectors, cache_keys, preferred_element_type=jnp.float32)
        * score_scale
    )
    own_score = (
        jnp.einsum(
            "rkgh,rkh->rkg", query_vectors, fresh_key_rows, preferred_element_type=jnp.float32
        )
        * score_scale
    )
    slot_ids = lax.broadcasted_iota(jnp.int32, (group_rows, 1, 1, window_size), 3)
    at_write = slot_ids == write_pos[:, None, None, None]
    scores = jnp.where(at_write, own_score[..., None], scores)
    scores = jnp.where(slot_ids <= lengths[:, None, None, None], scores, -jnp.inf)
    row_max = jnp.max(scores, axis=-1, keepdims=True)
    expd = jnp.exp(scores - row_max)
    softmax_weights = (expd / jnp.sum(expd, axis=-1, keepdims=True)).astype(jnp.bfloat16)
    stale_weights = jnp.where(at_write, jnp.zeros((), jnp.bfloat16), softmax_weights)
    fresh_weight = jnp.sum(
        jnp.where(at_write, softmax_weights, jnp.zeros((), jnp.bfloat16)).astype(jnp.float32),
        axis=-1,
    )
    mixed = jnp.einsum(
        "rkgw,rkhw->rkgh", stale_weights, value_cache_slots, preferred_element_type=jnp.float32
    )
    mixed = mixed + fresh_weight[..., None] * fresh_value_rows[:, :, None, :].astype(jnp.float32)
    attended = mixed.reshape(group_rows, heads_dev * queries_per_group * head_size).astype(
        jnp.bfloat16
    )
    inverse = jnp.zeros((total_rows,), jnp.int32).at[dealing].set(jnp.arange(total_rows))
    request_rows = lax.all_to_all(attended, "kv", split_axis=0, concat_axis=1, tiled=True)
    all_context = lax.all_gather(request_rows, ("req", "kv"), axis=0, tiled=True)
    own_ids = lax.dynamic_slice_in_dim(
        inverse, (group_index * kv_count + kv_index) * per_device, per_device
    )
    result = jnp.take(all_context, own_ids, axis=0)
    return result


def solution(mesh):
    in_specs = (
        P(("req", "kv"), None),
        P(),
        P(None, "kv"),
        P(None, "kv"),
        P(None, "kv"),
        P("req", "kv", None, None),
        P("req", "kv", None, None),
        P("req"),
        P("req"),
        P(),
    )
    out_specs = P(("req", "kv"), None)
    return jax.shard_map(local, mesh=mesh, in_specs=in_specs, out_specs=out_specs, check_vma=False)
```

profile of v0, /device:TPU:1, one launch (start us, length us, event | category | flops | bytes accessed | tf_op | source)
XLA Modules:
  0.0 256.5 jit_solution(114267257454325564)
XLA Ops:
  6.5 0.0 copy-start
  6.5 0.0 all-gather.5.cloned.1.call-start
  6.5 0.7 all-gather.5.cloned.1.call-update
  7.3 0.0 all-gather.7.cloned.1.call-start
  7.3 0.7 convert_element_type.52
  8.0 0.7 convert_element_type.50
  8.7 0.8 compare_and_fusion
  9.4 0.1 multiply_cosine_fusion.1
  9.6 0.8 iota_compare_fusion
  10.3 109.8 %all-gather.5.cloned.1.call-done = bf16[256,1,2560]{2,1,0:T(2,128)(2,1)} async-done(((bf16[1,1,2560]{2,1,0:T(2,128)(2,1)}), bf16[256,1,2560]{2,1,0:T(2,128)(2,1)}) %all-gather.5.cloned.1.call-update) | async-done | bytes 1310736 | tf_op jit(solution)/shard_map/all_gather | solution.py:42
  120.1 1.9 copy.19
  122.0 0.6 gather_fusion
  122.6 0.2 fusion.26
  122.8 1.3 convolution_bitcast_fusion
  124.1 0.1 fusion.41
  124.2 1.3 fusion.22
  125.5 0.0 copy-done
  125.5 0.5 fusion.47
  126.0 0.1 reshape.261
  126.1 0.1 maximum_bitcast_fusion
  126.2 0.1 subtract_convert_fusion
  126.3 0.2 fusion.38
  126.5 0.0 copy-start.1
  126.5 3.7 %fusion.49 = (f32[8,4]{1,0:T(8,128)S(1)}, f32[8,4,4096]{2,1,0:T(4,128)S(1)}) fusion(bf16[8,1,80,4096]{3,2,1,0:T(8,128)(2,1)} %param.15, f32[8,4]{1,0:T(8,128)S(1)} %broadcast_multiply_fusion, pred[8,4096]{1,0:T(8,128)(4,1)S(1)} %get-tuple-element.28, pred[8,4096]{1,0:T(8,128)(4,1)S(1)} %get-tuple-element.29, bf16[8,4,40]{2,1,0:T(4,128)(2,1)S(1)} %get-tuple-element.21, ...), kind=kOutput, calls=%fused_computation.64 | convolution fusion | flops 21641216 | bytes 5838080 | tf_op jit(solution)/shard_map/sub | solution.py:86
  130.2 0.4 convert_reduce_fusion
  130.5 3.9 %fusion.19 = bf16[8,4,80]{2,1,0:T(4,128)(2,1)S(1)} fusion(bf16[8,1,80,4096]{3,2,1,0:T(8,128)(2,1)} %param.16, bf16[8,4,4096]{2,1,0:T(4,128)(2,1)S(1)} %get-tuple-element.17, pred[8,4096]{1,0:T(8,128)(4,1)S(1)} %get-tuple-element.29, f32[8,80]{1,0:T(8,128)S(1)} %fusion.22, f32[8,4]{1,0:T(8,128)S(1)} %get-tuple-element.16), kind=kOutput, calls=%fused_computation.14 | convolution fusion | flops 21110272 | bytes 5545600 | tf_op jit(solution)/shard_map/rkgw,rkhw->rkgh/dot_general | solution.py:93
  134.5 0.1 convert_element_type.59
  134.6 0.5 broadcast.209
  135.1 0.7 reduce.7
  135.8 0.1 reshape.323
  135.9 8.8 %all_to_all.13 = bf16[8,2,160]{2,1,0:T(2,128)(2,1)S(1)} all-to-all(bf16[8,2,160]{2,1,0:T(2,128)(2,1)S(1)} %reshape.323), channel_id=1, replica_groups=mesh['req'=32,'kv'=8] {'kv'}, dimensions={0} | all-to-all | bytes 10240 | tf_op jit(solution)/shard_map/all_to_all | solution.py:101
  144.7 0.1 reshape.324
  144.9 0.7 reshape.311
  145.5 0.0 all-gather.7.cloned.1.call-update
  145.6 0.0 copy-done.1
  145.6 1.4 scatter_custom_fusion
  147.0 0.7 dynamic_slice.6
  149.6 98.7 %all-gather.7.cloned.1.call-done = bf16[256,1,2560]{2,1,0:T(2,128)(2,1)} async-done(((bf16[1,1,2560]{2,1,0:T(2,128)(2,1)}), bf16[256,1,2560]{2,1,0:T(2,128)(2,1)}) %all-gather.7.cloned.1.call-update) | async-done | bytes 1310736 | tf_op jit(solution)/shard_map/all_gather | solution.py:102
  248.3 1.3 fusion.29
  (7 shorter events, 0.1 us)
Async XLA Ops:
  6.5 119.0 %copy-start = (bf16[2560,320]{0,1:T(8,128)(2,1)S(1)}, bf16[2560,320]{0,1:T(8,128)(2,1)}, u32[]{:S(2)}) copy-start(bf16[2560,320]{0,1:T(8,128)(2,1)} %param.12) | copy-start | bytes 4915204
  6.5 113.6 %all-gather.5.cloned.1.call-start = ((), (), s32[]{:S(2)}) async-start(), calls=%async_computation.1 | async-start | bytes 2631680 | tf_op jit(solution)/shard_map/all_gather | solution.py:42
  7.3 241.1 %all-gather.7.cloned.1.call-start = ((), (), s32[]{:S(2)}) async-start(), calls=%async_computation.2 | async-start | bytes 2631680 | tf_op jit(solution)/shard_map/all_gather | solution.py:102
  126.5 19.1 %copy-start.1 = (s32[256]{0:T(256)S(1)}, s32[256]{0:T(256)}, u32[]{:S(2)}) copy-start(s32[256]{0:T(256)} %param.19) | copy-start | bytes 3076
Sparse Core Ops, SparseCore 0:
  11.0 109.0 all-gather.4
  145.7 102.5 all-gather.6
where the time goes:
time: 257 us; the launch traced here: 256 us
  waiting for transfers between devices  209 us (81%)
  between operations  15.4 us (6%)
  matrix products  10.9 us (4%)
  blocking collectives  8.83 us (3%)
  local copies, waits for them, and re-layouts  6.11 us (2%)
  other arithmetic  5.97 us (2%)
    all_gather x1, waiting for transfers between devices, local(): all_rows = lax.all_gather(states, ('req', 'kv'), axis=0, tiled=True)  110 us
    all_gather x1, waiting for transfers between devices, local(): lax.all_gather(request_rows, ('req', 'kv'), axis=0, tiled=True)  98.7 us
    all_to_all x1, blocking collectives, local(): lax.all_to_all(attended, 'kv', split_axis=0, concat_axis=1, tiled=True)  8.83 us
  transfers between devices with their start and end apart: 2, of which 2 were waited for; matrix products, arithmetic and copies ran while one was open for 2% of the time, Pallas kernels for 0%

commit v1 on v0

--- a/solution.py
+++ b/solution.py
@@ -37,10 +37,13 @@
     group_rows = per_device * kv_count
     group_index = lax.axis_index("req")
     kv_index = lax.axis_index("kv")
-    total_rows = dealing.shape[0]
+    req_count = lax.axis_size("req")
     dealt_ids = lax.dynamic_slice_in_dim(dealing, group_index * group_rows, group_rows)
-    all_rows = lax.all_gather(states, ("req", "kv"), axis=0, tiled=True)
-    dealt_rows = jnp.take(all_rows, dealt_ids, axis=0)
+    column_rows = lax.all_gather(states, "req", axis=0, tiled=True)
+    column_ids = jnp.arange(req_count, dtype=jnp.int32) * kv_count + kv_index
+    pick_in = (dealt_ids[:, None] == column_ids[None, :]).astype(jnp.bfloat16)
+    own_part = jnp.dot(pick_in, column_rows, preferred_element_type=jnp.float32).astype(jnp.bfloat16)
+    dealt_rows = lax.psum(own_part, "kv")
     wide_rows = dealt_rows.astype(jnp.float32)
     inv_rms = lax.rsqrt(jnp.mean(wide_rows * wide_rows, axis=1, keepdims=True) + 1e-05)
     normalized_input = (wide_rows * inv_rms * norm_gain.astype(jnp.float32)[None, :]).astype(
@@ -97,13 +100,12 @@
     attended = mixed.reshape(group_rows, heads_dev * queries_per_group * head_size).astype(
         jnp.bfloat16
     )
-    inverse = jnp.zeros((total_rows,), jnp.int32).at[dealing].set(jnp.arange(total_rows))
-    request_rows = lax.all_to_all(attended, "kv", split_axis=0, concat_axis=1, tiled=True)
-    all_context = lax.all_gather(request_rows, ("req", "kv"), axis=0, tiled=True)
-    own_ids = lax.dynamic_slice_in_dim(
-        inverse, (group_index * kv_count + kv_index) * per_device, per_device
+    group_context = lax.all_gather(attended, "kv", axis=1, tiled=True)
+    pick_out = (column_ids[:, None] == dealt_ids[None, :]).astype(jnp.bfloat16)
+    routed = jnp.dot(pick_out, group_context, preferred_element_type=jnp.float32).astype(
+        jnp.bfloat16
     )
-    result = jnp.take(all_context, own_ids, axis=0)
+    result = lax.psum_scatter(routed, "req", scatter_dimension=0, tiled=True)
     return result
 
 

time: 257 us -> 263 us (1.023); the launches traced: 256 us -> 258 us
  blocking collectives: 8.83 us -> 91 us
  waiting for transfers between devices: 209 us -> 134 us
    all_gather x2 -> x0, waiting for transfers between devices: 209 us -> none  [the longest x1 110 us: local(): all_rows = lax.all_gather(states, ('req', 'kv'), axis=0, tiled=True)]
    unnamed x2, waiting for transfers between devices: 0.73 us -> 134 us
    all_gather x0 -> x2, blocking collectives: none -> 57.2 us  [the longest x1 41.4 us: local(): column_rows = lax.all_gather(states, 'req', axis=0, tiled=True)]
    psum x0 -> x1, blocking collectives: none -> 33.8 us  [local(): dealt_rows = lax.psum(own_part, 'kv')]
    all_to_all x1 -> x0, blocking collectives: 8.83 us -> none  [local(): lax.all_to_all(attended, 'kv', split_axis=0, concat_axis=1, tiled=True)]
  transfers between devices with their start and end apart: 2 -> 1, of which waited for: 2 -> 1; matrix products, arithmetic and copies ran while one was open for 2% -> 0% of each run, Pallas kernels for 0% -> 0%
where the time goes in v1:
time: 263 us; the launch traced here: 258 us
  waiting for transfers between devices  134 us (51%)
  blocking collectives  91 us (35%)
  between operations  13.5 us (5%)
  matrix products  12 us (5%)
  other arithmetic  3.91 us (1%)
  local copies, waits for them, and re-layouts  3.79 us (1%)
    unnamed x2, waiting for transfers between devices  134 us
    all_gather x1, blocking collectives, local(): column_rows = lax.all_gather(states, 'req', axis=0, tiled=True)  41.4 us
    psum x1, blocking collectives, local(): dealt_rows = lax.psum(own_part, 'kv')  33.8 us
    all_gather x1, blocking collectives, local(): group_context = lax.all_gather(attended, 'kv', axis=1, tiled=True)  15.8 us
  transfers between devices with their start and end apart: 1, of which 1 were waited for; matrix products, arithmetic and copies ran while one was open for 0% of the time, Pallas kernels for 0%

profile of v1, /device:TPU:1, one launch (start us, length us, event | category | flops | bytes accessed | tf_op | source)
XLA Modules:
  0.0 258.4 jit_solution(17877185251697256283)
XLA Ops:
  6.5 0.0 copy-start
  6.5 0.0 all-reduce.3.cloned.1.call-start
  6.6 0.8 convert_element_type.54
  7.3 0.7 iota_compare_fusion
  8.1 0.7 convert_element_type.52
  8.8 0.7 iota_compare_fusion.1
  9.5 41.4 %all-gather = bf16[32,1,2560]{2,1,0:T(2,128)(2,1)S(1)} all-gather(bf16[1,1,2560]{2,1,0:T(2,128)(2,1)} %bitcast.43), channel_id=1, replica_groups=mesh['req'=32,'kv'=8] {'req'}, dimensions={0}, use_global_device_ids=true | all-gather | bytes 168960 | tf_op jit(solution)/shard_map/all_gather | solution.py:42
  50.9 0.8 dynamic_slice.3
  51.7 0.2 convolution_convert_fusion.1
  51.9 33.8 %psum.7 = bf16[8,2560]{1,0:T(8,128)(2,1)S(1)} all-reduce(bf16[8,2560]{1,0:T(8,128)(2,1)S(1)} %convolution_convert_fusion.1), channel_id=1, replica_groups=mesh['req'=32,'kv'=8] {'kv'}, use_global_device_ids=true, to_apply=%region_0.0 | all-reduce | flops 20480 | bytes 81920 | tf_op jit(solution)/shard_map/psum | solution.py:46
  85.6 0.1 fusion.28
  85.8 0.1 multiply_cosine_fusion.1
  85.9 1.3 convolution_bitcast_fusion
  87.2 0.1 fusion.48
  87.3 1.3 fusion.22
  88.5 0.0 copy-done
  88.6 0.5 fusion.52
  89.1 0.1 reshape.241
  89.2 0.1 maximum_bitcast_fusion
  89.3 0.1 subtract_convert_fusion
  89.4 0.2 fusion.43
  89.6 0.0 copy-start.1
  89.6 3.7 %fusion.54 = (f32[8,4]{1,0:T(8,128)S(1)}, f32[8,4,4096]{2,1,0:T(4,128)S(1)}) fusion(bf16[8,1,80,4096]{3,2,1,0:T(8,128)(2,1)} %param.15, f32[8,4]{1,0:T(8,128)S(1)} %broadcast_multiply_fusion, pred[8,4096]{1,0:T(8,128)(4,1)S(1)} %iota_compare_fusion, pred[8,4096]{1,0:T(8,128)(4,1)S(1)} %iota_compare_fusion.1, bf16[8,4,40]{2,1,0:T(4,128)(2,1)S(1)} %get-tuple-element.8, ...), kind=kOutput, calls=%fused_computation.64 | convolution fusion | flops 21641216 | bytes 5838080 | tf_op jit(solution)/shard_map/sub | solution.py:89
  93.2 0.4 convert_reduce_fusion
  93.6 4.0 %fusion.19 = bf16[8,4,80]{2,1,0:T(4,128)(2,1)S(1)} fusion(bf16[8,1,80,4096]{3,2,1,0:T(8,128)(2,1)} %param.16, bf16[8,4,4096]{2,1,0:T(4,128)(2,1)S(1)} %get-tuple-element.6, pred[8,4096]{1,0:T(8,128)(4,1)S(1)} %iota_compare_fusion.1, f32[8,80]{1,0:T(8,128)S(1)} %fusion.22, f32[8,4]{1,0:T(8,128)S(1)} %get-tuple-element.5), kind=kOutput, calls=%fused_computation.13 | convolution fusion | flops 21110272 | bytes 5545600 | tf_op jit(solution)/shard_map/rkgw,rkhw->rkgh/dot_general | solution.py:96
  97.6 0.1 convert_element_type.60
  97.7 15.8 %all-gather.1 = bf16[8,320,8]{1,2,0:T(8,128)(2,1)S(1)} all-gather(bf16[1,320,8]{1,2,0:T(8,128)(2,1)S(1)} %bitcast.42), channel_id=1, replica_groups=mesh['req'=32,'kv'=8] {'kv'}, dimensions={0}, use_global_device_ids=true | all-gather | bytes 46080 | tf_op jit(solution)/shard_map/all_gather | solution.py:103
  113.5 0.1 reshape.248
  113.6 0.9 convolution_convert_fusion
  114.5 0.0 all-reduce.3.cloned.1.call-update
  114.5 0.0 copy-done.1
  114.5 0.7 dynamic-slice
  115.2 134.3 %all-reduce.3.cloned.1.call-done = bf16[32,2560]{1,0:T(8,128)(2,1)} async-done(((bf16[32,2560]{1,0:T(8,128)(2,1)}), bf16[32,2560]{1,0:T(8,128)(2,1)}) %all-reduce.3.cloned.1.call-update) | async-done | bytes 163856
  249.5 2.1 constant_dynamic-slice_fusion
  (5 shorter events, 0.0 us)
Async XLA Ops:
  6.5 82.0 %copy-start = (bf16[2560,320]{0,1:T(8,128)(2,1)S(1)}, bf16[2560,320]{0,1:T(8,128)(2,1)}, u32[]{:S(2)}) copy-start(bf16[2560,320]{0,1:T(8,128)(2,1)} %param.12) | copy-start | bytes 4915204
  6.5 242.9 %all-reduce.3.cloned.1.call-start = ((), (), s32[]{:S(2)}) async-start(), calls=%async_computation | async-start | bytes 327680
  89.6 24.9 %copy-start.1 = (u32[256]{0:T(256)S(1)}, u32[256]{0:T(256)}, u32[]{:S(2)}) copy-start(u32[256]{0:T(256)} %constant.44) | copy-start | bytes 3076
Sparse Core Ops, SparseCore 0:
  114.6 134.8 all-reduce.2

commit v2 on v0

--- a/solution.py
+++ b/solution.py
@@ -33,39 +33,58 @@
     dealing,
 ):
     kv_count = lax.axis_size("kv")
+    req_count = lax.axis_size("req")
     per_device = states.shape[0]
     group_rows = per_device * kv_count
     group_index = lax.axis_index("req")
     kv_index = lax.axis_index("kv")
     total_rows = dealing.shape[0]
-    dealt_ids = lax.dynamic_slice_in_dim(dealing, group_index * group_rows, group_rows)
-    all_rows = lax.all_gather(states, ("req", "kv"), axis=0, tiled=True)
-    dealt_rows = jnp.take(all_rows, dealt_ids, axis=0)
-    wide_rows = dealt_rows.astype(jnp.float32)
+    head_size = HEAD_DIMENSION
+    heads_dev = key_projection_weight.shape[1] // head_size
+    queries_per_group = w_query.shape[1] // key_projection_weight.shape[1]
+    window_size = cache_keys.shape[3]
+    query_width = w_query.shape[1]
+    key_width = key_projection_weight.shape[1]
+
+    row_block = lax.all_gather(states, "kv", axis=0, tiled=True)
+    wide_rows = row_block.astype(jnp.float32)
     inv_rms = lax.rsqrt(jnp.mean(wide_rows * wide_rows, axis=1, keepdims=True) + 1e-05)
     normalized_input = (wide_rows * inv_rms * norm_gain.astype(jnp.float32)[None, :]).astype(
         jnp.bfloat16
     )
-    head_size = HEAD_DIMENSION
-    heads_dev = key_projection_weight.shape[1] // head_size
-    queries_per_group = w_query.shape[1] // key_projection_weight.shape[1]
-    window_size = cache_keys.shape[3]
-    query_vectors = jnp.dot(normalized_input, w_query, preferred_element_type=jnp.float32).reshape(
-        group_rows, heads_dev * queries_per_group, head_size
+    raw_query = jnp.dot(normalized_input, w_query, preferred_element_type=jnp.float32)
+    raw_key = jnp.dot(normalized_input, key_projection_weight, preferred_element_type=jnp.float32)
+    raw_value = (
+        jnp.dot(normalized_input, value_projection_weight, preferred_element_type=jnp.float32)
+        .astype(jnp.bfloat16)
+        .astype(jnp.float32)
     )
+    packed = jnp.concatenate([raw_query, raw_key, raw_value], axis=1)
+
+    inverse = jnp.zeros((total_rows,), jnp.int32).at[dealing].set(
+        jnp.arange(total_rows, dtype=jnp.int32)
+    )
+    local_ids = group_index * group_rows + jnp.arange(group_rows, dtype=jnp.int32)
+    dest_group = inverse[local_ids] // group_rows
+    to_group = dest_group[None, :, None] == jnp.arange(req_count, dtype=jnp.int32)[:, None, None]
+    send_rows = jnp.where(to_group, packed[None], jnp.zeros((), jnp.float32))
+    recv_rows = lax.all_to_all(send_rows, "req", 0, 0, tiled=True)
+    recv_flat = recv_rows.reshape(req_count * group_rows, packed.shape[1])
+    dealt_ids = lax.dynamic_slice_in_dim(dealing, group_index * group_rows, group_rows)
+    mine = jnp.take(recv_flat, dealt_ids, axis=0)
+
+    query_vectors = mine[:, :query_width].reshape(group_rows, heads_dev * queries_per_group, head_size)
     query_vectors = (
         apply_rotary(query_vectors, lengths)
         .astype(jnp.bfloat16)
         .reshape(group_rows, heads_dev, queries_per_group, head_size)
     )
-    fresh_key_rows = jnp.dot(
-        normalized_input, key_projection_weight, preferred_element_type=jnp.float32
-    ).reshape(group_rows, heads_dev, head_size)
+    fresh_key_rows = mine[:, query_width : query_width + key_width].reshape(
+        group_rows, heads_dev, head_size
+    )
     fresh_key_rows = apply_rotary(fresh_key_rows, lengths).astype(jnp.bfloat16)
     fresh_value_rows = (
-        jnp.dot(normalized_input, value_projection_weight, preferred_element_type=jnp.float32)
-        .astype(jnp.bfloat16)
-        .reshape(group_rows, heads_dev, head_size)
+        mine[:, query_width + key_width :].astype(jnp.bfloat16).reshape(group_rows, heads_dev, head_size)
     )
     score_scale = 1.0 / head_size**0.5
     scores = (
@@ -97,14 +116,16 @@
     attended = mixed.reshape(group_rows, heads_dev * queries_per_group * head_size).astype(
         jnp.bfloat16
     )
-    inverse = jnp.zeros((total_rows,), jnp.int32).at[dealing].set(jnp.arange(total_rows))
-    request_rows = lax.all_to_all(attended, "kv", split_axis=0, concat_axis=1, tiled=True)
-    all_context = lax.all_gather(request_rows, ("req", "kv"), axis=0, tiled=True)
-    own_ids = lax.dynamic_slice_in_dim(
-        inverse, (group_index * kv_count + kv_index) * per_device, per_device
-    )
-    result = jnp.take(all_context, own_ids, axis=0)
-    return result
+
+    pick_out = (
+        jnp.arange(total_rows, dtype=jnp.int32)[:, None] == dealt_ids[None, :]
+    ).astype(jnp.bfloat16)
+    send_out = jnp.dot(pick_out, attended, preferred_element_type=jnp.float32).astype(jnp.bfloat16)
+    recv_out = lax.all_to_all(send_out, ("req", "kv"), 0, 0, tiled=True)
+    own_index = (group_index * kv_count + kv_index) * per_device
+    own_group = inverse[own_index] // group_rows
+    blocks = lax.dynamic_slice_in_dim(recv_out, own_group * kv_count, kv_count)
+    return blocks.reshape(per_device, kv_count * attended.shape[1])
 
 
 def solution(mesh):

time: 257 us -> 88.2 us (0.34)
  waiting for transfers between devices: 209 us -> 26.6 us
  starting transfers between devices: 0.04 us -> 20.7 us
  between operations: 15.4 us -> 2.76 us
  blocking collectives: 8.83 us -> 16.1 us
    all_gather x2 -> x0, waiting for transfers between devices: 209 us -> none  [the longest x1 110 us: local(): all_rows = lax.all_gather(states, ('req', 'kv'), axis=0, tiled=True)]
    all_to_all x0 -> x2, waiting for transfers between devices: none -> 26.6 us  [the longest x1 14.3 us: local(): recv_rows = lax.all_to_all(send_rows, 'req', 0, 0, tiled=True)]
    all_to_all x0 -> x2, starting transfers between devices: none -> 20.7 us  [the longest x1 10.9 us: local(): recv_out = lax.all_to_all(send_out, ('req', 'kv'), 0, 0, tiled=True)]
    all_gather x0 -> x1, blocking collectives: none -> 16.1 us  [local(): row_block = lax.all_gather(states, 'kv', axis=0, tiled=True)]
    all_to_all x1 -> x0, blocking collectives: 8.83 us -> none  [local(): lax.all_to_all(attended, 'kv', split_axis=0, concat_axis=1, tiled=True)]
  transfers between devices with their start and end apart: 2 -> 2, of which waited for: 2 -> 2; matrix products, arithmetic and copies ran while one was open for 2% -> 1% of each run, Pallas kernels for 0% -> 0%
where the time goes in v2:
time: 88.2 us; the launch traced here: 87.8 us
  waiting for transfers between devices  26.6 us (30%)
  starting transfers between devices  20.7 us (23%)
  blocking collectives  16.1 us (18%)
  matrix products  11.1 us (13%)
  local copies, waits for them, and re-layouts  5.97 us (7%)
  other arithmetic  4.46 us (5%)
  between operations  2.76 us (3%)
    all_gather x1, blocking collectives, local(): row_block = lax.all_gather(states, 'kv', axis=0, tiled=True)  16.1 us
    all_to_all x1, waiting for transfers between devices, local(): recv_rows = lax.all_to_all(send_rows, 'req', 0, 0, tiled=True)  14.3 us
    all_to_all x1, waiting for transfers between devices, local(): recv_out = lax.all_to_all(send_out, ('req', 'kv'), 0, 0, tiled=True)  12.3 us
    all_to_all x1, starting transfers between devices, local(): recv_out = lax.all_to_all(send_out, ('req', 'kv'), 0, 0, tiled=True)  10.9 us
    all_to_all x1, starting transfers between devices, local(): recv_rows = lax.all_to_all(send_rows, 'req', 0, 0, tiled=True)  9.85 us
    dot_general x1, matrix products, local(): jnp.einsum('rkgw,rkhw->rkgh', stale_weights, value_cache_slots, preferred...  3.95 us
    sub x1, matrix products, local(): expd = jnp.exp(scores - row_max)  3.63 us
  transfers between devices with their start and end apart: 2, of which 2 were waited for; matrix products, arithmetic and copies ran while one was open for 1% of the time, Pallas kernels for 0%

profile of v2, /device:TPU:1, one launch (start us, length us, event | category | flops | bytes accessed | tf_op | source)
XLA Modules:
  0.0 87.8 jit_solution(16967848428657635239)
XLA Ops:
  0.0 0.0 copy-start
  0.0 0.0 copy-start.1
  0.0 0.0 copy-start.3
  0.0 16.1 %all-gather = bf16[8,1,2560]{2,1,0:T(2,128)(2,1)S(1)} all-gather(bf16[1,1,2560]{2,1,0:T(2,128)(2,1)} %bitcast.52), channel_id=1, replica_groups=mesh['req'=32,'kv'=8] {'kv'}, dimensions={0}, use_global_device_ids=true | all-gather | bytes 46080 | tf_op jit(solution)/shard_map/all_gather | solution.py:49
  16.2 0.1 convert_element_type.62
  16.3 0.1 fusion.27
  16.4 0.7 convert_element_type.51
  17.1 0.0 copy-done
  17.1 0.5 fusion.54
  17.6 1.3 %fusion.52 = f32[8,80]{1,0:T(8,128)S(1)} fusion(bf16[2560,80]{0,1:T(8,128)(2,1)} %param.13, f32[8,1,2560]{2,1,0:T(1,128)S(1)} %convert_element_type.62, f32[2560]{0:T(1024)S(1)} %convert_element_type.51, f32[8]{0:T(128)S(1)} %add_rsqrt_fusion), kind=kOutput, calls=%fused_computation.79 | convolution fusion | flops 3338240 | bytes 504352 | tf_op jit(solution)/shard_map/dot_general | solution.py:56
  18.9 1.3 %fusion.23 = f32[8,80]{1,0:T(8,128)S(1)} fusion(bf16[2560,80]{0,1:T(8,128)(2,1)} %param.14, f32[8,1,2560]{2,1,0:T(1,128)S(1)} %convert_element_type.62, f32[2560]{0:T(1024)S(1)} %convert_element_type.51, f32[8]{0:T(128)S(1)} %add_rsqrt_fusion), kind=kOutput, calls=%fused_computation.18 | convolution fusion | flops 3339520 | bytes 504352 | tf_op jit(solution)/shard_map/dot_general | solution.py:58
  20.2 0.7 compare_select_fusion
  20.9 1.4 %scatter_custom_fusion = s32[256]{0:T(256)S(1)} fusion(s32[256]{0:T(256)S(1)} %compare_select_fusion, s32[256]{0:T(256)S(1)} %iota.39, s32[]{:T(128)} %constant.61.clone.1), kind=kCustom, calls=%fused_computation.75 | custom fusion | bytes 1028 | tf_op jit(solution)/shard_map/scatter | solution.py:64
  22.3 0.6 gather_fusion
  23.0 0.1 pad_maximum_fusion
  23.0 0.9 %broadcast_select_fusion = f32[32,8,480]{2,1,0:T(8,128)} fusion(f32[8,480]{1,0:T(8,128)S(1)} %pad_maximum_fusion, pred[32,8]{1,0:T(8,128)(4,1)S(1)} %iota_compare_fusion.4), kind=kLoop, calls=%fused_computation.22 | loop fusion | flops 122880 | bytes 507136 | tf_op jit(solution)/shard_map/jit(_where)/select_n | solution.py:70
  23.9 9.9 %all-to-all-start = ((f32[32,8,480]{2,1,0:T(8,128)}), f32[32,8,480]{2,1,0:T(8,128)S(1)}, u32[]{:S(2)}, u32[]{:S(2)}) async-start(f32[32,8,480]{2,1,0:T(8,128)} %broadcast_select_fusion), calls=%async_computation | async-start | bytes 1048576 | tf_op jit(solution)/shard_map/all_to_all | solution.py:71
  33.8 0.0 copy-done.1
  33.8 0.1 compare_and_fusion
  33.9 0.0 copy-done.2
  33.9 0.1 multiply_cosine_fusion.1
  34.0 0.0 copy-done.3
  34.1 0.1 iota_compare_fusion
  34.2 14.3 %all-to-all-done = f32[32,8,480]{2,1,0:T(8,128)S(1)} async-done(((f32[32,8,480]{2,1,0:T(8,128)}), f32[32,8,480]{2,1,0:T(8,128)S(1)}, u32[]{:S(2)}, u32[]{:S(2)}) %all-to-all-start) | async-done | bytes 491552 | tf_op jit(solution)/shard_map/all_to_all | solution.py:71
  48.5 0.6 gather_fusion.1
  49.0 0.1 broadcast_select_fusion.1
  49.1 0.1 slice_bitcast_fusion
  49.2 0.1 fusion.41
  49.3 0.1 fusion.43
  49.4 0.1 reshape.303
  49.5 0.1 maximum_bitcast_fusion
  49.5 0.1 subtract_convert_fusion
  49.6 0.2 fusion.39
  49.8 3.6 %fusion.48 = (f32[8,4]{1,0:T(8,128)S(1)}, f32[8,4,4096]{2,1,0:T(4,128)S(1)}) fusion(bf16[8,1,80,4096]{3,2,1,0:T(8,128)(2,1)} %param.15, f32[8,4]{1,0:T(8,128)S(1)} %broadcast_multiply_fusion, pred[8,4096]{1,0:T(8,128)(4,1)S(1)} %get-tuple-element.17, pred[8,4096]{1,0:T(8,128)(4,1)S(1)} %get-tuple-element.18, bf16[8,4,40]{2,1,0:T(4,128)(2,1)S(1)} %get-tuple-element.10, ...), kind=kOutput, calls=%fused_computation.78 | convolution fusion | flops 21641216 | bytes 5838080 | tf_op jit(solution)/shard_map/sub | solution.py:105
  53.5 0.4 convert_reduce_fusion
  53.8 3.9 %fusion.20 = bf16[8,4,80]{2,1,0:T(4,128)(2,1)S(1)} fusion(bf16[8,1,80,4096]{3,2,1,0:T(8,128)(2,1)} %param.16, bf16[8,4,4096]{2,1,0:T(4,128)(2,1)S(1)} %get-tuple-element.6, pred[8,4096]{1,0:T(8,128)(4,1)S(1)} %get-tuple-element.18, f32[8,80]{1,0:T(8,128)S(1)} %fusion.41, f32[8,4]{1,0:T(8,128)S(1)} %get-tuple-element.5), kind=kOutput, calls=%fused_computation.16 | convolution fusion | flops 21110272 | bytes 5545600 | tf_op jit(solution)/shard_map/rkgw,rkhw->rkgh/dot_general | solution.py:112
  57.8 0.1 convert_element_type.60
  57.9 0.3 fusion.16
  58.1 0.5 broadcast.249
  58.7 0.7 reduce.8
  59.4 0.2 copy.23
  59.5 0.8 reshape.342
  60.4 10.9 %all-to-all-start.1 = ((bf16[256,2,160]{2,1,0:T(2,128)(2,1)}), bf16[256,2,160]{2,1,0:T(2,128)(2,1)S(1)}, u32[]{:S(2)}, u32[]{:S(2)}) async-start(bf16[256,2,160]{2,1,0:T(2,128)(2,1)} %reshape.342), calls=%async_computation.1 | async-start | bytes 524288 | tf_op jit(solution)/shard_map/all_to_all | solution.py:124
  71.3 0.6 dynamic_slice.10
  74.5 12.3 %all-to-all-done.1 = bf16[256,2,160]{2,1,0:T(2,128)(2,1)S(1)} async-done(((bf16[256,2,160]{2,1,0:T(2,128)(2,1)}), bf16[256,2,160]{2,1,0:T(2,128)(2,1)S(1)}, u32[]{:S(2)}, u32[]{:S(2)}) %all-to-all-start.1) | async-done | bytes 163872 | tf_op jit(solution)/shard_map/all_to_all | solution.py:124
  86.7 0.3 reshape.343
  87.0 0.1 dynamic-slice_reduce_fusion
  87.1 0.7 reshape.307
  (13 shorter events, 0.1 us)
Async XLA Ops:
  0.0 17.1 %copy-start = (bf16[2560,320]{0,1:T(8,128)(2,1)S(1)}, bf16[2560,320]{0,1:T(8,128)(2,1)}, u32[]{:S(2)}) copy-start(bf16[2560,320]{0,1:T(8,128)(2,1)} %param.12) | copy-start | bytes 4915204
  0.0 33.8 %copy-start.1 = (s32[256]{0:T(256)S(1)}, s32[256]{0:T(256)}, u32[]{:S(2)}) copy-start(s32[256]{0:T(256)} %param.19) | copy-start | bytes 3076
  0.0 33.9 %copy-start.2 = (s32[8]{0:T(128)S(1)}, s32[8]{0:T(128)}, u32[]{:S(2)}) copy-start(s32[8]{0:T(128)} %param.17) | copy-start | bytes 100
  0.0 34.0 %copy-start.3 = (s32[8]{0:T(128)S(1)}, s32[8]{0:T(128)}, u32[]{:S(2)}) copy-start(s32[8]{0:T(128)} %param.18) | copy-start | bytes 100
  23.9 24.5 %all-to-all-start = ((f32[32,8,480]{2,1,0:T(8,128)}), f32[32,8,480]{2,1,0:T(8,128)S(1)}, u32[]{:S(2)}, u32[]{:S(2)}) async-start(f32[32,8,480]{2,1,0:T(8,128)} %broadcast_select_fusion), calls=%async_computation | async-start | bytes 1048576 | tf_op jit(solution)/shard_map/all_to_all | solution.py:71
  60.4 26.4 %all-to-all-start.1 = ((bf16[256,2,160]{2,1,0:T(2,128)(2,1)}), bf16[256,2,160]{2,1,0:T(2,128)(2,1)S(1)}, u32[]{:S(2)}, u32[]{:S(2)}) async-start(bf16[256,2,160]{2,1,0:T(2,128)(2,1)} %reshape.342), calls=%async_computation.1 | async-start | bytes 524288 | tf_op jit(solution)/shard_map/all_to_all | solution.py:124

commit v3 on v2

--- a/solution.py
+++ b/solution.py
@@ -46,7 +46,9 @@
     query_width = w_query.shape[1]
     key_width = key_projection_weight.shape[1]
 
-    row_block = lax.all_gather(states, "kv", axis=0, tiled=True)
+    row_block = lax.all_to_all(
+        jnp.broadcast_to(states[None], (kv_count,) + states.shape), "kv", 0, 0, tiled=True
+    ).reshape(group_rows, states.shape[1])
     wide_rows = row_block.astype(jnp.float32)
     inv_rms = lax.rsqrt(jnp.mean(wide_rows * wide_rows, axis=1, keepdims=True) + 1e-05)
     normalized_input = (wide_rows * inv_rms * norm_gain.astype(jnp.float32)[None, :]).astype(
@@ -61,11 +63,12 @@
     )
     packed = jnp.concatenate([raw_query, raw_key, raw_value], axis=1)
 
-    inverse = jnp.zeros((total_rows,), jnp.int32).at[dealing].set(
-        jnp.arange(total_rows, dtype=jnp.int32)
+    places = jnp.arange(total_rows, dtype=jnp.int32)
+    local_ids = group_index * group_rows + jnp.arange(group_rows, dtype=jnp.int32)
+    dest_group = (
+        jnp.sum(jnp.where(dealing[None, :] == local_ids[:, None], places[None, :], 0), axis=1)
+        // group_rows
     )
-    local_ids = group_index * group_rows + jnp.arange(group_rows, dtype=jnp.int32)
-    dest_group = inverse[local_ids] // group_rows
     to_group = dest_group[None, :, None] == jnp.arange(req_count, dtype=jnp.int32)[:, None, None]
     send_rows = jnp.where(to_group, packed[None], jnp.zeros((), jnp.float32))
     recv_rows = lax.all_to_all(send_rows, "req", 0, 0, tiled=True)
@@ -123,7 +126,7 @@
     send_out = jnp.dot(pick_out, attended, preferred_element_type=jnp.float32).astype(jnp.bfloat16)
     recv_out = lax.all_to_all(send_out, ("req", "kv"), 0, 0, tiled=True)
     own_index = (group_index * kv_count + kv_index) * per_device
-    own_group = inverse[own_index] // group_rows
+    own_group = jnp.sum(jnp.where(dealing == own_index, places, 0)) // group_rows
     blocks = lax.dynamic_slice_in_dim(recv_out, own_group * kv_count, kv_count)
     return blocks.reshape(per_device, kv_count * attended.shape[1])
 

time: 88.2 us -> 82.1 us (0.931)
  blocking collectives: 16.1 us -> 0 us
  starting transfers between devices: 20.7 us -> 26.9 us
  other arithmetic: 4.46 us -> 9.01 us
  local copies, waits for them, and re-layouts: 5.97 us -> 4.03 us
  waiting for transfers between devices: 26.6 us -> 27.7 us
    all_gather x1 -> x0, blocking collectives: 16.1 us -> none  [local(): row_block = lax.all_gather(states, 'kv', axis=0, tiled=True)]
    all_to_all x0 -> x1, starting transfers between devices: none -> 6.44 us  [local(): lax.all_to_all(jnp.broadcast_to(states[None], (kv_count,) + states.shape)...]
    all_to_all x0 -> x1, waiting for transfers between devices: none -> 1.62 us  [local(): lax.all_to_all(jnp.broadcast_to(states[None], (kv_count,) + states.shape)...]
    reduce_sum x0 -> x2, other arithmetic: none -> 1.49 us  [the longest x1 0.86 us: local(): jnp.sum(jnp.where(dealing[None, :] == local_ids[:, None], places[None, :]...]
    scatter x1 -> x0, local copies, waits for them, and re-layouts: 1.39 us -> none  [local(): jnp.zeros((total_rows,), jnp.int32).at[dealing]]
    all_to_all x1, starting transfers between devices: 10.9 us -> 9.95 us  [local(): recv_out = lax.all_to_all(send_out, ('req', 'kv'), 0, 0, tiled=True)]
    unnamed x11 -> x9, local copies, waits for them, and re-layouts: 1.28 us -> 1.93 us
  transfers between devices with their start and end apart: 2 -> 3, of which waited for: 2 -> 3; matrix products, arithmetic and copies ran while one was open for 1% -> 6% of each run, Pallas kernels for 0% -> 0%
where the time goes in v3:
time: 82.1 us; the launch traced here: 81.5 us
  waiting for transfers between devices  27.7 us (34%)
  starting transfers between devices  26.9 us (33%)
  matrix products  11.1 us (14%)
  other arithmetic  9.01 us (11%)
  local copies, waits for them, and re-layouts  4.03 us (5%)
  between operations  2.74 us (3%)
    all_to_all x1, waiting for transfers between devices, local(): recv_rows = lax.all_to_all(send_rows, 'req', 0, 0, tiled=True)  13.9 us
    all_to_all x1, waiting for transfers between devices, local(): recv_out = lax.all_to_all(send_out, ('req', 'kv'), 0, 0, tiled=True)  12.2 us
    all_to_all x1, starting transfers between devices, local(): recv_rows = lax.all_to_all(send_rows, 'req', 0, 0, tiled=True)  10.5 us
    all_to_all x1, starting transfers between devices, local(): recv_out = lax.all_to_all(send_out, ('req', 'kv'), 0, 0, tiled=True)  9.95 us
    all_to_all x1, starting transfers between devices, local(): lax.all_to_all(jnp.broadcast_to(states[None], (kv_count,) + states.shape)...  6.44 us
    dot_general x1, matrix products, local(): jnp.einsum('rkgw,rkhw->rkgh', stale_weights, value_cache_slots, preferred...  3.95 us
    sub x1, matrix products, local(): expd = jnp.exp(scores - row_max)  3.64 us
    unnamed x9, local copies, waits for them, and re-layouts  1.93 us
  transfers between devices with their start and end apart: 3, of which 3 were waited for; matrix products, arithmetic and copies ran while one was open for 6% of the time, Pallas kernels for 0%

profile of v3, /device:TPU:1, one launch (start us, length us, event | category | flops | bytes accessed | tf_op | source)
XLA Modules:
  0.0 81.5 jit_solution(6959216694433660856)
XLA Ops:
  0.0 0.0 copy-start
  0.0 0.9 %reduce.6 = bf16[2560]{0:T(1024)(128)(2,1)S(1)} reduce(bf16[1,2560]{1,0:T(2,128)(2,1)} %param.10, bf16[]{:T(256)} %constant.79), dimensions={0}, to_apply=%param.10.reduce_sub_computation | reduce | bytes 10242 | tf_op args[0]
  0.9 0.5 broadcast.222
  1.4 0.9 %reduce.9 = bf16[8,2560]{1,0:T(8,128)(2,1)S(1)} reduce(bf16[8,1,2560]{2,1,0:T(2,128)(2,1)S(1)} %broadcast_in_dim.134, bf16[]{:T(256)} %broadcast.222), dimensions={1}, to_apply=%broadcast_in_dim.134.reduce_sub_computation | reduce | bytes 81922 | tf_op jit(solution)/shard_map/broadcast_in_dim | solution.py:50
  2.3 0.6 reshape.317
  2.9 6.4 %all-to-all-start = ((bf16[8,2,1280]{2,1,0:T(2,128)(2,1)}), bf16[8,2,1280]{2,1,0:T(2,128)(2,1)S(1)}, u32[]{:S(2)}, u32[]{:S(2)}) async-start(bf16[8,2,1280]{2,1,0:T(2,128)(2,1)} %reshape.317), calls=%async_computation | async-start | bytes 81920 | tf_op jit(solution)/shard_map/all_to_all | solution.py:49
  9.4 0.9 %select_reduce_fusion = s32[8]{0:T(128)S(1)} fusion(s32[256]{0:T(256)} %param.19, s32[8]{0:T(128)S(1)} %iota_add_fusion), kind=kLoop, calls=%fused_computation.39 | loop fusion | flops 6136 | bytes 1088 | tf_op jit(solution)/shard_map/reduce_sum | solution.py:69
  10.3 0.8 compare_and_fusion
  11.1 0.7 convert_element_type.59
  11.7 0.1 multiply_cosine_fusion.1
  11.8 0.7 convert_element_type.55
  12.5 1.6 %all-to-all-done = bf16[8,2,1280]{2,1,0:T(2,128)(2,1)S(1)} async-done(((bf16[8,2,1280]{2,1,0:T(2,128)(2,1)}), bf16[8,2,1280]{2,1,0:T(2,128)(2,1)S(1)}, u32[]{:S(2)}, u32[]{:S(2)}) %all-to-all-start) | async-done | bytes 40992 | tf_op jit(solution)/shard_map/all_to_all | solution.py:49
  14.2 0.1 convert_element_type.66
  14.3 0.1 fusion.27
  14.4 0.0 copy-done
  14.4 0.5 fusion.52
  15.0 1.3 %fusion.50 = f32[8,80]{1,0:T(8,128)S(1)} fusion(bf16[2560,80]{0,1:T(8,128)(2,1)} %param.13, f32[8,1,2560]{2,1,0:T(1,128)S(1)} %convert_element_type.66, f32[2560]{0:T(1024)S(1)} %convert_element_type.55, f32[8]{0:T(128)S(1)} %add_rsqrt_fusion), kind=kOutput, calls=%fused_computation.75 | convolution fusion | flops 3338240 | bytes 504352 | tf_op jit(solution)/shard_map/dot_general | solution.py:58
  16.2 1.3 %fusion.23 = f32[8,80]{1,0:T(8,128)S(1)} fusion(bf16[2560,80]{0,1:T(8,128)(2,1)} %param.14, f32[8,1,2560]{2,1,0:T(1,128)S(1)} %convert_element_type.66, f32[2560]{0:T(1024)S(1)} %convert_element_type.55, f32[8]{0:T(128)S(1)} %add_rsqrt_fusion), kind=kOutput, calls=%fused_computation.16 | convolution fusion | flops 3339520 | bytes 504352 | tf_op jit(solution)/shard_map/dot_general | solution.py:60
  17.5 0.1 pad_maximum_fusion
  17.6 0.9 %broadcast_select_fusion = f32[32,8,480]{2,1,0:T(8,128)} fusion(f32[8,480]{1,0:T(8,128)S(1)} %pad_maximum_fusion, pred[32,8]{1,0:T(8,128)(4,1)S(1)} %iota_compare_fusion.4), kind=kLoop, calls=%fused_computation.20 | loop fusion | flops 122880 | bytes 507136 | tf_op jit(solution)/shard_map/jit(_where)/select_n | solution.py:73
  18.5 10.5 %all-to-all-start.1 = ((f32[32,8,480]{2,1,0:T(8,128)}), f32[32,8,480]{2,1,0:T(8,128)S(1)}, u32[]{:S(2)}, u32[]{:S(2)}) async-start(f32[32,8,480]{2,1,0:T(8,128)} %broadcast_select_fusion), calls=%async_computation.1 | async-start | bytes 1048576 | tf_op jit(solution)/shard_map/all_to_all | solution.py:74
  29.0 0.8 iota_compare_fusion
  29.8 13.9 %all-to-all-done.1 = f32[32,8,480]{2,1,0:T(8,128)S(1)} async-done(((f32[32,8,480]{2,1,0:T(8,128)}), f32[32,8,480]{2,1,0:T(8,128)S(1)}, u32[]{:S(2)}, u32[]{:S(2)}) %all-to-all-start.1) | async-done | bytes 491552 | tf_op jit(solution)/shard_map/all_to_all | solution.py:74
  43.7 0.6 gather_fusion
  44.3 0.1 broadcast_select_fusion.1
  44.3 0.1 slice_bitcast_fusion
  44.4 0.1 fusion.41
  44.5 0.1 fusion.43
  44.6 0.1 reshape.298
  44.7 0.1 maximum_bitcast_fusion
  44.8 0.1 subtract_convert_fusion
  44.8 0.2 fusion.39
  45.0 3.6 %fusion.46 = (f32[8,4]{1,0:T(8,128)S(1)}, f32[8,4,4096]{2,1,0:T(4,128)S(1)}) fusion(bf16[8,1,80,4096]{3,2,1,0:T(8,128)(2,1)} %param.15, f32[8,4]{1,0:T(8,128)S(1)} %broadcast_multiply_fusion, pred[8,4096]{1,0:T(8,128)(4,1)S(1)} %get-tuple-element.17, pred[8,4096]{1,0:T(8,128)(4,1)S(1)} %get-tuple-element.18, bf16[8,4,40]{2,1,0:T(4,128)(2,1)S(1)} %get-tuple-element.10, ...), kind=kOutput, calls=%fused_computation.74 | convolution fusion | flops 21641216 | bytes 5838080 | tf_op jit(solution)/shard_map/sub | solution.py:108
  48.7 0.0 copy-start.1
  48.7 0.4 convert_reduce_fusion
  49.1 3.9 %fusion.20 = bf16[8,4,80]{2,1,0:T(4,128)(2,1)S(1)} fusion(bf16[8,1,80,4096]{3,2,1,0:T(8,128)(2,1)} %param.16, bf16[8,4,4096]{2,1,0:T(4,128)(2,1)S(1)} %get-tuple-element.6, pred[8,4096]{1,0:T(8,128)(4,1)S(1)} %get-tuple-element.18, f32[8,80]{1,0:T(8,128)S(1)} %fusion.41, f32[8,4]{1,0:T(8,128)S(1)} %get-tuple-element.5), kind=kOutput, calls=%fused_computation.14 | convolution fusion | flops 21110272 | bytes 5545600 | tf_op jit(solution)/shard_map/rkgw,rkhw->rkgh/dot_general | solution.py:115
  53.0 0.1 convert_element_type.64
  53.1 0.3 fusion.16
  53.4 0.7 reduce.10
  54.1 0.2 copy.25
  54.3 0.8 %reshape.319 = bf16[256,2,160]{2,1,0:T(2,128)(2,1)} reshape(bf16[256,320]{1,0:T(8,128)(2,1)S(1)} %copy.25) | data formatting | bytes 327680
  55.1 9.9 %all-to-all-start.2 = ((bf16[256,2,160]{2,1,0:T(2,128)(2,1)}), bf16[256,2,160]{2,1,0:T(2,128)(2,1)S(1)}, u32[]{:S(2)}, u32[]{:S(2)}) async-start(bf16[256,2,160]{2,1,0:T(2,128)(2,1)} %reshape.319), calls=%async_computation.2 | async-start | bytes 524288 | tf_op jit(solution)/shard_map/all_to_all | solution.py:127
  65.1 0.0 copy-done.1
  65.1 0.6 fusion.44
  68.3 12.2 %all-to-all-done.2 = bf16[256,2,160]{2,1,0:T(2,128)(2,1)S(1)} async-done(((bf16[256,2,160]{2,1,0:T(2,128)(2,1)}), bf16[256,2,160]{2,1,0:T(2,128)(2,1)S(1)}, u32[]{:S(2)}, u32[]{:S(2)}) %all-to-all-start.2) | async-done | bytes 163872 | tf_op jit(solution)/shard_map/all_to_all | solution.py:127
  80.5 0.3 reshape.320
  80.8 0.1 dynamic-slice_reduce_fusion
  80.8 0.7 reshape.302
  (11 shorter events, 0.1 us)
Async XLA Ops:
  0.0 14.4 %copy-start = (bf16[2560,320]{0,1:T(8,128)(2,1)S(1)}, bf16[2560,320]{0,1:T(8,128)(2,1)}, u32[]{:S(2)}) copy-start(bf16[2560,320]{0,1:T(8,128)(2,1)} %param.12) | copy-start | bytes 4915204
  2.9 11.2 %all-to-all-start = ((bf16[8,2,1280]{2,1,0:T(2,128)(2,1)}), bf16[8,2,1280]{2,1,0:T(2,128)(2,1)S(1)}, u32[]{:S(2)}, u32[]{:S(2)}) async-start(bf16[8,2,1280]{2,1,0:T(2,128)(2,1)} %reshape.317), calls=%async_computation | async-start | bytes 81920 | tf_op jit(solution)/shard_map/all_to_all | solution.py:49
  18.5 25.2 %all-to-all-start.1 = ((f32[32,8,480]{2,1,0:T(8,128)}), f32[32,8,480]{2,1,0:T(8,128)S(1)}, u32[]{:S(2)}, u32[]{:S(2)}) async-start(f32[32,8,480]{2,1,0:T(8,128)} %broadcast_select_fusion), calls=%async_computation.1 | async-start | bytes 1048576 | tf_op jit(solution)/shard_map/all_to_all | solution.py:74
  48.7 16.4 %copy-start.1 = (s32[256]{0:T(256)S(1)}, s32[256]{0:T(256)}, u32[]{:S(2)}) copy-start(s32[256]{0:T(256)} %param.19) | copy-start | bytes 3076
  55.1 25.4 %all-to-all-start.2 = ((bf16[256,2,160]{2,1,0:T(2,128)(2,1)}), bf16[256,2,160]{2,1,0:T(2,128)(2,1)S(1)}, u32[]{:S(2)}, u32[]{:S(2)}) async-start(bf16[256,2,160]{2,1,0:T(2,128)(2,1)} %reshape.319), calls=%async_computation.2 | async-start | bytes 524288 | tf_op jit(solution)/shard_map/all_to_all | solution.py:127

commit v4 on v3

--- a/solution.py
+++ b/solution.py
@@ -1,7 +1,7 @@
 import jax
 import jax.numpy as jnp
 from jax import lax
-from jax.sharding import PartitionSpec as P
+from jax.sharding import Mesh, PartitionSpec as P
 
 HEAD_DIMENSION = 80
 
@@ -33,10 +33,12 @@
     dealing,
 ):
     kv_count = lax.axis_size("kv")
-    req_count = lax.axis_size("req")
+    req_hi = lax.axis_size("req_hi")
+    req_lo = lax.axis_size("req_lo")
+    req_count = req_hi * req_lo
     per_device = states.shape[0]
     group_rows = per_device * kv_count
-    group_index = lax.axis_index("req")
+    group_index = lax.axis_index("req_hi") * req_lo + lax.axis_index("req_lo")
     kv_index = lax.axis_index("kv")
     total_rows = dealing.shape[0]
     head_size = HEAD_DIMENSION
@@ -69,9 +71,26 @@
         jnp.sum(jnp.where(dealing[None, :] == local_ids[:, None], places[None, :], 0), axis=1)
         // group_rows
     )
-    to_group = dest_group[None, :, None] == jnp.arange(req_count, dtype=jnp.int32)[:, None, None]
-    send_rows = jnp.where(to_group, packed[None], jnp.zeros((), jnp.float32))
-    recv_rows = lax.all_to_all(send_rows, "req", 0, 0, tiled=True)
+    to_lo = (dest_group % req_lo)[None, :, None] == jnp.arange(req_lo, dtype=jnp.int32)[:, None, None]
+    lo_rows = lax.all_to_all(
+        jnp.where(to_lo, packed[None], jnp.zeros((), jnp.float32)), "req_lo", 0, 0, tiled=True
+    )
+    lo_ids = (lax.axis_index("req_hi") * req_lo + jnp.arange(req_lo, dtype=jnp.int32))[
+        :, None
+    ] * group_rows + jnp.arange(group_rows, dtype=jnp.int32)[None, :]
+    lo_groups = (
+        jnp.sum(
+            jnp.where(dealing[None, None, :] == lo_ids[:, :, None], places[None, None, :], 0),
+            axis=2,
+        )
+        // group_rows
+    )
+    to_hi = (lo_groups // req_lo)[None, :, :, None] == jnp.arange(req_hi, dtype=jnp.int32)[
+        :, None, None, None
+    ]
+    recv_rows = lax.all_to_all(
+        jnp.where(to_hi, lo_rows[None], jnp.zeros((), jnp.float32)), "req_hi", 0, 0, tiled=True
+    )
     recv_flat = recv_rows.reshape(req_count * group_rows, packed.shape[1])
     dealt_ids = lax.dynamic_slice_in_dim(dealing, group_index * group_rows, group_rows)
     mine = jnp.take(recv_flat, dealt_ids, axis=0)
@@ -124,7 +143,7 @@
         jnp.arange(total_rows, dtype=jnp.int32)[:, None] == dealt_ids[None, :]
     ).astype(jnp.bfloat16)
     send_out = jnp.dot(pick_out, attended, preferred_element_type=jnp.float32).astype(jnp.bfloat16)
-    recv_out = lax.all_to_all(send_out, ("req", "kv"), 0, 0, tiled=True)
+    recv_out = lax.all_to_all(send_out, ("req_hi", "req_lo", "kv"), 0, 0, tiled=True)
     own_index = (group_index * kv_count + kv_index) * per_device
     own_group = jnp.sum(jnp.where(dealing == own_index, places, 0)) // group_rows
     blocks = lax.dynamic_slice_in_dim(recv_out, own_group * kv_count, kv_count)
@@ -132,17 +151,28 @@
 
 
 def solution(mesh):
+    req_devices = mesh.devices[:, 0]
+    outer = len({device.coords[0] for device in req_devices})
+    if len(req_devices) % outer:
+        outer = 1
+    split_mesh = Mesh(
+        mesh.devices.reshape(outer, len(req_devices) // outer, mesh.devices.shape[1]),
+        ("req_hi", "req_lo", "kv"),
+    )
+    req = ("req_hi", "req_lo")
     in_specs = (
-        P(("req", "kv"), None),
+        P(req + ("kv",), None),
         P(),
         P(None, "kv"),
         P(None, "kv"),
         P(None, "kv"),
-        P("req", "kv", None, None),
-        P("req", "kv", None, None),
-        P("req"),
-        P("req"),
+        P(req, "kv", None, None),
+        P(req, "kv", None, None),
+        P(req),
+        P(req),
         P(),
     )
-    out_specs = P(("req", "kv"), None)
-    return jax.shard_map(local, mesh=mesh, in_specs=in_specs, out_specs=out_specs, check_vma=False)
+    out_specs = P(req + ("kv",), None)
+    return jax.shard_map(
+        local, mesh=split_mesh, in_specs=in_specs, out_specs=out_specs, check_vma=False
+    )

time: 82.1 us -> 83.7 us (1.019)
  other arithmetic: 9.01 us -> 10.1 us
    all_to_all x1, waiting for transfers between devices: 1.62 us -> 0.56 us  [local(): lax.all_to_all(jnp.broadcast_to(states[None], (kv_count,) + states.shape)...]
    reduce_sum x0 -> x1, other arithmetic: none -> 0.96 us  [local(): jnp.sum(jnp.where(dealing[None, None, :] == lo_ids[:, :, None], places[No...]
    all_to_all x2 -> x3, starting transfers between devices: 20.5 us -> 21.3 us  [the longest x1 9.58 us: local(): lax.all_to_all(send_out, ('req_hi', 'req_lo', 'kv'), 0, 0, tiled=True)]
    all_to_all x2 -> x3, waiting for transfers between devices: 26.1 us -> 26.7 us  [the longest x1 12.2 us: local(): lax.all_to_all(send_out, ('req_hi', 'req_lo', 'kv'), 0, 0, tiled=True)]
    unnamed x9 -> x11, local copies, waits for them, and re-layouts: 1.93 us -> 1.93 us
  transfers between devices with their start and end apart: 3 -> 4, of which waited for: 3 -> 4; matrix products, arithmetic and copies ran while one was open for 6% -> 6% of each run, Pallas kernels for 0% -> 0%
where the time goes in v4:
time: 83.7 us; the launch traced here: 83.1 us
  starting transfers between devices  27.7 us (33%)
  waiting for transfers between devices  27.3 us (33%)
  matrix products  11.1 us (13%)
  other arithmetic  10.1 us (12%)
  local copies, waits for them, and re-layouts  4.04 us (5%)
  between operations  2.76 us (3%)
    all_to_all x1, waiting for transfers between devices, local(): lax.all_to_all(send_out, ('req_hi', 'req_lo', 'kv'), 0, 0, tiled=True)  12.2 us
    all_to_all x1, starting transfers between devices, local(): lax.all_to_all(send_out, ('req_hi', 'req_lo', 'kv'), 0, 0, tiled=True)  9.58 us
    all_to_all x1, waiting for transfers between devices, local(): lax.all_to_all(jnp.where(to_lo, packed[None], jnp.zeros((), jnp.float32))...  7.75 us
    all_to_all x1, starting transfers between devices, local(): lax.all_to_all(jnp.where(to_lo, packed[None], jnp.zeros((), jnp.float32))...  7.68 us
    all_to_all x1, waiting for transfers between devices, local(): lax.all_to_all(jnp.where(to_hi, lo_rows[None], jnp.zeros((), jnp.float32)...  6.78 us
    all_to_all x1, starting transfers between devices, local(): lax.all_to_all(jnp.broadcast_to(states[None], (kv_count,) + states.shape)...  6.44 us
    all_to_all x1, starting transfers between devices, local(): lax.all_to_all(jnp.where(to_hi, lo_rows[None], jnp.zeros((), jnp.float32)...  4.01 us
    dot_general x1, matrix products, local(): jnp.einsum('rkgw,rkhw->rkgh', stale_weights, value_cache_slots, preferred...  3.95 us
  transfers between devices with their start and end apart: 4, of which 4 were waited for; matrix products, arithmetic and copies ran while one was open for 6% of the time, Pallas kernels for 0%

profile of v4, /device:TPU:1, one launch (start us, length us, event | category | flops | bytes accessed | tf_op | source)
XLA Modules:
  0.0 83.1 jit_solution(1883710767129823731)
XLA Ops:
  0.0 0.9 %reduce.6 = bf16[2560]{0:T(1024)(128)(2,1)S(1)} reduce(bf16[1,2560]{1,0:T(2,128)(2,1)} %param.10, bf16[]{:T(256)} %constant.110), dimensions={0}, to_apply=%param.10.reduce_sub_computation | reduce | bytes 10242 | tf_op args[0]
  0.9 0.5 broadcast.348
  1.4 0.9 %reduce.9 = bf16[8,2560]{1,0:T(8,128)(2,1)S(1)} reduce(bf16[8,1,2560]{2,1,0:T(2,128)(2,1)S(1)} %broadcast_in_dim.177, bf16[]{:T(256)} %broadcast.348), dimensions={1}, to_apply=%broadcast_in_dim.177.reduce_sub_computation | reduce | bytes 81922 | tf_op jit(solution)/shard_map/broadcast_in_dim | solution.py:52
  2.3 0.6 reshape.395
  2.9 6.4 %all-to-all-start = ((bf16[8,2,1280]{2,1,0:T(2,128)(2,1)}), bf16[8,2,1280]{2,1,0:T(2,128)(2,1)S(1)}, u32[]{:S(2)}, u32[]{:S(2)}) async-start(bf16[8,2,1280]{2,1,0:T(2,128)(2,1)} %reshape.395), calls=%async_computation | async-start | bytes 81920 | tf_op jit(solution)/shard_map/all_to_all | solution.py:51
  9.4 0.9 %select_reduce_fusion.1 = s32[8]{0:T(128)S(1)} fusion(s32[256]{0:T(256)} %param.19, s32[8]{0:T(128)S(1)} %iota_add_fusion.1), kind=kLoop, calls=%fused_computation.41 | loop fusion | flops 6136 | bytes 1088 | tf_op jit(solution)/shard_map/reduce_sum | solution.py:71
  10.3 0.1 iota_add_fusion
  10.4 1.0 %select_reduce_fusion = s32[8,8]{1,0:T(8,128)S(1)} fusion(s32[8,8]{1,0:T(8,128)S(1)} %iota_add_fusion, s32[256]{0:T(256)} %param.19), kind=kLoop, calls=%fused_computation.32 | loop fusion | flops 49088 | bytes 1536 | tf_op jit(solution)/shard_map/reduce_sum | solution.py:82
  11.4 0.8 iota_compare_fusion
  12.1 0.8 compare_and_fusion
  12.9 0.7 convert_element_type.55
  13.6 0.6 all-to-all-done
  14.2 0.1 convert_element_type.66
  14.3 0.1 fusion.27
  14.4 0.5 fusion.57
  15.0 1.3 %fusion.55 = f32[8,80]{1,0:T(8,128)S(1)} fusion(bf16[2560,80]{0,1:T(8,128)(2,1)} %param.13, f32[8,1,2560]{2,1,0:T(1,128)S(1)} %convert_element_type.66, f32[2560]{0:T(1024)S(1)} %convert_element_type.55, f32[8]{0:T(128)S(1)} %add_rsqrt_fusion), kind=kOutput, calls=%fused_computation.98 | convolution fusion | flops 3338240 | bytes 504352 | tf_op jit(solution)/shard_map/dot_general | solution.py:60
  16.2 1.3 %fusion.23 = f32[8,80]{1,0:T(8,128)S(1)} fusion(bf16[2560,80]{0,1:T(8,128)(2,1)} %param.14, f32[8,1,2560]{2,1,0:T(1,128)S(1)} %convert_element_type.66, f32[2560]{0:T(1024)S(1)} %convert_element_type.55, f32[8]{0:T(128)S(1)} %add_rsqrt_fusion), kind=kOutput, calls=%fused_computation.16 | convolution fusion | flops 3339520 | bytes 504352 | tf_op jit(solution)/shard_map/dot_general | solution.py:62
  17.5 0.1 pad_maximum_fusion
  17.6 0.7 broadcast_select_fusion.1
  18.3 7.7 %all-to-all-start.1 = ((f32[8,8,480]{2,1,0:T(8,128)}), f32[8,8,480]{2,1,0:T(8,128)S(1)}, u32[]{:S(2)}, u32[]{:S(2)}) async-start(f32[8,8,480]{2,1,0:T(8,128)} %broadcast_select_fusion.1), calls=%async_computation.1 | async-start | bytes 262144 | tf_op jit(solution)/shard_map/all_to_all | solution.py:75
  26.0 7.7 %all-to-all-done.1 = f32[8,8,480]{2,1,0:T(8,128)S(1)} async-done(((f32[8,8,480]{2,1,0:T(8,128)}), f32[8,8,480]{2,1,0:T(8,128)S(1)}, u32[]{:S(2)}, u32[]{:S(2)}) %all-to-all-start.1) | async-done | bytes 122912 | tf_op jit(solution)/shard_map/all_to_all | solution.py:75
  33.7 0.9 %broadcast_select_fusion = f32[4,8,8,480]{3,2,1,0:T(8,128)} fusion(f32[8,8,480]{2,1,0:T(8,128)S(1)} %all-to-all-done.1, pred[4,8,8]{2,1,0:T(8,128)(4,1)S(1)} %iota_compare_fusion.4), kind=kLoop, calls=%fused_computation.20 | loop fusion | flops 122880 | bytes 614656 | tf_op jit(solution)/shard_map/jit(_where)/select_n | solution.py:92
  34.6 4.0 %all-to-all-start.2 = ((f32[4,8,8,480]{3,2,1,0:T(8,128)}), f32[4,8,8,480]{3,2,1,0:T(8,128)S(1)}, u32[]{:S(2)}, u32[]{:S(2)}) async-start(f32[4,8,8,480]{3,2,1,0:T(8,128)} %broadcast_select_fusion), calls=%async_computation.2 | async-start | bytes 1048576 | tf_op jit(solution)/shard_map/all_to_all | solution.py:91
  38.7 0.1 multiply_cosine_fusion.1
  38.8 6.8 %all-to-all-done.2 = f32[4,8,8,480]{3,2,1,0:T(8,128)S(1)} async-done(((f32[4,8,8,480]{3,2,1,0:T(8,128)}), f32[4,8,8,480]{3,2,1,0:T(8,128)S(1)}, u32[]{:S(2)}, u32[]{:S(2)}) %all-to-all-start.2) | async-done | bytes 491552 | tf_op jit(solution)/shard_map/all_to_all | solution.py:91
  45.6 0.6 gather_fusion
  46.2 0.1 broadcast_select_fusion.2
  46.2 0.1 slice_bitcast_fusion
  46.3 0.1 fusion.45
  46.4 0.1 fusion.47
  46.5 0.1 reshape.376
  46.6 0.1 maximum_bitcast_fusion
  46.6 0.1 subtract_convert_fusion
  46.7 0.2 fusion.43
  46.9 3.7 %fusion.51 = (f32[8,4]{1,0:T(8,128)S(1)}, f32[8,4,4096]{2,1,0:T(4,128)S(1)}) fusion(bf16[8,1,80,4096]{3,2,1,0:T(8,128)(2,1)} %param.15, f32[8,4]{1,0:T(8,128)S(1)} %broadcast_multiply_fusion, pred[8,4096]{1,0:T(8,128)(4,1)S(1)} %get-tuple-element.17, pred[8,4096]{1,0:T(8,128)(4,1)S(1)} %get-tuple-element.18, bf16[8,4,40]{2,1,0:T(4,128)(2,1)S(1)} %get-tuple-element.10, ...), kind=kOutput, calls=%fused_computation.97 | convolution fusion | flops 21641216 | bytes 5838080 | tf_op jit(solution)/shard_map/sub | solution.py:127
  50.6 0.4 convert_reduce_fusion
  51.0 4.0 %fusion.20 = bf16[8,4,80]{2,1,0:T(4,128)(2,1)S(1)} fusion(bf16[8,1,80,4096]{3,2,1,0:T(8,128)(2,1)} %param.16, bf16[8,4,4096]{2,1,0:T(4,128)(2,1)S(1)} %get-tuple-element.6, pred[8,4096]{1,0:T(8,128)(4,1)S(1)} %get-tuple-element.18, f32[8,80]{1,0:T(8,128)S(1)} %fusion.45, f32[8,4]{1,0:T(8,128)S(1)} %get-tuple-element.5), kind=kOutput, calls=%fused_computation.14 | convolution fusion | flops 21110272 | bytes 5545600 | tf_op jit(solution)/shard_map/rkgw,rkhw->rkgh/dot_general | solution.py:134
  54.9 0.1 convert_element_type.64
  55.0 0.3 fusion.16
  55.3 0.7 reduce.10
  56.0 0.2 copy.25
  56.2 0.8 %reshape.397 = bf16[256,2,160]{2,1,0:T(2,128)(2,1)} reshape(bf16[256,320]{1,0:T(8,128)(2,1)S(1)} %copy.25) | data formatting | bytes 327680
  57.0 9.6 %all-to-all-start.3 = ((bf16[256,2,160]{2,1,0:T(2,128)(2,1)}), bf16[256,2,160]{2,1,0:T(2,128)(2,1)S(1)}, u32[]{:S(2)}, u32[]{:S(2)}) async-start(bf16[256,2,160]{2,1,0:T(2,128)(2,1)} %reshape.397), calls=%async_computation.3 | async-start | bytes 524288 | tf_op jit(solution)/shard_map/all_to_all | solution.py:146
  66.6 0.6 fusion.48
  69.9 12.2 %all-to-all-done.3 = bf16[256,2,160]{2,1,0:T(2,128)(2,1)S(1)} async-done(((bf16[256,2,160]{2,1,0:T(2,128)(2,1)}), bf16[256,2,160]{2,1,0:T(2,128)(2,1)S(1)}, u32[]{:S(2)}, u32[]{:S(2)}) %all-to-all-start.3) | async-done | bytes 163872 | tf_op jit(solution)/shard_map/all_to_all | solution.py:146
  82.1 0.3 reshape.398
  82.3 0.1 dynamic-slice_reduce_fusion
  82.4 0.7 reshape.380
  (21 shorter events, 0.2 us)
Async XLA Ops:
  0.0 14.4 %copy-start = (bf16[2560,320]{0,1:T(8,128)(2,1)S(1)}, bf16[2560,320]{0,1:T(8,128)(2,1)}, u32[]{:S(2)}) copy-start(bf16[2560,320]{0,1:T(8,128)(2,1)} %param.12) | copy-start | bytes 4915204
  0.0 38.7 %copy-start.2 = (s32[8]{0:T(128)S(1)}, s32[8]{0:T(128)}, u32[]{:S(2)}) copy-start(s32[8]{0:T(128)} %param.17) | copy-start | bytes 100
  2.9 11.2 %all-to-all-start = ((bf16[8,2,1280]{2,1,0:T(2,128)(2,1)}), bf16[8,2,1280]{2,1,0:T(2,128)(2,1)S(1)}, u32[]{:S(2)}, u32[]{:S(2)}) async-start(bf16[8,2,1280]{2,1,0:T(2,128)(2,1)} %reshape.395), calls=%async_computation | async-start | bytes 81920 | tf_op jit(solution)/shard_map/all_to_all | solution.py:51
  18.3 15.4 %all-to-all-start.1 = ((f32[8,8,480]{2,1,0:T(8,128)}), f32[8,8,480]{2,1,0:T(8,128)S(1)}, u32[]{:S(2)}, u32[]{:S(2)}) async-start(f32[8,8,480]{2,1,0:T(8,128)} %broadcast_select_fusion.1), calls=%async_computation.1 | async-start | bytes 262144 | tf_op jit(solution)/shard_map/all_to_all | solution.py:75
  34.6 10.9 %all-to-all-start.2 = ((f32[4,8,8,480]{3,2,1,0:T(8,128)}), f32[4,8,8,480]{3,2,1,0:T(8,128)S(1)}, u32[]{:S(2)}, u32[]{:S(2)}) async-start(f32[4,8,8,480]{3,2,1,0:T(8,128)} %broadcast_select_fusion), calls=%async_computation.2 | async-start | bytes 1048576 | tf_op jit(solution)/shard_map/all_to_all | solution.py:91
  50.6 16.0 %copy-start.1 = (s32[256]{0:T(256)S(1)}, s32[256]{0:T(256)}, u32[]{:S(2)}) copy-start(s32[256]{0:T(256)} %param.19) | copy-start | bytes 3076
  57.0 25.1 %all-to-all-start.3 = ((bf16[256,2,160]{2,1,0:T(2,128)(2,1)}), bf16[256,2,160]{2,1,0:T(2,128)(2,1)S(1)}, u32[]{:S(2)}, u32[]{:S(2)}) async-start(bf16[256,2,160]{2,1,0:T(2,128)(2,1)} %reshape.397), calls=%async_computation.3 | async-start | bytes 524288 | tf_op jit(solution)/shard_map/all_to_all | solution.py:146

commit v5 on v3

--- a/solution.py
+++ b/solution.py
@@ -65,10 +65,13 @@
 
     places = jnp.arange(total_rows, dtype=jnp.int32)
     local_ids = group_index * group_rows + jnp.arange(group_rows, dtype=jnp.int32)
-    dest_group = (
-        jnp.sum(jnp.where(dealing[None, :] == local_ids[:, None], places[None, :], 0), axis=1)
+    own_index = (group_index * kv_count + kv_index) * per_device
+    lookup_ids = jnp.concatenate([local_ids, own_index[None]])
+    lookup_groups = (
+        jnp.sum(jnp.where(dealing[None, :] == lookup_ids[:, None], places[None, :], 0), axis=1)
         // group_rows
     )
+    dest_group = lookup_groups[:group_rows]
     to_group = dest_group[None, :, None] == jnp.arange(req_count, dtype=jnp.int32)[:, None, None]
     send_rows = jnp.where(to_group, packed[None], jnp.zeros((), jnp.float32))
     recv_rows = lax.all_to_all(send_rows, "req", 0, 0, tiled=True)
@@ -125,8 +128,7 @@
     ).astype(jnp.bfloat16)
     send_out = jnp.dot(pick_out, attended, preferred_element_type=jnp.float32).astype(jnp.bfloat16)
     recv_out = lax.all_to_all(send_out, ("req", "kv"), 0, 0, tiled=True)
-    own_index = (group_index * kv_count + kv_index) * per_device
-    own_group = jnp.sum(jnp.where(dealing == own_index, places, 0)) // group_rows
+    own_group = lookup_groups[group_rows]
     blocks = lax.dynamic_slice_in_dim(recv_out, own_group * kv_count, kv_count)
     return blocks.reshape(per_device, kv_count * attended.shape[1])
 

time: 82.1 us -> 82.2 us (level)
  waiting for transfers between devices: 27.7 us -> 29.7 us
  between operations: 2.74 us -> 0.78 us
    all_to_all x1, waiting for transfers between devices: 12.2 us -> 14.2 us  [local(): recv_out = lax.all_to_all(send_out, ('req', 'kv'), 0, 0, tiled=True)]
    unnamed x9 -> x7, local copies, waits for them, and re-layouts: 1.93 us -> 1.93 us
where the time goes in v5:
time: 82.2 us; the launch traced here: 81.6 us
  waiting for transfers between devices  29.7 us (36%)
  starting transfers between devices  27 us (33%)
  matrix products  11.1 us (14%)
  other arithmetic  8.46 us (10%)
  local copies, waits for them, and re-layouts  4.62 us (6%)
    all_to_all x1, waiting for transfers between devices, local(): recv_out = lax.all_to_all(send_out, ('req', 'kv'), 0, 0, tiled=True)  14.2 us
    all_to_all x1, waiting for transfers between devices, local(): recv_rows = lax.all_to_all(send_rows, 'req', 0, 0, tiled=True)  13.9 us
    all_to_all x1, starting transfers between devices, local(): recv_rows = lax.all_to_all(send_rows, 'req', 0, 0, tiled=True)  10.5 us
    all_to_all x1, starting transfers between devices, local(): recv_out = lax.all_to_all(send_out, ('req', 'kv'), 0, 0, tiled=True)  10 us
    all_to_all x1, starting transfers between devices, local(): lax.all_to_all(jnp.broadcast_to(states[None], (kv_count,) + states.shape)...  6.44 us
    dot_general x1, matrix products, local(): jnp.einsum('rkgw,rkhw->rkgh', stale_weights, value_cache_slots, preferred...  3.96 us
    sub x1, matrix products, local(): expd = jnp.exp(scores - row_max)  3.66 us
    unnamed x7, local copies, waits for them, and re-layouts  1.93 us
  transfers between devices with their start and end apart: 3, of which 3 were waited for; matrix products, arithmetic and copies ran while one was open for 6% of the time, Pallas kernels for 0%

profile of v5, /device:TPU:1, one launch (start us, length us, event | category | flops | bytes accessed | tf_op | source)
XLA Modules:
  0.0 81.6 jit_solution(9368020595055362915)
XLA Ops:
  0.0 0.0 copy-start
  0.0 0.9 %reduce.6 = bf16[2560]{0:T(1024)(128)(2,1)S(1)} reduce(bf16[1,2560]{1,0:T(2,128)(2,1)} %param.10, bf16[]{:T(256)} %constant.72), dimensions={0}, to_apply=%param.10.reduce_sub_computation | reduce | bytes 10242 | tf_op args[0]
  0.9 0.5 broadcast.197
  1.4 0.9 %reduce.9 = bf16[8,2560]{1,0:T(8,128)(2,1)S(1)} reduce(bf16[8,1,2560]{2,1,0:T(2,128)(2,1)S(1)} %broadcast_in_dim.134, bf16[]{:T(256)} %broadcast.197), dimensions={1}, to_apply=%broadcast_in_dim.134.reduce_sub_computation | reduce | bytes 81922 | tf_op jit(solution)/shard_map/broadcast_in_dim | solution.py:50
  2.3 0.6 reshape.298
  2.9 6.4 %all-to-all-start = ((bf16[8,2,1280]{2,1,0:T(2,128)(2,1)}), bf16[8,2,1280]{2,1,0:T(2,128)(2,1)S(1)}, u32[]{:S(2)}, u32[]{:S(2)}) async-start(bf16[8,2,1280]{2,1,0:T(2,128)(2,1)} %reshape.298), calls=%async_computation | async-start | bytes 81920 | tf_op jit(solution)/shard_map/all_to_all | solution.py:49
  9.4 0.1 pad_add_fusion
  9.5 0.9 %select_reduce_fusion = s32[9]{0:T(128)S(1)} fusion(s32[256]{0:T(256)} %param.19, s32[9]{0:T(128)S(1)} %pad_add_fusion), kind=kLoop, calls=%fused_computation.36 | loop fusion | flops 6903 | bytes 1096 | tf_op jit(solution)/shard_map/reduce_sum | solution.py:71
  10.4 0.8 compare_and_fusion
  11.1 0.7 convert_element_type.59
  11.8 0.1 multiply_cosine_fusion.1
  11.9 0.7 convert_element_type.55
  12.6 1.5 %all-to-all-done = bf16[8,2,1280]{2,1,0:T(2,128)(2,1)S(1)} async-done(((bf16[8,2,1280]{2,1,0:T(2,128)(2,1)}), bf16[8,2,1280]{2,1,0:T(2,128)(2,1)S(1)}, u32[]{:S(2)}, u32[]{:S(2)}) %all-to-all-start) | async-done | bytes 40992 | tf_op jit(solution)/shard_map/all_to_all | solution.py:49
  14.2 0.1 convert_element_type.66
  14.3 0.1 fusion.27
  14.4 0.0 copy-done
  14.4 0.5 fusion.51
  15.0 1.3 %fusion.49 = f32[8,80]{1,0:T(8,128)S(1)} fusion(bf16[2560,80]{0,1:T(8,128)(2,1)} %param.13, f32[8,1,2560]{2,1,0:T(1,128)S(1)} %convert_element_type.66, f32[2560]{0:T(1024)S(1)} %convert_element_type.55, f32[8]{0:T(128)S(1)} %add_rsqrt_fusion), kind=kOutput, calls=%fused_computation.74 | convolution fusion | flops 3338240 | bytes 504352 | tf_op jit(solution)/shard_map/dot_general | solution.py:58
  16.2 1.3 %fusion.23 = f32[8,80]{1,0:T(8,128)S(1)} fusion(bf16[2560,80]{0,1:T(8,128)(2,1)} %param.14, f32[8,1,2560]{2,1,0:T(1,128)S(1)} %convert_element_type.66, f32[2560]{0:T(1024)S(1)} %convert_element_type.55, f32[8]{0:T(128)S(1)} %add_rsqrt_fusion), kind=kOutput, calls=%fused_computation.16 | convolution fusion | flops 3339520 | bytes 504352 | tf_op jit(solution)/shard_map/dot_general | solution.py:60
  17.5 0.1 pad_maximum_fusion
  17.6 0.9 %broadcast_select_fusion = f32[32,8,480]{2,1,0:T(8,128)} fusion(f32[8,480]{1,0:T(8,128)S(1)} %pad_maximum_fusion, pred[32,8]{1,0:T(8,128)(4,1)S(1)} %iota_compare_fusion.4), kind=kLoop, calls=%fused_computation.20 | loop fusion | flops 122880 | bytes 507136 | tf_op jit(solution)/shard_map/jit(_where)/select_n | solution.py:76
  18.5 10.5 %all-to-all-start.1 = ((f32[32,8,480]{2,1,0:T(8,128)}), f32[32,8,480]{2,1,0:T(8,128)S(1)}, u32[]{:S(2)}, u32[]{:S(2)}) async-start(f32[32,8,480]{2,1,0:T(8,128)} %broadcast_select_fusion), calls=%async_computation.1 | async-start | bytes 1048576 | tf_op jit(solution)/shard_map/all_to_all | solution.py:77
  29.0 0.8 iota_compare_fusion
  29.8 13.9 %all-to-all-done.1 = f32[32,8,480]{2,1,0:T(8,128)S(1)} async-done(((f32[32,8,480]{2,1,0:T(8,128)}), f32[32,8,480]{2,1,0:T(8,128)S(1)}, u32[]{:S(2)}, u32[]{:S(2)}) %all-to-all-start.1) | async-done | bytes 491552 | tf_op jit(solution)/shard_map/all_to_all | solution.py:77
  43.7 0.6 gather_fusion
  44.3 0.1 broadcast_select_fusion.1
  44.3 0.1 slice_bitcast_fusion
  44.4 0.1 fusion.41
  44.5 0.1 fusion.43
  44.6 0.1 reshape.279
  44.7 0.1 maximum_bitcast_fusion
  44.8 0.1 subtract_convert_fusion
  44.8 0.2 fusion.39
  45.0 3.7 %fusion.45 = (f32[8,4]{1,0:T(8,128)S(1)}, f32[8,4,4096]{2,1,0:T(4,128)S(1)}) fusion(bf16[8,1,80,4096]{3,2,1,0:T(8,128)(2,1)} %param.15, f32[8,4]{1,0:T(8,128)S(1)} %broadcast_multiply_fusion, pred[8,4096]{1,0:T(8,128)(4,1)S(1)} %get-tuple-element.17, pred[8,4096]{1,0:T(8,128)(4,1)S(1)} %get-tuple-element.18, bf16[8,4,40]{2,1,0:T(4,128)(2,1)S(1)} %get-tuple-element.10, ...), kind=kOutput, calls=%fused_computation.73 | convolution fusion | flops 21641216 | bytes 5838080 | tf_op jit(solution)/shard_map/sub | solution.py:111
  48.7 0.4 convert_reduce_fusion
  49.1 4.0 %fusion.20 = bf16[8,4,80]{2,1,0:T(4,128)(2,1)S(1)} fusion(bf16[8,1,80,4096]{3,2,1,0:T(8,128)(2,1)} %param.16, bf16[8,4,4096]{2,1,0:T(4,128)(2,1)S(1)} %get-tuple-element.6, pred[8,4096]{1,0:T(8,128)(4,1)S(1)} %get-tuple-element.18, f32[8,80]{1,0:T(8,128)S(1)} %fusion.41, f32[8,4]{1,0:T(8,128)S(1)} %get-tuple-element.5), kind=kOutput, calls=%fused_computation.14 | convolution fusion | flops 21110272 | bytes 5545600 | tf_op jit(solution)/shard_map/rkgw,rkhw->rkgh/dot_general | solution.py:118
  53.0 0.1 convert_element_type.64
  53.1 0.3 fusion.16
  53.4 0.7 reduce.10
  54.1 0.2 copy.25
  54.3 0.8 %reshape.300 = bf16[256,2,160]{2,1,0:T(2,128)(2,1)} reshape(bf16[256,320]{1,0:T(8,128)(2,1)S(1)} %copy.25) | data formatting | bytes 327680
  55.1 10.0 %all-to-all-start.2 = ((bf16[256,2,160]{2,1,0:T(2,128)(2,1)}), bf16[256,2,160]{2,1,0:T(2,128)(2,1)S(1)}, u32[]{:S(2)}, u32[]{:S(2)}) async-start(bf16[256,2,160]{2,1,0:T(2,128)(2,1)} %reshape.300), calls=%async_computation.2 | async-start | bytes 524288 | tf_op jit(solution)/shard_map/all_to_all | solution.py:130
  65.2 0.6 slice.36
  66.4 14.2 %all-to-all-done.2 = bf16[256,2,160]{2,1,0:T(2,128)(2,1)S(1)} async-done(((bf16[256,2,160]{2,1,0:T(2,128)(2,1)}), bf16[256,2,160]{2,1,0:T(2,128)(2,1)S(1)}, u32[]{:S(2)}, u32[]{:S(2)}) %all-to-all-start.2) | async-done | bytes 163872 | tf_op jit(solution)/shard_map/all_to_all | solution.py:130
  80.6 0.3 reshape.301
  80.9 0.1 dynamic-slice_reduce_fusion
  81.0 0.7 reshape.283
  (11 shorter events, 0.1 us)
Async XLA Ops:
  0.0 14.4 %copy-start = (bf16[2560,320]{0,1:T(8,128)(2,1)S(1)}, bf16[2560,320]{0,1:T(8,128)(2,1)}, u32[]{:S(2)}) copy-start(bf16[2560,320]{0,1:T(8,128)(2,1)} %param.12) | copy-start | bytes 4915204
  2.9 11.2 %all-to-all-start = ((bf16[8,2,1280]{2,1,0:T(2,128)(2,1)}), bf16[8,2,1280]{2,1,0:T(2,128)(2,1)S(1)}, u32[]{:S(2)}, u32[]{:S(2)}) async-start(bf16[8,2,1280]{2,1,0:T(2,128)(2,1)} %reshape.298), calls=%async_computation | async-start | bytes 81920 | tf_op jit(solution)/shard_map/all_to_all | solution.py:49
  18.5 25.2 %all-to-all-start.1 = ((f32[32,8,480]{2,1,0:T(8,128)}), f32[32,8,480]{2,1,0:T(8,128)S(1)}, u32[]{:S(2)}, u32[]{:S(2)}) async-start(f32[32,8,480]{2,1,0:T(8,128)} %broadcast_select_fusion), calls=%async_computation.1 | async-start | bytes 1048576 | tf_op jit(solution)/shard_map/all_to_all | solution.py:77
  55.1 25.5 %all-to-all-start.2 = ((bf16[256,2,160]{2,1,0:T(2,128)(2,1)}), bf16[256,2,160]{2,1,0:T(2,128)(2,1)S(1)}, u32[]{:S(2)}, u32[]{:S(2)}) async-start(bf16[256,2,160]{2,1,0:T(2,128)(2,1)} %reshape.300), calls=%async_computation.2 | async-start | bytes 524288 | tf_op jit(solution)/shard_map/all_to_all | solution.py:130

commit v6 on v5

--- a/solution.py
+++ b/solution.py
@@ -46,8 +46,9 @@
     query_width = w_query.shape[1]
     key_width = key_projection_weight.shape[1]
 
+    lane_rows = states.reshape(per_device * states.shape[1] // 128, 128)
     row_block = lax.all_to_all(
-        jnp.broadcast_to(states[None], (kv_count,) + states.shape), "kv", 0, 0, tiled=True
+        jnp.broadcast_to(lane_rows[None], (kv_count,) + lane_rows.shape), "kv", 0, 0, tiled=True
     ).reshape(group_rows, states.shape[1])
     wide_rows = row_block.astype(jnp.float32)
     inv_rms = lax.rsqrt(jnp.mean(wide_rows * wide_rows, axis=1, keepdims=True) + 1e-05)

time: 82.2 us -> 81.2 us (0.988)
  other arithmetic: 8.46 us -> 7.5 us
    broadcast_in_dim x1 -> x0, other arithmetic: 0.87 us -> none  [local(): jnp.broadcast_to(states[None], (kv_count,) + states.shape)]
    unnamed x7 -> x5, local copies, waits for them, and re-layouts: 1.93 us -> 1.27 us
where the time goes in v6:
time: 81.2 us; the launch traced here: 80.6 us
  waiting for transfers between devices  29.7 us (37%)
  starting transfers between devices  27 us (33%)
  matrix products  11.1 us (14%)
  other arithmetic  7.5 us (9%)
  local copies, waits for them, and re-layouts  4.54 us (6%)
    all_to_all x1, waiting for transfers between devices, local(): recv_out = lax.all_to_all(send_out, ('req', 'kv'), 0, 0, tiled=True)  14.2 us
    all_to_all x1, waiting for transfers between devices, local(): recv_rows = lax.all_to_all(send_rows, 'req', 0, 0, tiled=True)  13.9 us
    all_to_all x1, starting transfers between devices, local(): recv_rows = lax.all_to_all(send_rows, 'req', 0, 0, tiled=True)  10.5 us
    all_to_all x1, starting transfers between devices, local(): recv_out = lax.all_to_all(send_out, ('req', 'kv'), 0, 0, tiled=True)  10 us
    all_to_all x1, starting transfers between devices, local(): lax.all_to_all(jnp.broadcast_to(lane_rows[None], (kv_count,) + lane_rows....  6.45 us
    dot_general x1, matrix products, local(): jnp.einsum('rkgw,rkhw->rkgh', stale_weights, value_cache_slots, preferred...  3.96 us
    sub x1, matrix products, local(): expd = jnp.exp(scores - row_max)  3.66 us
  transfers between devices with their start and end apart: 3, of which 3 were waited for; matrix products, arithmetic and copies ran while one was open for 6% of the time, Pallas kernels for 0%

profile of v6, /device:TPU:1, one launch (start us, length us, event | category | flops | bytes accessed | tf_op | source)
XLA Modules:
  0.0 80.6 jit_solution(8462801071591495490)
XLA Ops:
  0.0 0.0 copy-start
  0.0 0.9 %reduce.7 = bf16[2560]{0:T(1024)(128)(2,1)S(1)} reduce(bf16[1,2560]{1,0:T(2,128)(2,1)} %param.10, bf16[]{:T(256)} %constant.72), dimensions={0}, to_apply=%param.10.reduce_sub_computation | reduce | bytes 10242 | tf_op args[0]
  0.9 0.6 broadcast_in_dim.133
  1.5 6.4 %all-to-all-start = ((bf16[8,20,128]{2,1,0:T(8,128)(2,1)}), bf16[8,20,128]{2,1,0:T(8,128)(2,1)S(1)}, u32[]{:S(2)}, u32[]{:S(2)}) async-start(bf16[8,20,128]{2,1,0:T(8,128)(2,1)} %broadcast_in_dim.133), calls=%async_computation | async-start | bytes 98304 | tf_op jit(solution)/shard_map/all_to_all | solution.py:50
  8.0 0.1 pad_add_fusion
  8.0 0.9 %select_reduce_fusion = s32[9]{0:T(128)S(1)} fusion(s32[256]{0:T(256)} %param.19, s32[9]{0:T(128)S(1)} %pad_add_fusion), kind=kLoop, calls=%fused_computation.37 | loop fusion | flops 6903 | bytes 1096 | tf_op jit(solution)/shard_map/reduce_sum | solution.py:72
  8.9 0.8 compare_and_fusion
  9.7 0.7 convert_element_type.63
  10.4 0.1 multiply_cosine_fusion.1
  10.5 0.7 convert_element_type.59
  11.2 1.6 %all-to-all-done = bf16[8,20,128]{2,1,0:T(8,128)(2,1)S(1)} async-done(((bf16[8,20,128]{2,1,0:T(8,128)(2,1)}), bf16[8,20,128]{2,1,0:T(8,128)(2,1)S(1)}, u32[]{:S(2)}, u32[]{:S(2)}) %all-to-all-start) | async-done | bytes 40992 | tf_op jit(solution)/shard_map/all_to_all | solution.py:50
  12.7 0.1 fusion.30
  12.9 0.0 copy-done
  12.9 0.5 fusion.49
  13.4 1.3 %fusion.23 = f32[8,80]{1,0:T(8,128)S(1)} fusion(bf16[2560,80]{0,1:T(8,128)(2,1)} %param.14, f32[2560]{0:T(1024)S(1)} %convert_element_type.59, f32[8]{0:T(128)S(1)} %add_rsqrt_fusion, bf16[8,20,128]{2,1,0:T(8,128)(2,1)S(1)} %all-to-all-done), kind=kOutput, calls=%fused_computation.16 | convolution fusion | flops 3360000 | bytes 463392 | tf_op jit(solution)/shard_map/dot_general | solution.py:61
  14.7 1.3 %fusion.47 = f32[8,80]{1,0:T(8,128)S(1)} fusion(bf16[2560,80]{0,1:T(8,128)(2,1)} %param.13, f32[2560]{0:T(1024)S(1)} %convert_element_type.59, f32[8]{0:T(128)S(1)} %add_rsqrt_fusion, bf16[8,20,128]{2,1,0:T(8,128)(2,1)S(1)} %all-to-all-done), kind=kOutput, calls=%fused_computation.74 | convolution fusion | flops 3358720 | bytes 463392 | tf_op jit(solution)/shard_map/dot_general | solution.py:59
  16.0 0.1 pad_maximum_fusion
  16.0 0.9 %broadcast_select_fusion = f32[32,8,480]{2,1,0:T(8,128)} fusion(f32[8,480]{1,0:T(8,128)S(1)} %pad_maximum_fusion, pred[32,8]{1,0:T(8,128)(4,1)S(1)} %iota_compare_fusion.4), kind=kLoop, calls=%fused_computation.20 | loop fusion | flops 122880 | bytes 507136 | tf_op jit(solution)/shard_map/jit(_where)/select_n | solution.py:77
  17.0 10.5 %all-to-all-start.1 = ((f32[32,8,480]{2,1,0:T(8,128)}), f32[32,8,480]{2,1,0:T(8,128)S(1)}, u32[]{:S(2)}, u32[]{:S(2)}) async-start(f32[32,8,480]{2,1,0:T(8,128)} %broadcast_select_fusion), calls=%async_computation.1 | async-start | bytes 1048576 | tf_op jit(solution)/shard_map/all_to_all | solution.py:78
  27.5 0.8 iota_compare_fusion
  28.3 13.9 %all-to-all-done.1 = f32[32,8,480]{2,1,0:T(8,128)S(1)} async-done(((f32[32,8,480]{2,1,0:T(8,128)}), f32[32,8,480]{2,1,0:T(8,128)S(1)}, u32[]{:S(2)}, u32[]{:S(2)}) %all-to-all-start.1) | async-done | bytes 491552 | tf_op jit(solution)/shard_map/all_to_all | solution.py:78
  42.2 0.6 gather_fusion
  42.7 0.1 broadcast_select_fusion.1
  42.8 0.1 slice_bitcast_fusion
  42.9 0.1 fusion.42
  42.9 0.1 fusion.44
  43.1 0.1 reshape.277
  43.1 0.1 maximum_bitcast_fusion
  43.2 0.1 subtract_convert_fusion
  43.3 0.2 fusion.40
  43.5 3.7 %fusion.51 = (f32[8,4]{1,0:T(8,128)S(1)}, f32[8,4,4096]{2,1,0:T(4,128)S(1)}) fusion(bf16[8,1,80,4096]{3,2,1,0:T(8,128)(2,1)} %param.15, f32[8,4]{1,0:T(8,128)S(1)} %broadcast_multiply_fusion, pred[8,4096]{1,0:T(8,128)(4,1)S(1)} %get-tuple-element.17, pred[8,4096]{1,0:T(8,128)(4,1)S(1)} %get-tuple-element.18, bf16[8,4,40]{2,1,0:T(4,128)(2,1)S(1)} %get-tuple-element.10, ...), kind=kOutput, calls=%fused_computation.76 | convolution fusion | flops 21641216 | bytes 5838080 | tf_op jit(solution)/shard_map/sub | solution.py:112
  47.2 0.4 convert_reduce_fusion
  47.5 4.0 %fusion.20 = bf16[8,4,80]{2,1,0:T(4,128)(2,1)S(1)} fusion(bf16[8,1,80,4096]{3,2,1,0:T(8,128)(2,1)} %param.16, bf16[8,4,4096]{2,1,0:T(4,128)(2,1)S(1)} %get-tuple-element.6, pred[8,4096]{1,0:T(8,128)(4,1)S(1)} %get-tuple-element.18, f32[8,80]{1,0:T(8,128)S(1)} %fusion.42, f32[8,4]{1,0:T(8,128)S(1)} %get-tuple-element.5), kind=kOutput, calls=%fused_computation.14 | convolution fusion | flops 21110272 | bytes 5545600 | tf_op jit(solution)/shard_map/rkgw,rkhw->rkgh/dot_general | solution.py:119
  51.5 0.1 convert_element_type.68
  51.6 0.3 fusion.16
  51.9 0.5 broadcast.196
  52.4 0.7 reduce.10
  53.1 0.2 copy.25
  53.3 0.8 %reshape.296 = bf16[256,2,160]{2,1,0:T(2,128)(2,1)} reshape(bf16[256,320]{1,0:T(8,128)(2,1)S(1)} %copy.25) | data formatting | bytes 327680
  54.1 10.0 %all-to-all-start.2 = ((bf16[256,2,160]{2,1,0:T(2,128)(2,1)}), bf16[256,2,160]{2,1,0:T(2,128)(2,1)S(1)}, u32[]{:S(2)}, u32[]{:S(2)}) async-start(bf16[256,2,160]{2,1,0:T(2,128)(2,1)} %reshape.296), calls=%async_computation.2 | async-start | bytes 524288 | tf_op jit(solution)/shard_map/all_to_all | solution.py:131
  64.1 0.6 slice.36
  65.3 14.2 %all-to-all-done.2 = bf16[256,2,160]{2,1,0:T(2,128)(2,1)S(1)} async-done(((bf16[256,2,160]{2,1,0:T(2,128)(2,1)}), bf16[256,2,160]{2,1,0:T(2,128)(2,1)S(1)}, u32[]{:S(2)}, u32[]{:S(2)}) %all-to-all-start.2) | async-done | bytes 163872 | tf_op jit(solution)/shard_map/all_to_all | solution.py:131
  79.6 0.3 reshape.297
  79.9 0.1 dynamic-slice_reduce_fusion
  79.9 0.7 reshape.281
  (9 shorter events, 0.1 us)
Async XLA Ops:
  0.0 12.9 %copy-start = (bf16[2560,320]{0,1:T(8,128)(2,1)S(1)}, bf16[2560,320]{0,1:T(8,128)(2,1)}, u32[]{:S(2)}) copy-start(bf16[2560,320]{0,1:T(8,128)(2,1)} %param.12) | copy-start | bytes 4915204
  1.5 11.3 %all-to-all-start = ((bf16[8,20,128]{2,1,0:T(8,128)(2,1)}), bf16[8,20,128]{2,1,0:T(8,128)(2,1)S(1)}, u32[]{:S(2)}, u32[]{:S(2)}) async-start(bf16[8,20,128]{2,1,0:T(8,128)(2,1)} %broadcast_in_dim.133), calls=%async_computation | async-start | bytes 98304 | tf_op jit(solution)/shard_map/all_to_all | solution.py:50
  17.0 25.2 %all-to-all-start.1 = ((f32[32,8,480]{2,1,0:T(8,128)}), f32[32,8,480]{2,1,0:T(8,128)S(1)}, u32[]{:S(2)}, u32[]{:S(2)}) async-start(f32[32,8,480]{2,1,0:T(8,128)} %broadcast_select_fusion), calls=%async_computation.1 | async-start | bytes 1048576 | tf_op jit(solution)/shard_map/all_to_all | solution.py:78
  54.1 25.5 %all-to-all-start.2 = ((bf16[256,2,160]{2,1,0:T(2,128)(2,1)}), bf16[256,2,160]{2,1,0:T(2,128)(2,1)S(1)}, u32[]{:S(2)}, u32[]{:S(2)}) async-start(bf16[256,2,160]{2,1,0:T(2,128)(2,1)} %reshape.296), calls=%async_computation.2 | async-start | bytes 524288 | tf_op jit(solution)/shard_map/all_to_all | solution.py:131

commit v7 on v6

--- a/solution.py
+++ b/solution.py
@@ -124,10 +124,17 @@
         jnp.bfloat16
     )
 
-    pick_out = (
-        jnp.arange(total_rows, dtype=jnp.int32)[:, None] == dealt_ids[None, :]
-    ).astype(jnp.bfloat16)
-    send_out = jnp.dot(pick_out, attended, preferred_element_type=jnp.float32).astype(jnp.bfloat16)
+    inverse = jnp.sum(
+        jnp.where(dealing[None, :] == places[:, None], places[None, :], 0), axis=1
+    )
+    in_group = inverse // group_rows == group_index
+    slot_of = jnp.where(in_group, inverse % group_rows, 0)
+    block_width = attended.shape[1]
+    halves = 2 if block_width % 2 == 0 else 1
+    split_blocks = attended.reshape(group_rows, halves, block_width // halves)
+    send_out = jnp.where(
+        in_group[:, None, None], jnp.take(split_blocks, slot_of, axis=0), jnp.zeros((), jnp.bfloat16)
+    )
     recv_out = lax.all_to_all(send_out, ("req", "kv"), 0, 0, tiled=True)
     own_group = lookup_groups[group_rows]
     blocks = lax.dynamic_slice_in_dim(recv_out, own_group * kv_count, kv_count)

time: 81.2 us -> 82.6 us (1.017)
  other arithmetic: 7.5 us -> 9.74 us
  waiting for transfers between devices: 29.7 us -> 28.8 us
    select_n x0 -> x2, other arithmetic: none -> 2.14 us  [the longest x1 2.13 us: local(): jnp.where(in_group[:, None, None], jnp.take(split_blocks, slot_of, axis=0...]
    unnamed x5 -> x2, local copies, waits for them, and re-layouts: 1.27 us -> 0.01 us
    gather x0 -> x1, local copies, waits for them, and re-layouts: none -> 1.24 us  [local(): jnp.take(split_blocks, slot_of, axis=0)]
    all_to_all x1, waiting for transfers between devices: 1.57 us -> 0.73 us  [local(): lax.all_to_all(jnp.broadcast_to(lane_rows[None], (kv_count,) + lane_rows....]
    all_to_all x1, starting transfers between devices: 10 us -> 10.8 us  [local(): recv_out = lax.all_to_all(send_out, ('req', 'kv'), 0, 0, tiled=True)]
  transfers between devices with their start and end apart: 3 -> 3, of which waited for: 3 -> 3; matrix products, arithmetic and copies ran while one was open for 6% -> 7% of each run, Pallas kernels for 0% -> 0%
where the time goes in v7:
time: 82.6 us; the launch traced here: 82 us
  waiting for transfers between devices  28.8 us (35%)
  starting transfers between devices  27.8 us (34%)
  matrix products  10.9 us (13%)
  other arithmetic  9.74 us (12%)
  local copies, waits for them, and re-layouts  3.97 us (5%)
    all_to_all x1, waiting for transfers between devices, local(): recv_out = lax.all_to_all(send_out, ('req', 'kv'), 0, 0, tiled=True)  14.2 us
    all_to_all x1, waiting for transfers between devices, local(): recv_rows = lax.all_to_all(send_rows, 'req', 0, 0, tiled=True)  13.9 us
    all_to_all x1, starting transfers between devices, local(): recv_out = lax.all_to_all(send_out, ('req', 'kv'), 0, 0, tiled=True)  10.8 us
    all_to_all x1, starting transfers between devices, local(): recv_rows = lax.all_to_all(send_rows, 'req', 0, 0, tiled=True)  10.5 us
    all_to_all x1, starting transfers between devices, local(): lax.all_to_all(jnp.broadcast_to(lane_rows[None], (kv_count,) + lane_rows....  6.45 us
    dot_general x1, matrix products, local(): jnp.einsum('rkgw,rkhw->rkgh', stale_weights, value_cache_slots, preferred...  3.96 us
    sub x1, matrix products, local(): expd = jnp.exp(scores - row_max)  3.64 us
    select_n x1, other arithmetic, local(): jnp.where(in_group[:, None, None], jnp.take(split_blocks, slot_of, axis=0...  2.13 us
  transfers between devices with their start and end apart: 3, of which 3 were waited for; matrix products, arithmetic and copies ran while one was open for 7% of the time, Pallas kernels for 0%

profile of v7, /device:TPU:1, one launch (start us, length us, event | category | flops | bytes accessed | tf_op | source)
XLA Modules:
  0.0 82.0 jit_solution(1310360571765313168)
XLA Ops:
  0.0 0.0 copy-start
  0.0 0.9 %reduce.7 = bf16[2560]{0:T(1024)(128)(2,1)S(1)} reduce(bf16[1,2560]{1,0:T(2,128)(2,1)} %param.10, bf16[]{:T(256)} %constant.106), dimensions={0}, to_apply=%param.10.reduce_sub_computation | reduce | bytes 10242 | tf_op args[0]
  0.9 0.6 broadcast_in_dim.175
  1.5 6.4 %all-to-all-start = ((bf16[8,20,128]{2,1,0:T(8,128)(2,1)}), bf16[8,20,128]{2,1,0:T(8,128)(2,1)S(1)}, u32[]{:S(2)}, u32[]{:S(2)}) async-start(bf16[8,20,128]{2,1,0:T(8,128)(2,1)} %broadcast_in_dim.175), calls=%async_computation | async-start | bytes 98304 | tf_op jit(solution)/shard_map/all_to_all | solution.py:50
  8.0 0.8 select_reduce_fusion
  8.8 0.1 pad_add_fusion
  8.9 0.9 %select_reduce_fusion.1 = s32[9]{0:T(128)S(1)} fusion(s32[256]{0:T(256)} %param.19, s32[9]{0:T(128)S(1)} %pad_add_fusion), kind=kLoop, calls=%fused_computation.38 | loop fusion | flops 6903 | bytes 1096 | tf_op jit(solution)/shard_map/reduce_sum | solution.py:72
  9.7 0.8 compare_and_fusion
  10.5 0.7 convert_element_type.60
  11.2 0.1 multiply_cosine_fusion.1
  11.3 0.7 convert_element_type.56
  12.0 0.7 all-to-all-done
  12.7 0.1 fusion.29
  12.9 0.0 copy-done
  12.9 0.5 fusion.49
  13.4 1.3 %fusion.22 = f32[8,80]{1,0:T(8,128)S(1)} fusion(bf16[2560,80]{0,1:T(8,128)(2,1)} %param.14, f32[2560]{0:T(1024)S(1)} %convert_element_type.56, f32[8]{0:T(128)S(1)} %add_rsqrt_fusion, bf16[8,20,128]{2,1,0:T(8,128)(2,1)S(1)} %all-to-all-done), kind=kOutput, calls=%fused_computation.15 | convolution fusion | flops 3360000 | bytes 463392 | tf_op jit(solution)/shard_map/dot_general | solution.py:61
  14.7 1.3 %fusion.47 = f32[8,80]{1,0:T(8,128)S(1)} fusion(bf16[2560,80]{0,1:T(8,128)(2,1)} %param.13, f32[2560]{0:T(1024)S(1)} %convert_element_type.56, f32[8]{0:T(128)S(1)} %add_rsqrt_fusion, bf16[8,20,128]{2,1,0:T(8,128)(2,1)S(1)} %all-to-all-done), kind=kOutput, calls=%fused_computation.94 | convolution fusion | flops 3358720 | bytes 463392 | tf_op jit(solution)/shard_map/dot_general | solution.py:59
  16.0 0.1 pad_maximum_fusion
  16.0 0.9 %broadcast_select_fusion.2 = f32[32,8,480]{2,1,0:T(8,128)} fusion(f32[8,480]{1,0:T(8,128)S(1)} %pad_maximum_fusion, pred[32,8]{1,0:T(8,128)(4,1)S(1)} %iota_compare_fusion.3), kind=kLoop, calls=%fused_computation.21 | loop fusion | flops 122880 | bytes 507136 | tf_op jit(solution)/shard_map/jit(_where)/select_n | solution.py:77
  17.0 10.5 %all-to-all-start.1 = ((f32[32,8,480]{2,1,0:T(8,128)}), f32[32,8,480]{2,1,0:T(8,128)S(1)}, u32[]{:S(2)}, u32[]{:S(2)}) async-start(f32[32,8,480]{2,1,0:T(8,128)} %broadcast_select_fusion.2), calls=%async_computation.1 | async-start | bytes 1048576 | tf_op jit(solution)/shard_map/all_to_all | solution.py:78
  27.5 0.8 iota_compare_fusion.1
  28.3 13.9 %all-to-all-done.1 = f32[32,8,480]{2,1,0:T(8,128)S(1)} async-done(((f32[32,8,480]{2,1,0:T(8,128)}), f32[32,8,480]{2,1,0:T(8,128)S(1)}, u32[]{:S(2)}, u32[]{:S(2)}) %all-to-all-start.1) | async-done | bytes 491552 | tf_op jit(solution)/shard_map/all_to_all | solution.py:78
  42.2 0.6 gather_fusion
  42.7 0.1 broadcast_select_fusion.3
  42.8 0.1 slice_bitcast_fusion
  42.9 0.1 fusion.40
  42.9 0.1 fusion.42
  43.1 0.1 reshape.380
  43.1 0.1 maximum_bitcast_fusion
  43.2 0.1 subtract_convert_fusion
  43.3 0.2 fusion.38
  43.5 3.6 %fusion.52 = (f32[8,4]{1,0:T(8,128)S(1)}, f32[8,4,4096]{2,1,0:T(4,128)S(1)}) fusion(bf16[8,1,80,4096]{3,2,1,0:T(8,128)(2,1)} %param.15, f32[8,4]{1,0:T(8,128)S(1)} %broadcast_multiply_fusion, pred[8,4096]{1,0:T(8,128)(4,1)S(1)} %get-tuple-element.19, pred[8,4096]{1,0:T(8,128)(4,1)S(1)} %get-tuple-element.20, bf16[8,4,40]{2,1,0:T(4,128)(2,1)S(1)} %get-tuple-element.12, ...), kind=kOutput, calls=%fused_computation.96 | convolution fusion | flops 21641216 | bytes 5838080 | tf_op jit(solution)/shard_map/sub | solution.py:112
  47.2 0.4 convert_reduce_fusion
  47.5 4.0 %fusion.19 = bf16[8,4,80]{2,1,0:T(4,128)(2,1)S(1)} fusion(bf16[8,1,80,4096]{3,2,1,0:T(8,128)(2,1)} %param.16, bf16[8,4,4096]{2,1,0:T(4,128)(2,1)S(1)} %get-tuple-element.8, pred[8,4096]{1,0:T(8,128)(4,1)S(1)} %get-tuple-element.20, f32[8,80]{1,0:T(8,128)S(1)} %fusion.40, f32[8,4]{1,0:T(8,128)S(1)} %get-tuple-element.7), kind=kOutput, calls=%fused_computation.13 | convolution fusion | flops 21110272 | bytes 5545600 | tf_op jit(solution)/shard_map/rkgw,rkhw->rkgh/dot_general | solution.py:119
  51.5 0.1 convert_element_type.65
  51.6 1.2 %gather_fusion.1 = bf16[256,2,160]{2,1,0:T(2,128)(2,1)S(1)} fusion(bf16[8,2,160]{2,1,0:T(2,128)(2,1)S(1)} %convert_element_type.65, s32[1024]{0:T(1024)S(1)} %pad_clamp_fusion), kind=kCustom, calls=%fused_computation.1 | custom fusion | bytes 328704 | tf_op jit(solution)/shard_map/jit(_take)/gather | solution.py:136
  52.8 2.1 %broadcast_select_fusion.1 = bf16[256,2,160]{2,1,0:T(2,128)(2,1)} fusion(pred[256]{0:T(512)(128)(4,1)S(1)} %get-tuple-element.6, bf16[256,2,160]{2,1,0:T(2,128)(2,1)S(1)} %gather_fusion.1, pred[256]{0:T(512)(128)(4,1)S(1)} %get-tuple-element.5), kind=kLoop, calls=%fused_computation.19 | loop fusion | flops 163840 | bytes 328192 | tf_op jit(solution)/shard_map/jit(_where)/select_n | solution.py:135
  55.0 10.8 %all-to-all-start.2 = ((bf16[256,2,160]{2,1,0:T(2,128)(2,1)}), bf16[256,2,160]{2,1,0:T(2,128)(2,1)S(1)}, u32[]{:S(2)}, u32[]{:S(2)}) async-start(bf16[256,2,160]{2,1,0:T(2,128)(2,1)} %broadcast_select_fusion.1), calls=%async_computation.2 | async-start | bytes 524288 | tf_op jit(solution)/shard_map/all_to_all | solution.py:138
  65.8 0.6 slice.36
  67.0 14.2 %all-to-all-done.2 = bf16[256,2,160]{2,1,0:T(2,128)(2,1)S(1)} async-done(((bf16[256,2,160]{2,1,0:T(2,128)(2,1)}), bf16[256,2,160]{2,1,0:T(2,128)(2,1)S(1)}, u32[]{:S(2)}, u32[]{:S(2)}) %all-to-all-start.2) | async-done | bytes 163872 | tf_op jit(solution)/shard_map/all_to_all | solution.py:138
  81.3 0.7 reshape.384
  (12 shorter events, 0.1 us)
Async XLA Ops:
  0.0 12.9 %copy-start = (bf16[2560,320]{0,1:T(8,128)(2,1)S(1)}, bf16[2560,320]{0,1:T(8,128)(2,1)}, u32[]{:S(2)}) copy-start(bf16[2560,320]{0,1:T(8,128)(2,1)} %param.12) | copy-start | bytes 4915204
  1.5 11.3 %all-to-all-start = ((bf16[8,20,128]{2,1,0:T(8,128)(2,1)}), bf16[8,20,128]{2,1,0:T(8,128)(2,1)S(1)}, u32[]{:S(2)}, u32[]{:S(2)}) async-start(bf16[8,20,128]{2,1,0:T(8,128)(2,1)} %broadcast_in_dim.175), calls=%async_computation | async-start | bytes 98304 | tf_op jit(solution)/shard_map/all_to_all | solution.py:50
  17.0 25.2 %all-to-all-start.1 = ((f32[32,8,480]{2,1,0:T(8,128)}), f32[32,8,480]{2,1,0:T(8,128)S(1)}, u32[]{:S(2)}, u32[]{:S(2)}) async-start(f32[32,8,480]{2,1,0:T(8,128)} %broadcast_select_fusion.2), calls=%async_computation.1 | async-start | bytes 1048576 | tf_op jit(solution)/shard_map/all_to_all | solution.py:78
  55.0 26.3 %all-to-all-start.2 = ((bf16[256,2,160]{2,1,0:T(2,128)(2,1)}), bf16[256,2,160]{2,1,0:T(2,128)(2,1)S(1)}, u32[]{:S(2)}, u32[]{:S(2)}) async-start(bf16[256,2,160]{2,1,0:T(2,128)(2,1)} %broadcast_select_fusion.1), calls=%async_computation.2 | async-start | bytes 524288 | tf_op jit(solution)/shard_map/all_to_all | solution.py:138

commit v8 on v7

--- a/solution.py
+++ b/solution.py
@@ -128,13 +128,13 @@
         jnp.where(dealing[None, :] == places[:, None], places[None, :], 0), axis=1
     )
     in_group = inverse // group_rows == group_index
-    slot_of = jnp.where(in_group, inverse % group_rows, 0)
+    slot_of = jnp.where(in_group, inverse % group_rows, group_rows)
     block_width = attended.shape[1]
     halves = 2 if block_width % 2 == 0 else 1
-    split_blocks = attended.reshape(group_rows, halves, block_width // halves)
-    send_out = jnp.where(
-        in_group[:, None, None], jnp.take(split_blocks, slot_of, axis=0), jnp.zeros((), jnp.bfloat16)
-    )
+    split_blocks = jnp.concatenate(
+        [attended, jnp.zeros((1, block_width), jnp.bfloat16)], axis=0
+    ).reshape(group_rows + 1, halves, block_width // halves)
+    send_out = split_blocks.at[slot_of].get(mode="promise_in_bounds")
     recv_out = lax.all_to_all(send_out, ("req", "kv"), 0, 0, tiled=True)
     own_group = lookup_groups[group_rows]
     blocks = lax.dynamic_slice_in_dim(recv_out, own_group * kv_count, kv_count)

time: 82.6 us -> 81.2 us (0.983)
  other arithmetic: 9.74 us -> 7.59 us
    select_n x2 -> x1, other arithmetic: 2.14 us -> 0.01 us  [local(): send_out = split_blocks.at[slot_of].get(mode='promise_in_bounds')]
where the time goes in v8:
time: 81.2 us; the launch traced here: 80.6 us
  waiting for transfers between devices  28.9 us (36%)
  starting transfers between devices  27.8 us (34%)
  matrix products  10.9 us (13%)
  other arithmetic  7.59 us (9%)
  local copies, waits for them, and re-layouts  4.73 us (6%)
    all_to_all x1, waiting for transfers between devices, local(): recv_out = lax.all_to_all(send_out, ('req', 'kv'), 0, 0, tiled=True)  14.2 us
    all_to_all x1, waiting for transfers between devices, local(): recv_rows = lax.all_to_all(send_rows, 'req', 0, 0, tiled=True)  13.9 us
    all_to_all x1, starting transfers between devices, local(): recv_out = lax.all_to_all(send_out, ('req', 'kv'), 0, 0, tiled=True)  10.8 us
    all_to_all x1, starting transfers between devices, local(): recv_rows = lax.all_to_all(send_rows, 'req', 0, 0, tiled=True)  10.5 us
    all_to_all x1, starting transfers between devices, local(): lax.all_to_all(jnp.broadcast_to(lane_rows[None], (kv_count,) + lane_rows....  6.45 us
    dot_general x1, matrix products, local(): jnp.einsum('rkgw,rkhw->rkgh', stale_weights, value_cache_slots, preferred...  3.95 us
    sub x1, matrix products, local(): expd = jnp.exp(scores - row_max)  3.66 us
    gather x1, local copies, waits for them, and re-layouts, local(): send_out = split_blocks.at[slot_of].get(mode='promise_in_bounds')  1.9 us
  transfers between devices with their start and end apart: 3, of which 3 were waited for; matrix products, arithmetic and copies ran while one was open for 7% of the time, Pallas kernels for 0%

profile of v8, /device:TPU:1, one launch (start us, length us, event | category | flops | bytes accessed | tf_op | source)
XLA Modules:
  0.0 80.6 jit_solution(2859049158518932141)
XLA Ops:
  0.0 0.0 copy-start
  0.0 0.9 %reduce.7 = bf16[2560]{0:T(1024)(128)(2,1)S(1)} reduce(bf16[1,2560]{1,0:T(2,128)(2,1)} %param.10, bf16[]{:T(256)} %constant.97), dimensions={0}, to_apply=%param.10.reduce_sub_computation | reduce | bytes 10242 | tf_op args[0]
  0.9 0.6 broadcast_in_dim.150
  1.5 6.4 %all-to-all-start = ((bf16[8,20,128]{2,1,0:T(8,128)(2,1)}), bf16[8,20,128]{2,1,0:T(8,128)(2,1)S(1)}, u32[]{:S(2)}, u32[]{:S(2)}) async-start(bf16[8,20,128]{2,1,0:T(8,128)(2,1)} %broadcast_in_dim.150), calls=%async_computation | async-start | bytes 98304 | tf_op jit(solution)/shard_map/all_to_all | solution.py:50
  8.0 0.8 select_reduce_fusion
  8.8 0.1 pad_add_fusion
  8.9 0.9 %select_reduce_fusion.1 = s32[9]{0:T(128)S(1)} fusion(s32[256]{0:T(256)} %param.19, s32[9]{0:T(128)S(1)} %pad_add_fusion), kind=kLoop, calls=%fused_computation.36 | loop fusion | flops 6903 | bytes 1096 | tf_op jit(solution)/shard_map/reduce_sum | solution.py:72
  9.7 0.8 compare_and_fusion
  10.5 0.7 convert_element_type.59
  11.2 0.1 multiply_cosine_fusion.1
  11.3 0.7 convert_element_type.55
  12.0 0.8 all-to-all-done
  12.7 0.1 fusion.29
  12.9 0.0 copy-done
  12.9 0.5 fusion.47
  13.4 1.3 %fusion.22 = f32[8,80]{1,0:T(8,128)S(1)} fusion(bf16[2560,80]{0,1:T(8,128)(2,1)} %param.14, f32[2560]{0:T(1024)S(1)} %convert_element_type.55, f32[8]{0:T(128)S(1)} %add_rsqrt_fusion, bf16[8,20,128]{2,1,0:T(8,128)(2,1)S(1)} %all-to-all-done), kind=kOutput, calls=%fused_computation.15 | convolution fusion | flops 3360000 | bytes 463392 | tf_op jit(solution)/shard_map/dot_general | solution.py:61
  14.7 1.3 %fusion.45 = f32[8,80]{1,0:T(8,128)S(1)} fusion(bf16[2560,80]{0,1:T(8,128)(2,1)} %param.13, f32[2560]{0:T(1024)S(1)} %convert_element_type.55, f32[8]{0:T(128)S(1)} %add_rsqrt_fusion, bf16[8,20,128]{2,1,0:T(8,128)(2,1)S(1)} %all-to-all-done), kind=kOutput, calls=%fused_computation.81 | convolution fusion | flops 3358720 | bytes 463392 | tf_op jit(solution)/shard_map/dot_general | solution.py:59
  16.0 0.1 pad_maximum_fusion
  16.0 0.9 %broadcast_select_fusion = f32[32,8,480]{2,1,0:T(8,128)} fusion(f32[8,480]{1,0:T(8,128)S(1)} %pad_maximum_fusion, pred[32,8]{1,0:T(8,128)(4,1)S(1)} %iota_compare_fusion.3), kind=kLoop, calls=%fused_computation.21 | loop fusion | flops 122880 | bytes 507136 | tf_op jit(solution)/shard_map/jit(_where)/select_n | solution.py:77
  17.0 10.5 %all-to-all-start.1 = ((f32[32,8,480]{2,1,0:T(8,128)}), f32[32,8,480]{2,1,0:T(8,128)S(1)}, u32[]{:S(2)}, u32[]{:S(2)}) async-start(f32[32,8,480]{2,1,0:T(8,128)} %broadcast_select_fusion), calls=%async_computation.1 | async-start | bytes 1048576 | tf_op jit(solution)/shard_map/all_to_all | solution.py:78
  27.5 0.8 iota_compare_fusion.1
  28.3 13.9 %all-to-all-done.1 = f32[32,8,480]{2,1,0:T(8,128)S(1)} async-done(((f32[32,8,480]{2,1,0:T(8,128)}), f32[32,8,480]{2,1,0:T(8,128)S(1)}, u32[]{:S(2)}, u32[]{:S(2)}) %all-to-all-start.1) | async-done | bytes 491552 | tf_op jit(solution)/shard_map/all_to_all | solution.py:78
  42.2 0.6 gather_fusion
  42.7 0.1 broadcast_select_fusion.1
  42.8 0.1 slice_bitcast_fusion
  42.9 0.1 fusion.40
  42.9 0.1 fusion.42
  43.1 0.1 reshape.358
  43.1 0.1 maximum_bitcast_fusion
  43.2 0.1 subtract_convert_fusion
  43.3 0.2 fusion.38
  43.5 3.7 %fusion.49 = (f32[8,4]{1,0:T(8,128)S(1)}, f32[8,4,4096]{2,1,0:T(4,128)S(1)}) fusion(bf16[8,1,80,4096]{3,2,1,0:T(8,128)(2,1)} %param.15, f32[8,4]{1,0:T(8,128)S(1)} %broadcast_multiply_fusion, pred[8,4096]{1,0:T(8,128)(4,1)S(1)} %get-tuple-element.17, pred[8,4096]{1,0:T(8,128)(4,1)S(1)} %get-tuple-element.18, bf16[8,4,40]{2,1,0:T(4,128)(2,1)S(1)} %get-tuple-element.10, ...), kind=kOutput, calls=%fused_computation.83 | convolution fusion | flops 21641216 | bytes 5838080 | tf_op jit(solution)/shard_map/sub | solution.py:112
  47.2 0.4 convert_reduce_fusion
  47.5 4.0 %fusion.19 = bf16[8,4,80]{2,1,0:T(4,128)(2,1)S(1)} fusion(bf16[8,1,80,4096]{3,2,1,0:T(8,128)(2,1)} %param.16, bf16[8,4,4096]{2,1,0:T(4,128)(2,1)S(1)} %get-tuple-element.6, pred[8,4096]{1,0:T(8,128)(4,1)S(1)} %get-tuple-element.18, f32[8,80]{1,0:T(8,128)S(1)} %fusion.40, f32[8,4]{1,0:T(8,128)S(1)} %get-tuple-element.5), kind=kOutput, calls=%fused_computation.13 | convolution fusion | flops 21110272 | bytes 5545600 | tf_op jit(solution)/shard_map/rkgw,rkhw->rkgh/dot_general | solution.py:119
  51.5 0.1 convert_element_type.64
  51.6 0.1 reshape.362
  51.7 1.9 %gather_fusion.1 = bf16[256,2,160]{2,1,0:T(2,128)(2,1)} fusion(bf16[9,2,160]{2,1,0:T(2,128)(2,1)S(1)} %reshape.362, s32[1024]{0:T(1024)S(1)} %pad_clamp_fusion), kind=kCustom, calls=%fused_computation.1 | custom fusion | bytes 328704 | tf_op jit(solution)/shard_map/gather | solution.py:137
  53.6 10.8 %all-to-all-start.2 = ((bf16[256,2,160]{2,1,0:T(2,128)(2,1)}), bf16[256,2,160]{2,1,0:T(2,128)(2,1)S(1)}, u32[]{:S(2)}, u32[]{:S(2)}) async-start(bf16[256,2,160]{2,1,0:T(2,128)(2,1)} %gather_fusion.1), calls=%async_computation.2 | async-start | bytes 524288 | tf_op jit(solution)/shard_map/all_to_all | solution.py:138
  64.4 0.6 slice.36
  65.7 14.2 %all-to-all-done.2 = bf16[256,2,160]{2,1,0:T(2,128)(2,1)S(1)} async-done(((bf16[256,2,160]{2,1,0:T(2,128)(2,1)}), bf16[256,2,160]{2,1,0:T(2,128)(2,1)S(1)}, u32[]{:S(2)}, u32[]{:S(2)}) %all-to-all-start.2) | async-done | bytes 163872 | tf_op jit(solution)/shard_map/all_to_all | solution.py:138
  79.9 0.7 reshape.363
  (12 shorter events, 0.1 us)
Async XLA Ops:
  0.0 12.9 %copy-start = (bf16[2560,320]{0,1:T(8,128)(2,1)S(1)}, bf16[2560,320]{0,1:T(8,128)(2,1)}, u32[]{:S(2)}) copy-start(bf16[2560,320]{0,1:T(8,128)(2,1)} %param.12) | copy-start | bytes 4915204
  1.5 11.3 %all-to-all-start = ((bf16[8,20,128]{2,1,0:T(8,128)(2,1)}), bf16[8,20,128]{2,1,0:T(8,128)(2,1)S(1)}, u32[]{:S(2)}, u32[]{:S(2)}) async-start(bf16[8,20,128]{2,1,0:T(8,128)(2,1)} %broadcast_in_dim.150), calls=%async_computation | async-start | bytes 98304 | tf_op jit(solution)/shard_map/all_to_all | solution.py:50
  17.0 25.2 %all-to-all-start.1 = ((f32[32,8,480]{2,1,0:T(8,128)}), f32[32,8,480]{2,1,0:T(8,128)S(1)}, u32[]{:S(2)}, u32[]{:S(2)}) async-start(f32[32,8,480]{2,1,0:T(8,128)} %broadcast_select_fusion), calls=%async_computation.1 | async-start | bytes 1048576 | tf_op jit(solution)/shard_map/all_to_all | solution.py:78
  53.6 26.3 %all-to-all-start.2 = ((bf16[256,2,160]{2,1,0:T(2,128)(2,1)}), bf16[256,2,160]{2,1,0:T(2,128)(2,1)S(1)}, u32[]{:S(2)}, u32[]{:S(2)}) async-start(bf16[256,2,160]{2,1,0:T(2,128)(2,1)} %gather_fusion.1), calls=%async_computation.2 | async-start | bytes 524288 | tf_op jit(solution)/shard_map/all_to_all | solution.py:138

commit v9 on v6

--- a/solution.py
+++ b/solution.py
@@ -46,7 +46,7 @@
     query_width = w_query.shape[1]
     key_width = key_projection_weight.shape[1]
 
-    lane_rows = states.reshape(per_device * states.shape[1] // 128, 128)
+    lane_rows = states.astype(jnp.float32).reshape(per_device * states.shape[1] // 128, 128)
     row_block = lax.all_to_all(
         jnp.broadcast_to(lane_rows[None], (kv_count,) + lane_rows.shape), "kv", 0, 0, tiled=True
     ).reshape(group_rows, states.shape[1])

time: 81.2 us -> 81.2 us (level)
    unnamed x1 -> x0, other arithmetic: 0.86 us -> none
    broadcast_in_dim x0 -> x1, other arithmetic: none -> 0.85 us  [local(): jnp.broadcast_to(lane_rows[None], (kv_count,) + lane_rows.shape)]
where the time goes in v9:
time: 81.2 us; the launch traced here: 80.6 us
  waiting for transfers between devices  29.8 us (37%)
  starting transfers between devices  26.8 us (33%)
  matrix products  11 us (14%)
  other arithmetic  7.59 us (9%)
  local copies, waits for them, and re-layouts  4.54 us (6%)
    all_to_all x1, waiting for transfers between devices, local(): recv_out = lax.all_to_all(send_out, ('req', 'kv'), 0, 0, tiled=True)  14.2 us
    all_to_all x1, waiting for transfers between devices, local(): recv_rows = lax.all_to_all(send_rows, 'req', 0, 0, tiled=True)  13.8 us
    all_to_all x1, starting transfers between devices, local(): recv_rows = lax.all_to_all(send_rows, 'req', 0, 0, tiled=True)  10.5 us
    all_to_all x1, starting transfers between devices, local(): recv_out = lax.all_to_all(send_out, ('req', 'kv'), 0, 0, tiled=True)  9.87 us
    all_to_all x1, starting transfers between devices, local(): lax.all_to_all(jnp.broadcast_to(lane_rows[None], (kv_count,) + lane_rows....  6.46 us
    dot_general x1, matrix products, local(): jnp.einsum('rkgw,rkhw->rkgh', stale_weights, value_cache_slots, preferred...  3.96 us
    sub x1, matrix products, local(): expd = jnp.exp(scores - row_max)  3.66 us
    all_to_all x1, waiting for transfers between devices, local(): lax.all_to_all(jnp.broadcast_to(lane_rows[None], (kv_count,) + lane_rows....  1.77 us
  transfers between devices with their start and end apart: 3, of which 3 were waited for; matrix products, arithmetic and copies ran while one was open for 6% of the time, Pallas kernels for 0%

profile of v9, /device:TPU:1, one launch (start us, length us, event | category | flops | bytes accessed | tf_op | source)
XLA Modules:
  0.0 80.6 jit_solution(9695193249449061079)
XLA Ops:
  0.0 0.0 copy-start
  0.0 0.9 %convert_reduce_fusion.1 = f32[2560]{0:T(1024)S(1)} fusion(bf16[1,2560]{1,0:T(2,128)(2,1)} %param.10), kind=kLoop, calls=%fused_computation.37 | loop fusion | flops 2560 | bytes 15360 | tf_op jit(solution)/shard_map/broadcast_in_dim | solution.py:51
  0.9 0.6 broadcast_in_dim.137
  1.5 6.5 %all-to-all-start = ((f32[8,20,128]{2,1,0:T(8,128)}), f32[8,20,128]{2,1,0:T(8,128)S(1)}, u32[]{:S(2)}, u32[]{:S(2)}) async-start(f32[8,20,128]{2,1,0:T(8,128)} %broadcast_in_dim.137), calls=%async_computation | async-start | bytes 196608 | tf_op jit(solution)/shard_map/all_to_all | solution.py:50
  8.0 0.1 pad_add_fusion
  8.1 0.9 %select_reduce_fusion = s32[9]{0:T(128)S(1)} fusion(s32[256]{0:T(256)} %param.19, s32[9]{0:T(128)S(1)} %pad_add_fusion), kind=kLoop, calls=%fused_computation.35 | loop fusion | flops 6903 | bytes 1096 | tf_op jit(solution)/shard_map/reduce_sum | solution.py:72
  8.9 0.8 compare_and_fusion
  9.7 0.7 convert_element_type.52
  10.4 0.1 multiply_cosine_fusion.1
  10.5 0.7 convert_element_type.48
  11.2 1.8 %all-to-all-done = f32[8,20,128]{2,1,0:T(8,128)S(1)} async-done(((f32[8,20,128]{2,1,0:T(8,128)}), f32[8,20,128]{2,1,0:T(8,128)S(1)}, u32[]{:S(2)}, u32[]{:S(2)}) %all-to-all-start) | async-done | bytes 81952 | tf_op jit(solution)/shard_map/all_to_all | solution.py:50
  13.0 0.1 multiply_reduce_fusion
  13.1 0.1 fusion.28
  13.2 0.0 copy-done
  13.2 0.5 fusion.47
  13.7 1.2 %fusion.23 = f32[8,80]{1,0:T(8,128)S(1)} fusion(bf16[8,2560]{1,0:T(8,128)(2,1)S(1)} %fusion.28, bf16[2560,80]{0,1:T(8,128)(2,1)} %param.14), kind=kOutput, calls=%fused_computation.16 | convolution fusion | flops 3278080 | bytes 453120 | tf_op jit(solution)/shard_map/dot_general | solution.py:61
  14.9 1.2 %fusion.48 = f32[8,80]{1,0:T(8,128)S(1)} fusion(bf16[8,2560]{1,0:T(8,128)(2,1)S(1)} %fusion.28, bf16[2560,80]{0,1:T(8,128)(2,1)} %param.13), kind=kOutput, calls=%fused_computation.75 | convolution fusion | flops 3276800 | bytes 453120 | tf_op jit(solution)/shard_map/dot_general | solution.py:59
  16.2 0.1 pad_maximum_fusion
  16.2 0.9 %broadcast_select_fusion = f32[32,8,480]{2,1,0:T(8,128)} fusion(f32[8,480]{1,0:T(8,128)S(1)} %pad_maximum_fusion, pred[32,8]{1,0:T(8,128)(4,1)S(1)} %iota_compare_fusion.4), kind=kLoop, calls=%fused_computation.20 | loop fusion | flops 122880 | bytes 507136 | tf_op jit(solution)/shard_map/jit(_where)/select_n | solution.py:77
  17.2 10.5 %all-to-all-start.1 = ((f32[32,8,480]{2,1,0:T(8,128)}), f32[32,8,480]{2,1,0:T(8,128)S(1)}, u32[]{:S(2)}, u32[]{:S(2)}) async-start(f32[32,8,480]{2,1,0:T(8,128)} %broadcast_select_fusion), calls=%async_computation.1 | async-start | bytes 1048576 | tf_op jit(solution)/shard_map/all_to_all | solution.py:78
  27.7 0.8 iota_compare_fusion
  28.5 13.8 %all-to-all-done.1 = f32[32,8,480]{2,1,0:T(8,128)S(1)} async-done(((f32[32,8,480]{2,1,0:T(8,128)}), f32[32,8,480]{2,1,0:T(8,128)S(1)}, u32[]{:S(2)}, u32[]{:S(2)}) %all-to-all-start.1) | async-done | bytes 491552 | tf_op jit(solution)/shard_map/all_to_all | solution.py:78
  42.3 0.6 gather_fusion
  42.8 0.1 broadcast_select_fusion.1
  42.9 0.1 slice_bitcast_fusion
  43.0 0.1 fusion.40
  43.1 0.1 fusion.42
  43.2 0.1 reshape.278
  43.3 0.1 maximum_bitcast_fusion
  43.3 0.1 subtract_convert_fusion
  43.4 0.2 fusion.38
  43.6 3.7 %fusion.44 = (f32[8,4]{1,0:T(8,128)S(1)}, f32[8,4,4096]{2,1,0:T(4,128)S(1)}) fusion(bf16[8,1,80,4096]{3,2,1,0:T(8,128)(2,1)} %param.15, f32[8,4]{1,0:T(8,128)S(1)} %broadcast_multiply_fusion, pred[8,4096]{1,0:T(8,128)(4,1)S(1)} %get-tuple-element.17, pred[8,4096]{1,0:T(8,128)(4,1)S(1)} %get-tuple-element.18, bf16[8,4,40]{2,1,0:T(4,128)(2,1)S(1)} %get-tuple-element.10, ...), kind=kOutput, calls=%fused_computation.73 | convolution fusion | flops 21641216 | bytes 5838080 | tf_op jit(solution)/shard_map/sub | solution.py:112
  47.3 0.4 convert_reduce_fusion
  47.7 4.0 %fusion.20 = bf16[8,4,80]{2,1,0:T(4,128)(2,1)S(1)} fusion(bf16[8,1,80,4096]{3,2,1,0:T(8,128)(2,1)} %param.16, bf16[8,4,4096]{2,1,0:T(4,128)(2,1)S(1)} %get-tuple-element.6, pred[8,4096]{1,0:T(8,128)(4,1)S(1)} %get-tuple-element.18, f32[8,80]{1,0:T(8,128)S(1)} %fusion.40, f32[8,4]{1,0:T(8,128)S(1)} %get-tuple-element.5), kind=kOutput, calls=%fused_computation.14 | convolution fusion | flops 21110272 | bytes 5545600 | tf_op jit(solution)/shard_map/rkgw,rkhw->rkgh/dot_general | solution.py:119
  51.6 0.1 convert_element_type.57
  51.7 0.3 fusion.16
  52.0 0.5 broadcast.196
  52.5 0.7 reduce.11
  53.2 0.2 copy.20
  53.4 0.8 %reshape.297 = bf16[256,2,160]{2,1,0:T(2,128)(2,1)} reshape(bf16[256,320]{1,0:T(8,128)(2,1)S(1)} %copy.20) | data formatting | bytes 327680
  54.2 9.9 %all-to-all-start.2 = ((bf16[256,2,160]{2,1,0:T(2,128)(2,1)}), bf16[256,2,160]{2,1,0:T(2,128)(2,1)S(1)}, u32[]{:S(2)}, u32[]{:S(2)}) async-start(bf16[256,2,160]{2,1,0:T(2,128)(2,1)} %reshape.297), calls=%async_computation.2 | async-start | bytes 524288 | tf_op jit(solution)/shard_map/all_to_all | solution.py:131
  64.1 0.6 slice.36
  65.3 14.2 %all-to-all-done.2 = bf16[256,2,160]{2,1,0:T(2,128)(2,1)S(1)} async-done(((bf16[256,2,160]{2,1,0:T(2,128)(2,1)}), bf16[256,2,160]{2,1,0:T(2,128)(2,1)S(1)}, u32[]{:S(2)}, u32[]{:S(2)}) %all-to-all-start.2) | async-done | bytes 163872 | tf_op jit(solution)/shard_map/all_to_all | solution.py:131
  79.6 0.3 reshape.298
  79.8 0.1 dynamic-slice_reduce_fusion
  79.9 0.7 reshape.282
  (9 shorter events, 0.1 us)
Async XLA Ops:
  0.0 13.2 %copy-start = (bf16[2560,320]{0,1:T(8,128)(2,1)S(1)}, bf16[2560,320]{0,1:T(8,128)(2,1)}, u32[]{:S(2)}) copy-start(bf16[2560,320]{0,1:T(8,128)(2,1)} %param.12) | copy-start | bytes 4915204
  1.5 11.5 %all-to-all-start = ((f32[8,20,128]{2,1,0:T(8,128)}), f32[8,20,128]{2,1,0:T(8,128)S(1)}, u32[]{:S(2)}, u32[]{:S(2)}) async-start(f32[8,20,128]{2,1,0:T(8,128)} %broadcast_in_dim.137), calls=%async_computation | async-start | bytes 196608 | tf_op jit(solution)/shard_map/all_to_all | solution.py:50
  17.2 25.1 %all-to-all-start.1 = ((f32[32,8,480]{2,1,0:T(8,128)}), f32[32,8,480]{2,1,0:T(8,128)S(1)}, u32[]{:S(2)}, u32[]{:S(2)}) async-start(f32[32,8,480]{2,1,0:T(8,128)} %broadcast_select_fusion), calls=%async_computation.1 | async-start | bytes 1048576 | tf_op jit(solution)/shard_map/all_to_all | solution.py:78
  54.2 25.4 %all-to-all-start.2 = ((bf16[256,2,160]{2,1,0:T(2,128)(2,1)}), bf16[256,2,160]{2,1,0:T(2,128)(2,1)S(1)}, u32[]{:S(2)}, u32[]{:S(2)}) async-start(bf16[256,2,160]{2,1,0:T(2,128)(2,1)} %reshape.297), calls=%async_computation.2 | async-start | bytes 524288 | tf_op jit(solution)/shard_map/all_to_all | solution.py:131

commit v10 on v6

--- a/solution.py
+++ b/solution.py
@@ -1,6 +1,8 @@
 import jax
 import jax.numpy as jnp
 from jax import lax
+from jax.experimental import pallas as pl
+from jax.experimental.pallas import tpu as pltpu
 from jax.sharding import PartitionSpec as P
 
 HEAD_DIMENSION = 80
@@ -18,6 +20,30 @@
         [front_half * cosine - back_half * sine_part, back_half * cosine + front_half * sine_part],
         axis=-1,
     )
+
+
+def stage_kernel(keys_hbm, values_hbm, keys_out, values_out, copy_sems):
+    key_copy = pltpu.make_async_copy(keys_hbm, keys_out, copy_sems.at[0])
+    value_copy = pltpu.make_async_copy(values_hbm, values_out, copy_sems.at[1])
+    key_copy.start()
+    value_copy.start()
+    key_copy.wait()
+    value_copy.wait()
+
+
+def stage_cache(cache_keys, value_cache):
+    shapes = (
+        jax.ShapeDtypeStruct(cache_keys.shape, cache_keys.dtype),
+        jax.ShapeDtypeStruct(value_cache.shape, value_cache.dtype),
+    )
+    return pl.pallas_call(
+        stage_kernel,
+        out_shape=shapes,
+        in_specs=[pl.BlockSpec(memory_space=pl.ANY)] * 2,
+        out_specs=[pl.BlockSpec(memory_space=pltpu.VMEM)] * 2,
+        scratch_shapes=[pltpu.SemaphoreType.DMA((2,))],
+        compiler_params=pltpu.CompilerParams(vmem_limit_bytes=32 * 1024 * 1024),
+    )(cache_keys, value_cache)
 
 
 def local(
@@ -93,6 +119,7 @@
     fresh_value_rows = (
         mine[:, query_width + key_width :].astype(jnp.bfloat16).reshape(group_rows, heads_dev, head_size)
     )
+    cache_keys, value_cache_slots = stage_cache(cache_keys, value_cache_slots)
     score_scale = 1.0 / head_size**0.5
     scores = (
         jnp.einsum("rkgh,rkhw->rkgw", query_vectors, cache_keys, preferred_element_type=jnp.float32)

time: 81.2 us -> 81.2 us (level)
  waiting for transfers between devices: 29.7 us -> 20 us
  local copies, waits for them, and re-layouts: 4.54 us -> 14.2 us
    all_to_all x1, waiting for transfers between devices: 13.9 us -> 4.17 us  [local(): recv_rows = lax.all_to_all(send_rows, 'req', 0, 0, tiled=True)]
    unnamed x5 -> x17, local copies, waits for them, and re-layouts: 1.27 us -> 10.9 us
  transfers between devices with their start and end apart: 3 -> 3, of which waited for: 3 -> 3; matrix products, arithmetic and copies ran while one was open for 6% -> 5% of each run, Pallas kernels for 0% -> 1%
where the time goes in v10:
time: 81.2 us; the launch traced here: 80.6 us
  starting transfers between devices  27 us (33%)
  waiting for transfers between devices  20 us (25%)
  local copies, waits for them, and re-layouts  14.2 us (17%)
  matrix products  11.1 us (14%)
  other arithmetic  6.85 us (8%)
    all_to_all x1, waiting for transfers between devices, local(): recv_out = lax.all_to_all(send_out, ('req', 'kv'), 0, 0, tiled=True)  14.2 us
    unnamed x17, local copies, waits for them, and re-layouts  10.9 us
    all_to_all x1, starting transfers between devices, local(): recv_rows = lax.all_to_all(send_rows, 'req', 0, 0, tiled=True)  10.5 us
    all_to_all x1, starting transfers between devices, local(): recv_out = lax.all_to_all(send_out, ('req', 'kv'), 0, 0, tiled=True)  9.99 us
    all_to_all x1, starting transfers between devices, local(): lax.all_to_all(jnp.broadcast_to(lane_rows[None], (kv_count,) + lane_rows....  6.45 us
    all_to_all x1, waiting for transfers between devices, local(): recv_rows = lax.all_to_all(send_rows, 'req', 0, 0, tiled=True)  4.17 us
    dot_general x1, matrix products, local(): jnp.einsum('rkgw,rkhw->rkgh', stale_weights, value_cache_slots, preferred...  3.95 us
    sub x1, matrix products, local(): expd = jnp.exp(scores - row_max)  3.63 us
  transfers between devices with their start and end apart: 3, of which 3 were waited for; matrix products, arithmetic and copies ran while one was open for 5% of the time, Pallas kernels for 1%

profile of v10, /device:TPU:1, one launch (start us, length us, event | category | flops | bytes accessed | tf_op | source)
XLA Modules:
  0.0 80.6 jit_solution(9734577753836891912)
XLA Ops:
  0.0 0.9 %reduce.7 = bf16[2560]{0:T(1024)(128)(2,1)S(1)} reduce(bf16[1,2560]{1,0:T(2,128)(2,1)} %param.10, bf16[]{:T(256)} %constant.72), dimensions={0}, to_apply=%param.10.reduce_sub_computation | reduce | bytes 10242 | tf_op args[0]
  0.9 0.6 broadcast_in_dim.133
  1.5 6.4 %all-to-all-start = ((bf16[8,20,128]{2,1,0:T(8,128)(2,1)}), bf16[8,20,128]{2,1,0:T(8,128)(2,1)S(1)}, u32[]{:S(2)}, u32[]{:S(2)}) async-start(bf16[8,20,128]{2,1,0:T(8,128)(2,1)} %broadcast_in_dim.133), calls=%async_computation | async-start | bytes 98304 | tf_op jit(solution)/shard_map/all_to_all | solution.py:76
  8.0 0.1 pad_add_fusion
  8.0 0.9 %select_reduce_fusion = s32[9]{0:T(128)S(1)} fusion(s32[256]{0:T(256)} %param.19, s32[9]{0:T(128)S(1)} %pad_add_fusion), kind=kLoop, calls=%fused_computation.37 | loop fusion | flops 6903 | bytes 1096 | tf_op jit(solution)/shard_map/reduce_sum | solution.py:98
  8.9 0.7 convert_element_type.63
  9.6 0.8 compare_and_fusion
  10.3 0.1 multiply_cosine_fusion.1
  10.5 0.7 convert_element_type.59
  11.2 1.6 %all-to-all-done = bf16[8,20,128]{2,1,0:T(8,128)(2,1)S(1)} async-done(((bf16[8,20,128]{2,1,0:T(8,128)(2,1)}), bf16[8,20,128]{2,1,0:T(8,128)(2,1)S(1)}, u32[]{:S(2)}, u32[]{:S(2)}) %all-to-all-start) | async-done | bytes 40992 | tf_op jit(solution)/shard_map/all_to_all | solution.py:76
  12.7 0.1 fusion.30
  12.9 1.3 %fusion.47 = f32[8,80]{1,0:T(8,128)S(1)} fusion(bf16[2560,80]{0,1:T(8,128)(2,1)} %param.13, f32[2560]{0:T(1024)S(1)} %convert_element_type.59, f32[8]{0:T(128)S(1)} %add_rsqrt_fusion, bf16[8,20,128]{2,1,0:T(8,128)(2,1)S(1)} %all-to-all-done), kind=kOutput, calls=%fused_computation.74 | convolution fusion | flops 3358720 | bytes 463392 | tf_op jit(solution)/shard_map/dot_general | solution.py:85
  14.1 1.3 %fusion.23 = f32[8,80]{1,0:T(8,128)S(1)} fusion(bf16[2560,80]{0,1:T(8,128)(2,1)} %param.14, f32[2560]{0:T(1024)S(1)} %convert_element_type.59, f32[8]{0:T(128)S(1)} %add_rsqrt_fusion, bf16[8,20,128]{2,1,0:T(8,128)(2,1)S(1)} %all-to-all-done), kind=kOutput, calls=%fused_computation.16 | convolution fusion | flops 3360000 | bytes 463392 | tf_op jit(solution)/shard_map/dot_general | solution.py:87
  15.4 0.5 fusion.49
  16.0 0.1 pad_maximum_fusion
  16.0 1.0 %broadcast_select_fusion = f32[32,8,480]{2,1,0:T(8,128)} fusion(f32[8,480]{1,0:T(8,128)S(1)} %pad_maximum_fusion, pred[32,8]{1,0:T(8,128)(4,1)S(1)} %iota_compare_fusion.4), kind=kLoop, calls=%fused_computation.20 | loop fusion | flops 122880 | bytes 507136 | tf_op jit(solution)/shard_map/jit(_where)/select_n | solution.py:103
  17.0 10.5 %all-to-all-start.1 = ((f32[32,8,480]{2,1,0:T(8,128)}), f32[32,8,480]{2,1,0:T(8,128)S(1)}, u32[]{:S(2)}, u32[]{:S(2)}) async-start(f32[32,8,480]{2,1,0:T(8,128)} %broadcast_select_fusion), calls=%async_computation.1 | async-start | bytes 1048576 | tf_op jit(solution)/shard_map/all_to_all | solution.py:104
  27.6 2.5 %copy-done.1 = bf16[8,1,80,4096]{3,2,1,0:T(8,128)(2,1)S(1)} copy-done((bf16[8,1,80,4096]{3,2,1,0:T(8,128)(2,1)S(1)}, bf16[8,1,80,4096]{3,2,1,0:T(8,128)(2,1)}, u32[]{:S(2)}) %copy-start.1) | copy-done | bytes 5242904
  30.0 2.5 %copy-done.2 = bf16[8,1,80,4096]{3,2,1,0:T(8,128)(2,1)S(1)} copy-done((bf16[8,1,80,4096]{3,2,1,0:T(8,128)(2,1)S(1)}, bf16[8,1,80,4096]{3,2,1,0:T(8,128)(2,1)}, u32[]{:S(2)}) %copy-start.2) | copy-done | bytes 5242904
  32.5 0.7 shard_map.100
  33.3 2.3 %copy-done.3 = bf16[8,1,80,4096]{3,2,1,0:T(8,128)(2,1)} copy-done((bf16[8,1,80,4096]{3,2,1,0:T(8,128)(2,1)}, bf16[8,1,80,4096]{3,2,1,0:T(8,128)(2,1)S(1)}, u32[]{:S(2)}) %copy-start.3) | copy-done | bytes 5242904
  35.6 2.3 %copy-done.4 = bf16[8,1,80,4096]{3,2,1,0:T(8,128)(2,1)} copy-done((bf16[8,1,80,4096]{3,2,1,0:T(8,128)(2,1)}, bf16[8,1,80,4096]{3,2,1,0:T(8,128)(2,1)S(1)}, u32[]{:S(2)}) %copy-start.4) | copy-done | bytes 5242904
  37.9 0.1 iota_compare_fusion
  38.0 4.2 %all-to-all-done.1 = f32[32,8,480]{2,1,0:T(8,128)S(1)} async-done(((f32[32,8,480]{2,1,0:T(8,128)}), f32[32,8,480]{2,1,0:T(8,128)S(1)}, u32[]{:S(2)}, u32[]{:S(2)}) %all-to-all-start.1) | async-done | bytes 491552 | tf_op jit(solution)/shard_map/all_to_all | solution.py:104
  42.2 0.6 gather_fusion
  42.8 0.1 broadcast_select_fusion.1
  42.8 0.1 fusion.42
  42.9 0.1 slice_bitcast_fusion
  43.0 0.1 fusion.44
  43.1 0.1 reshape.277
  43.2 0.1 maximum_bitcast_fusion
  43.3 0.1 subtract_convert_fusion
  43.3 0.2 fusion.40
  43.5 3.6 %fusion.51 = (f32[8,4]{1,0:T(8,128)S(1)}, f32[8,4,4096]{2,1,0:T(4,128)S(1)}) fusion(bf16[8,1,80,4096]{3,2,1,0:T(8,128)(2,1)} %copy-done.3, f32[8,4]{1,0:T(8,128)S(1)} %broadcast_multiply_fusion, pred[8,4096]{1,0:T(8,128)(4,1)S(1)} %get-tuple-element.21, pred[8,4096]{1,0:T(8,128)(4,1)S(1)} %get-tuple-element.22, ...), kind=kOutput, calls=%fused_computation.76 | convolution fusion | flops 21641216 | bytes 5838080 | tf_op jit(solution)/shard_map/sub | solution.py:139
  47.2 0.4 convert_reduce_fusion
  47.5 3.9 %fusion.20 = bf16[8,4,80]{2,1,0:T(4,128)(2,1)S(1)} fusion(bf16[8,1,80,4096]{3,2,1,0:T(8,128)(2,1)} %copy-done.4, bf16[8,4,4096]{2,1,0:T(4,128)(2,1)S(1)} %get-tuple-element.10, pred[8,4096]{1,0:T(8,128)(4,1)S(1)} %get-tuple-element.22, f32[8,80]{1,0:T(8,128)S(1)} %fusion.42, f32[8,4]{1,0:T(8,128)S(1)} %get-tuple-element.9), kind=kOutput, calls=%fused_computation.14 | convolution fusion | flops 21110272 | bytes 5545600 | tf_op jit(solution)/shard_map/rkgw,rkhw->rkgh/dot_general | solution.py:146
  51.5 0.1 convert_element_type.68
  51.6 0.3 fusion.16
  51.9 0.5 broadcast.196
  52.4 0.7 reduce.10
  53.1 0.2 copy.25
  53.3 0.8 %reshape.296 = bf16[256,2,160]{2,1,0:T(2,128)(2,1)} reshape(bf16[256,320]{1,0:T(8,128)(2,1)S(1)} %copy.25) | data formatting | bytes 327680
  54.1 10.0 %all-to-all-start.2 = ((bf16[256,2,160]{2,1,0:T(2,128)(2,1)}), bf16[256,2,160]{2,1,0:T(2,128)(2,1)S(1)}, u32[]{:S(2)}, u32[]{:S(2)}) async-start(bf16[256,2,160]{2,1,0:T(2,128)(2,1)} %reshape.296), calls=%async_computation.2 | async-start | bytes 524288 | tf_op jit(solution)/shard_map/all_to_all | solution.py:158
  64.1 0.6 slice.36
  65.3 14.2 %all-to-all-done.2 = bf16[256,2,160]{2,1,0:T(2,128)(2,1)S(1)} async-done(((bf16[256,2,160]{2,1,0:T(2,128)(2,1)}), bf16[256,2,160]{2,1,0:T(2,128)(2,1)S(1)}, u32[]{:S(2)}, u32[]{:S(2)}) %all-to-all-start.2) | async-done | bytes 163872 | tf_op jit(solution)/shard_map/all_to_all | solution.py:158
  79.6 0.3 reshape.297
  79.8 0.1 dynamic-slice_reduce_fusion
  79.9 0.7 reshape.281
  (19 shorter events, 0.1 us)
Async XLA Ops:
  0.0 15.4 %copy-start = (bf16[2560,320]{0,1:T(8,128)(2,1)S(1)}, bf16[2560,320]{0,1:T(8,128)(2,1)}, u32[]{:S(2)}) copy-start(bf16[2560,320]{0,1:T(8,128)(2,1)} %param.12) | copy-start | bytes 4915204
  1.5 11.3 %all-to-all-start = ((bf16[8,20,128]{2,1,0:T(8,128)(2,1)}), bf16[8,20,128]{2,1,0:T(8,128)(2,1)S(1)}, u32[]{:S(2)}, u32[]{:S(2)}) async-start(bf16[8,20,128]{2,1,0:T(8,128)(2,1)} %broadcast_in_dim.133), calls=%async_computation | async-start | bytes 98304 | tf_op jit(solution)/shard_map/all_to_all | solution.py:76
  17.0 25.2 %all-to-all-start.1 = ((f32[32,8,480]{2,1,0:T(8,128)}), f32[32,8,480]{2,1,0:T(8,128)S(1)}, u32[]{:S(2)}, u32[]{:S(2)}) async-start(f32[32,8,480]{2,1,0:T(8,128)} %broadcast_select_fusion), calls=%async_computation.1 | async-start | bytes 1048576 | tf_op jit(solution)/shard_map/all_to_all | solution.py:104
  27.5 2.5 %copy-start.1 = (bf16[8,1,80,4096]{3,2,1,0:T(8,128)(2,1)S(1)}, bf16[8,1,80,4096]{3,2,1,0:T(8,128)(2,1)}, u32[]{:S(2)}) copy-start(bf16[8,1,80,4096]{3,2,1,0:T(8,128)(2,1)} %keys_hbm.1) | copy-start | bytes 15728644
  30.0 2.5 %copy-start.2 = (bf16[8,1,80,4096]{3,2,1,0:T(8,128)(2,1)S(1)}, bf16[8,1,80,4096]{3,2,1,0:T(8,128)(2,1)}, u32[]{:S(2)}) copy-start(bf16[8,1,80,4096]{3,2,1,0:T(8,128)(2,1)} %values_hbm.1) | copy-start | bytes 15728644
  32.5 5.4 %copy-start.5 = (s32[8]{0:T(128)S(1)}, s32[8]{0:T(128)}, u32[]{:S(2)}) copy-start(s32[8]{0:T(128)} %param.17) | copy-start | bytes 100
  32.5 5.4 %copy-start.6 = (s32[8]{0:T(128)S(1)}, s32[8]{0:T(128)}, u32[]{:S(2)}) copy-start(s32[8]{0:T(128)} %param.18) | copy-start | bytes 100
  33.2 2.3 %copy-start.3 = (bf16[8,1,80,4096]{3,2,1,0:T(8,128)(2,1)}, bf16[8,1,80,4096]{3,2,1,0:T(8,128)(2,1)S(1)}, u32[]{:S(2)}) copy-start(bf16[8,1,80,4096]{3,2,1,0:T(8,128)(2,1)S(1)} %get-tuple-element.7) | copy-start | bytes 15728644
  35.6 2.3 %copy-start.4 = (bf16[8,1,80,4096]{3,2,1,0:T(8,128)(2,1)}, bf16[8,1,80,4096]{3,2,1,0:T(8,128)(2,1)S(1)}, u32[]{:S(2)}) copy-start(bf16[8,1,80,4096]{3,2,1,0:T(8,128)(2,1)S(1)} %get-tuple-element.8) | copy-start | bytes 15728644
  54.1 25.5 %all-to-all-start.2 = ((bf16[256,2,160]{2,1,0:T(2,128)(2,1)}), bf16[256,2,160]{2,1,0:T(2,128)(2,1)S(1)}, u32[]{:S(2)}, u32[]{:S(2)}) async-start(bf16[256,2,160]{2,1,0:T(2,128)(2,1)} %reshape.296), calls=%async_computation.2 | async-start | bytes 524288 | tf_op jit(solution)/shard_map/all_to_all | solution.py:158

commit v11 on v6

--- a/solution.py
+++ b/solution.py
@@ -95,7 +95,7 @@
     )
     score_scale = 1.0 / head_size**0.5
     scores = (
-        jnp.einsum("rkgh,rkhw->rkgw", query_vectors, cache_keys, preferred_element_type=jnp.float32)
+        jnp.einsum("rkhw,rkgh->rkwg", cache_keys, query_vectors, preferred_element_type=jnp.float32)
         * score_scale
     )
     own_score = (
@@ -104,20 +104,20 @@
         )
         * score_scale
     )
-    slot_ids = lax.broadcasted_iota(jnp.int32, (group_rows, 1, 1, window_size), 3)
+    slot_ids = lax.broadcasted_iota(jnp.int32, (group_rows, 1, window_size, 1), 2)
     at_write = slot_ids == write_pos[:, None, None, None]
-    scores = jnp.where(at_write, own_score[..., None], scores)
+    scores = jnp.where(at_write, own_score[:, :, None, :], scores)
     scores = jnp.where(slot_ids <= lengths[:, None, None, None], scores, -jnp.inf)
-    row_max = jnp.max(scores, axis=-1, keepdims=True)
+    row_max = jnp.max(scores, axis=2, keepdims=True)
     expd = jnp.exp(scores - row_max)
-    softmax_weights = (expd / jnp.sum(expd, axis=-1, keepdims=True)).astype(jnp.bfloat16)
+    softmax_weights = (expd / jnp.sum(expd, axis=2, keepdims=True)).astype(jnp.bfloat16)
     stale_weights = jnp.where(at_write, jnp.zeros((), jnp.bfloat16), softmax_weights)
     fresh_weight = jnp.sum(
         jnp.where(at_write, softmax_weights, jnp.zeros((), jnp.bfloat16)).astype(jnp.float32),
-        axis=-1,
+        axis=2,
     )
     mixed = jnp.einsum(
-        "rkgw,rkhw->rkgh", stale_weights, value_cache_slots, preferred_element_type=jnp.float32
+        "rkwg,rkhw->rkgh", stale_weights, value_cache_slots, preferred_element_type=jnp.float32
     )
     mixed = mixed + fresh_weight[..., None] * fresh_value_rows[:, :, None, :].astype(jnp.float32)
     attended = mixed.reshape(group_rows, heads_dev * queries_per_group * head_size).astype(

time: 81.2 us -> 81.2 us (level)
  no operation moved by 1% of the time
where the time goes in v11:
time: 81.2 us; the launch traced here: 80.6 us
  waiting for transfers between devices  29.7 us (37%)
  starting transfers between devices  27 us (33%)
  matrix products  11.1 us (14%)
  other arithmetic  7.5 us (9%)
  local copies, waits for them, and re-layouts  4.54 us (6%)
    all_to_all x1, waiting for transfers between devices, local(): recv_out = lax.all_to_all(send_out, ('req', 'kv'), 0, 0, tiled=True)  14.2 us
    all_to_all x1, waiting for transfers between devices, local(): recv_rows = lax.all_to_all(send_rows, 'req', 0, 0, tiled=True)  13.9 us
    all_to_all x1, starting transfers between devices, local(): recv_rows = lax.all_to_all(send_rows, 'req', 0, 0, tiled=True)  10.5 us
    all_to_all x1, starting transfers between devices, local(): recv_out = lax.all_to_all(send_out, ('req', 'kv'), 0, 0, tiled=True)  10 us
    all_to_all x1, starting transfers between devices, local(): lax.all_to_all(jnp.broadcast_to(lane_rows[None], (kv_count,) + lane_rows....  6.45 us
    dot_general x1, matrix products, local(): jnp.einsum('rkwg,rkhw->rkgh', stale_weights, value_cache_slots, preferred...  3.96 us
    sub x1, matrix products, local(): expd = jnp.exp(scores - row_max)  3.66 us
  transfers between devices with their start and end apart: 3, of which 3 were waited for; matrix products, arithmetic and copies ran while one was open for 6% of the time, Pallas kernels for 0%

profile of v11, /device:TPU:1, one launch (start us, length us, event | category | flops | bytes accessed | tf_op | source)
XLA Modules:
  0.0 80.6 jit_solution(5987990769051895699)
XLA Ops:
  0.0 0.0 copy-start
  0.0 0.9 %reduce.7 = bf16[2560]{0:T(1024)(128)(2,1)S(1)} reduce(bf16[1,2560]{1,0:T(2,128)(2,1)} %param.10, bf16[]{:T(256)} %constant.72), dimensions={0}, to_apply=%param.10.reduce_sub_computation | reduce | bytes 10242 | tf_op args[0]
  0.9 0.6 broadcast_in_dim.136
  1.5 6.4 %all-to-all-start = ((bf16[8,20,128]{2,1,0:T(8,128)(2,1)}), bf16[8,20,128]{2,1,0:T(8,128)(2,1)S(1)}, u32[]{:S(2)}, u32[]{:S(2)}) async-start(bf16[8,20,128]{2,1,0:T(8,128)(2,1)} %broadcast_in_dim.136), calls=%async_computation | async-start | bytes 98304 | tf_op jit(solution)/shard_map/all_to_all | solution.py:50
  8.0 0.1 pad_add_fusion
  8.0 0.9 %select_reduce_fusion = s32[9]{0:T(128)S(1)} fusion(s32[256]{0:T(256)} %param.19, s32[9]{0:T(128)S(1)} %pad_add_fusion), kind=kLoop, calls=%fused_computation.38 | loop fusion | flops 6903 | bytes 1096 | tf_op jit(solution)/shard_map/reduce_sum | solution.py:72
  8.9 0.8 compare_and_fusion
  9.7 0.7 convert_element_type.63
  10.4 0.1 multiply_cosine_fusion.1
  10.5 0.7 convert_element_type.59
  11.2 1.6 %all-to-all-done = bf16[8,20,128]{2,1,0:T(8,128)(2,1)S(1)} async-done(((bf16[8,20,128]{2,1,0:T(8,128)(2,1)}), bf16[8,20,128]{2,1,0:T(8,128)(2,1)S(1)}, u32[]{:S(2)}, u32[]{:S(2)}) %all-to-all-start) | async-done | bytes 40992 | tf_op jit(solution)/shard_map/all_to_all | solution.py:50
  12.7 0.1 fusion.33
  12.9 0.0 copy-done
  12.9 0.5 fusion.52
  13.4 1.3 %fusion.26 = f32[8,80]{1,0:T(8,128)S(1)} fusion(bf16[2560,80]{0,1:T(8,128)(2,1)} %param.14, f32[2560]{0:T(1024)S(1)} %convert_element_type.59, f32[8]{0:T(128)S(1)} %add_rsqrt_fusion, bf16[8,20,128]{2,1,0:T(8,128)(2,1)S(1)} %all-to-all-done), kind=kOutput, calls=%fused_computation.17 | convolution fusion | flops 3360000 | bytes 463392 | tf_op jit(solution)/shard_map/dot_general | solution.py:61
  14.7 1.3 %fusion.50 = f32[8,80]{1,0:T(8,128)S(1)} fusion(bf16[2560,80]{0,1:T(8,128)(2,1)} %param.13, f32[2560]{0:T(1024)S(1)} %convert_element_type.59, f32[8]{0:T(128)S(1)} %add_rsqrt_fusion, bf16[8,20,128]{2,1,0:T(8,128)(2,1)S(1)} %all-to-all-done), kind=kOutput, calls=%fused_computation.75 | convolution fusion | flops 3358720 | bytes 463392 | tf_op jit(solution)/shard_map/dot_general | solution.py:59
  16.0 0.1 pad_maximum_fusion
  16.0 0.9 %broadcast_select_fusion = f32[32,8,480]{2,1,0:T(8,128)} fusion(f32[8,480]{1,0:T(8,128)S(1)} %pad_maximum_fusion, pred[32,8]{1,0:T(8,128)(4,1)S(1)} %iota_compare_fusion.4), kind=kLoop, calls=%fused_computation.21 | loop fusion | flops 122880 | bytes 507136 | tf_op jit(solution)/shard_map/jit(_where)/select_n | solution.py:77
  17.0 10.5 %all-to-all-start.1 = ((f32[32,8,480]{2,1,0:T(8,128)}), f32[32,8,480]{2,1,0:T(8,128)S(1)}, u32[]{:S(2)}, u32[]{:S(2)}) async-start(f32[32,8,480]{2,1,0:T(8,128)} %broadcast_select_fusion), calls=%async_computation.1 | async-start | bytes 1048576 | tf_op jit(solution)/shard_map/all_to_all | solution.py:78
  27.5 0.8 iota_compare_fusion
  28.3 13.9 %all-to-all-done.1 = f32[32,8,480]{2,1,0:T(8,128)S(1)} async-done(((f32[32,8,480]{2,1,0:T(8,128)}), f32[32,8,480]{2,1,0:T(8,128)S(1)}, u32[]{:S(2)}, u32[]{:S(2)}) %all-to-all-start.1) | async-done | bytes 491552 | tf_op jit(solution)/shard_map/all_to_all | solution.py:78
  42.2 0.6 gather_fusion
  42.7 0.1 broadcast_select_fusion.1
  42.8 0.1 slice_bitcast_fusion
  42.9 0.1 fusion.45
  42.9 0.1 fusion.47
  43.1 0.1 reshape.283
  43.1 0.1 maximum_bitcast_fusion
  43.2 0.1 subtract_convert_fusion
  43.3 0.2 fusion.43
  43.5 3.7 %fusion.54 = (f32[8,4]{1,0:T(8,128)S(1)}, f32[8,4096,4]{1,2,0:T(4,128)S(1)}) fusion(bf16[8,1,80,4096]{3,2,1,0:T(8,128)(2,1)} %param.15, f32[8,4]{1,0:T(8,128)S(1)} %broadcast_multiply_fusion, pred[8,4096]{1,0:T(8,128)(4,1)S(1)} %get-tuple-element.18, pred[8,4096]{1,0:T(8,128)(4,1)S(1)} %get-tuple-element.17, bf16[8,4,40]{2,1,0:T(4,128)(2,1)S(1)} %get-tuple-element.10, ...), kind=kOutput, calls=%fused_computation.77 | convolution fusion | flops 21641216 | bytes 5838080 | tf_op jit(solution)/shard_map/sub | solution.py:112
  47.2 0.4 convert_reduce_fusion
  47.5 4.0 %fusion.23 = bf16[8,4,80]{2,1,0:T(4,128)(2,1)S(1)} fusion(bf16[8,1,80,4096]{3,2,1,0:T(8,128)(2,1)} %param.16, bf16[8,4096,4]{1,2,0:T(4,128)(2,1)S(1)} %get-tuple-element.6, pred[8,4096]{1,0:T(8,128)(4,1)S(1)} %get-tuple-element.18, f32[8,80]{1,0:T(8,128)S(1)} %fusion.45, f32[8,4]{1,0:T(8,128)S(1)} %get-tuple-element.5), kind=kOutput, calls=%fused_computation.15 | convolution fusion | flops 21110272 | bytes 5545600 | tf_op jit(solution)/shard_map/rkwg,rkhw->rkgh/dot_general | solution.py:119
  51.5 0.1 convert_element_type.68
  51.6 0.3 fusion.19
  51.9 0.5 broadcast.211
  52.4 0.7 reduce.10
  53.1 0.2 copy.25
  53.3 0.8 %reshape.302 = bf16[256,2,160]{2,1,0:T(2,128)(2,1)} reshape(bf16[256,320]{1,0:T(8,128)(2,1)S(1)} %copy.25) | data formatting | bytes 327680
  54.1 10.0 %all-to-all-start.2 = ((bf16[256,2,160]{2,1,0:T(2,128)(2,1)}), bf16[256,2,160]{2,1,0:T(2,128)(2,1)S(1)}, u32[]{:S(2)}, u32[]{:S(2)}) async-start(bf16[256,2,160]{2,1,0:T(2,128)(2,1)} %reshape.302), calls=%async_computation.2 | async-start | bytes 524288 | tf_op jit(solution)/shard_map/all_to_all | solution.py:131
  64.1 0.6 slice.36
  65.3 14.2 %all-to-all-done.2 = bf16[256,2,160]{2,1,0:T(2,128)(2,1)S(1)} async-done(((bf16[256,2,160]{2,1,0:T(2,128)(2,1)}), bf16[256,2,160]{2,1,0:T(2,128)(2,1)S(1)}, u32[]{:S(2)}, u32[]{:S(2)}) %all-to-all-start.2) | async-done | bytes 163872 | tf_op jit(solution)/shard_map/all_to_all | solution.py:131
  79.6 0.3 reshape.303
  79.9 0.1 dynamic-slice_reduce_fusion
  79.9 0.7 reshape.287
  (9 shorter events, 0.1 us)
Async XLA Ops:
  0.0 12.9 %copy-start = (bf16[2560,320]{0,1:T(8,128)(2,1)S(1)}, bf16[2560,320]{0,1:T(8,128)(2,1)}, u32[]{:S(2)}) copy-start(bf16[2560,320]{0,1:T(8,128)(2,1)} %param.12) | copy-start | bytes 4915204
  1.5 11.3 %all-to-all-start = ((bf16[8,20,128]{2,1,0:T(8,128)(2,1)}), bf16[8,20,128]{2,1,0:T(8,128)(2,1)S(1)}, u32[]{:S(2)}, u32[]{:S(2)}) async-start(bf16[8,20,128]{2,1,0:T(8,128)(2,1)} %broadcast_in_dim.136), calls=%async_computation | async-start | bytes 98304 | tf_op jit(solution)/shard_map/all_to_all | solution.py:50
  17.0 25.2 %all-to-all-start.1 = ((f32[32,8,480]{2,1,0:T(8,128)}), f32[32,8,480]{2,1,0:T(8,128)S(1)}, u32[]{:S(2)}, u32[]{:S(2)}) async-start(f32[32,8,480]{2,1,0:T(8,128)} %broadcast_select_fusion), calls=%async_computation.1 | async-start | bytes 1048576 | tf_op jit(solution)/shard_map/all_to_all | solution.py:78
  54.1 25.5 %all-to-all-start.2 = ((bf16[256,2,160]{2,1,0:T(2,128)(2,1)}), bf16[256,2,160]{2,1,0:T(2,128)(2,1)S(1)}, u32[]{:S(2)}, u32[]{:S(2)}) async-start(bf16[256,2,160]{2,1,0:T(2,128)(2,1)} %reshape.302), calls=%async_computation.2 | async-start | bytes 524288 | tf_op jit(solution)/shard_map/all_to_all | solution.py:131

commit v12 on v2

--- a/solution.py
+++ b/solution.py
@@ -46,32 +46,33 @@
     query_width = w_query.shape[1]
     key_width = key_projection_weight.shape[1]
 
-    row_block = lax.all_gather(states, "kv", axis=0, tiled=True)
-    wide_rows = row_block.astype(jnp.float32)
+    places = jnp.arange(total_rows, dtype=jnp.int32)
+    own_index = (group_index * kv_count + kv_index) * per_device
+    own_place = jnp.sum(jnp.where(dealing == own_index, places, 0))
+    to_group = (own_place // group_rows) == jnp.arange(req_count, dtype=jnp.int32)
+    send_rows = jnp.where(to_group[:, None], states, jnp.zeros((), states.dtype))
+    recv_rows = lax.all_to_all(send_rows, "req", 0, 0, tiled=True)
+    dealt_ids = lax.dynamic_slice_in_dim(dealing, group_index * group_rows, group_rows)
+    held = (dealt_ids % kv_count) == kv_index
+    slot_rows = jnp.where(
+        held[:, None],
+        jnp.take(recv_rows, dealt_ids // kv_count, axis=0, mode="clip"),
+        jnp.zeros((), states.dtype),
+    )
+    shared = lax.all_to_all(
+        jnp.broadcast_to(slot_rows[None], (kv_count,) + slot_rows.shape), "kv", 0, 0, tiled=True
+    )
+    wide_rows = jnp.sum(shared.astype(jnp.float32), axis=0)
     inv_rms = lax.rsqrt(jnp.mean(wide_rows * wide_rows, axis=1, keepdims=True) + 1e-05)
     normalized_input = (wide_rows * inv_rms * norm_gain.astype(jnp.float32)[None, :]).astype(
         jnp.bfloat16
     )
     raw_query = jnp.dot(normalized_input, w_query, preferred_element_type=jnp.float32)
     raw_key = jnp.dot(normalized_input, key_projection_weight, preferred_element_type=jnp.float32)
-    raw_value = (
-        jnp.dot(normalized_input, value_projection_weight, preferred_element_type=jnp.float32)
-        .astype(jnp.bfloat16)
-        .astype(jnp.float32)
+    raw_value = jnp.dot(
+        normalized_input, value_projection_weight, preferred_element_type=jnp.float32
     )
-    packed = jnp.concatenate([raw_query, raw_key, raw_value], axis=1)
-
-    inverse = jnp.zeros((total_rows,), jnp.int32).at[dealing].set(
-        jnp.arange(total_rows, dtype=jnp.int32)
-    )
-    local_ids = group_index * group_rows + jnp.arange(group_rows, dtype=jnp.int32)
-    dest_group = inverse[local_ids] // group_rows
-    to_group = dest_group[None, :, None] == jnp.arange(req_count, dtype=jnp.int32)[:, None, None]
-    send_rows = jnp.where(to_group, packed[None], jnp.zeros((), jnp.float32))
-    recv_rows = lax.all_to_all(send_rows, "req", 0, 0, tiled=True)
-    recv_flat = recv_rows.reshape(req_count * group_rows, packed.shape[1])
-    dealt_ids = lax.dynamic_slice_in_dim(dealing, group_index * group_rows, group_rows)
-    mine = jnp.take(recv_flat, dealt_ids, axis=0)
+    mine = jnp.concatenate([raw_query, raw_key, raw_value], axis=1)
 
     query_vectors = mine[:, :query_width].reshape(group_rows, heads_dev * queries_per_group, head_size)
     query_vectors = (
@@ -122,8 +123,7 @@
     ).astype(jnp.bfloat16)
     send_out = jnp.dot(pick_out, attended, preferred_element_type=jnp.float32).astype(jnp.bfloat16)
     recv_out = lax.all_to_all(send_out, ("req", "kv"), 0, 0, tiled=True)
-    own_index = (group_index * kv_count + kv_index) * per_device
-    own_group = inverse[own_index] // group_rows
+    own_group = own_place // group_rows
     blocks = lax.dynamic_slice_in_dim(recv_out, own_group * kv_count, kv_count)
     return blocks.reshape(per_device, kv_count * attended.shape[1])
 

time: 88.2 us -> 81.9 us (0.929)
  blocking collectives: 16.1 us -> 0 us
  other arithmetic: 4.46 us -> 8.83 us
  starting transfers between devices: 20.7 us -> 24.9 us
  waiting for transfers between devices: 26.6 us -> 29 us
  local copies, waits for them, and re-layouts: 5.97 us -> 4.83 us
    all_gather x1 -> x0, blocking collectives: 16.1 us -> none  [local(): row_block = lax.all_gather(states, 'kv', axis=0, tiled=True)]
    all_to_all x1, waiting for transfers between devices: 14.3 us -> 6.43 us  [local(): recv_rows = lax.all_to_all(send_rows, 'req', 0, 0, tiled=True)]
    all_to_all x0 -> x1, waiting for transfers between devices: none -> 6.96 us  [local(): lax.all_to_all(jnp.broadcast_to(slot_rows[None], (kv_count,) + slot_rows....]
    all_to_all x0 -> x1, starting transfers between devices: none -> 6.86 us  [local(): lax.all_to_all(jnp.broadcast_to(slot_rows[None], (kv_count,) + slot_rows....]
    all_to_all x1, starting transfers between devices: 10.9 us -> 6.16 us  [local(): recv_out = lax.all_to_all(send_out, ('req', 'kv'), 0, 0, tiled=True)]
    all_to_all x1, waiting for transfers between devices: 12.3 us -> 15.6 us  [local(): recv_out = lax.all_to_all(send_out, ('req', 'kv'), 0, 0, tiled=True)]
    all_to_all x1, starting transfers between devices: 9.85 us -> 11.9 us  [local(): recv_rows = lax.all_to_all(send_rows, 'req', 0, 0, tiled=True)]
    reduce_sum x0 -> x2, other arithmetic: none -> 1.48 us  [the longest x1 1.44 us: local(): own_place = jnp.sum(jnp.where(dealing == own_index, places, 0))]
  transfers between devices with their start and end apart: 2 -> 3, of which waited for: 2 -> 3; matrix products, arithmetic and copies ran while one was open for 1% -> 4% of each run, Pallas kernels for 0% -> 0%
where the time goes in v12:
time: 81.9 us; the launch traced here: 81.3 us
  waiting for transfers between devices  29 us (35%)
  starting transfers between devices  24.9 us (30%)
  matrix products  11 us (13%)
  other arithmetic  8.83 us (11%)
  local copies, waits for them, and re-layouts  4.83 us (6%)
  between operations  2.74 us (3%)
    all_to_all x1, waiting for transfers between devices, local(): recv_out = lax.all_to_all(send_out, ('req', 'kv'), 0, 0, tiled=True)  15.6 us
    all_to_all x1, starting transfers between devices, local(): recv_rows = lax.all_to_all(send_rows, 'req', 0, 0, tiled=True)  11.9 us
    all_to_all x1, waiting for transfers between devices, local(): lax.all_to_all(jnp.broadcast_to(slot_rows[None], (kv_count,) + slot_rows....  6.96 us
    all_to_all x1, starting transfers between devices, local(): lax.all_to_all(jnp.broadcast_to(slot_rows[None], (kv_count,) + slot_rows....  6.86 us
    all_to_all x1, waiting for transfers between devices, local(): recv_rows = lax.all_to_all(send_rows, 'req', 0, 0, tiled=True)  6.43 us
    all_to_all x1, starting transfers between devices, local(): recv_out = lax.all_to_all(send_out, ('req', 'kv'), 0, 0, tiled=True)  6.16 us
    dot_general x1, matrix products, local(): jnp.einsum('rkgw,rkhw->rkgh', stale_weights, value_cache_slots, preferred...  3.96 us
    sub x1, matrix products, local(): expd = jnp.exp(scores - row_max)  3.66 us
  transfers between devices with their start and end apart: 3, of which 3 were waited for; matrix products, arithmetic and copies ran while one was open for 4% of the time, Pallas kernels for 0%

profile of v12, /device:TPU:1, one launch (start us, length us, event | category | flops | bytes accessed | tf_op | source)
XLA Modules:
  0.0 81.3 jit_solution(5285668791473322355)
XLA Ops:
  0.0 0.0 copy-start
  0.0 1.4 %fusion.40 = s32[]{:T(128)} fusion(s32[256]{0:T(256)} %param.19, s32[]{:T(128)S(6)} %add.37), kind=kLoop, calls=%fused_computation.62 | loop fusion | flops 767 | bytes 1032 | tf_op jit(solution)/shard_map/reduce_sum | solution.py:51
  4.1 0.7 reduce.6
  4.8 0.3 broadcast_select_fusion
  5.1 0.5 broadcast.241
  5.6 1.6 %reduce.9 = bf16[32,2560]{1,0:T(8,128)(2,1)S(1)} reduce(bf16[32,1,2560]{2,1,0:T(2,128)(2,1)S(1)} %broadcast_select_fusion, bf16[]{:T(256)} %broadcast.241), dimensions={1}, to_apply=%broadcast_select_fusion.reduce_sub_computation | reduce | bytes 327682 | tf_op jit(solution)/shard_map/jit(_where)/select_n | solution.py:53
  7.2 0.7 reshape.320
  7.9 11.9 %all-to-all-start = ((bf16[32,2,1280]{2,1,0:T(2,128)(2,1)}), bf16[32,2,1280]{2,1,0:T(2,128)(2,1)S(1)}, u32[]{:S(2)}, u32[]{:S(2)}) async-start(bf16[32,2,1280]{2,1,0:T(2,128)(2,1)} %reshape.320), calls=%async_computation | async-start | bytes 327680 | tf_op jit(solution)/shard_map/all_to_all | solution.py:54
  19.8 0.8 fusion.41
  20.5 0.7 convert_element_type.49
  21.2 0.7 convert_element_type.47
  21.9 0.8 iota_compare_fusion
  22.7 6.4 %all-to-all-done = bf16[32,2,1280]{2,1,0:T(2,128)(2,1)S(1)} async-done(((bf16[32,2,1280]{2,1,0:T(2,128)(2,1)}), bf16[32,2,1280]{2,1,0:T(2,128)(2,1)S(1)}, u32[]{:S(2)}, u32[]{:S(2)}) %all-to-all-start) | async-done | bytes 163872 | tf_op jit(solution)/shard_map/all_to_all | solution.py:54
  29.1 0.1 reshape.321
  29.3 0.6 gather_fusion
  29.9 0.1 broadcast_select_fusion.1
  29.9 0.7 broadcast_in_dim.122
  30.7 6.9 %all-to-all-start.1 = ((bf16[8,8,2560]{2,1,0:T(8,128)(2,1)}), bf16[8,8,2560]{2,1,0:T(8,128)(2,1)S(1)}, u32[]{:S(2)}, u32[]{:S(2)}) async-start(bf16[8,8,2560]{2,1,0:T(8,128)(2,1)} %broadcast_in_dim.122), calls=%async_computation.1 | async-start | bytes 655360 | tf_op jit(solution)/shard_map/all_to_all | solution.py:62
  37.6 0.1 multiply_cosine_fusion.1
  37.7 7.0 %all-to-all-done.1 = bf16[8,8,2560]{2,1,0:T(8,128)(2,1)S(1)} async-done(((bf16[8,8,2560]{2,1,0:T(8,128)(2,1)}), bf16[8,8,2560]{2,1,0:T(8,128)(2,1)S(1)}, u32[]{:S(2)}, u32[]{:S(2)}) %all-to-all-start.1) | async-done | bytes 327712 | tf_op jit(solution)/shard_map/all_to_all | solution.py:62
  44.7 0.1 multiply_reduce_fusion
  44.8 0.1 multiply_convert_fusion
  44.9 1.2 %fusion.23 = f32[8,80]{1,0:T(8,128)S(1)} fusion(bf16[8,2560]{1,0:T(8,128)(2,1)S(1)} %multiply_convert_fusion, bf16[2560,80]{0,1:T(8,128)(2,1)} %param.14), kind=kOutput, calls=%fused_computation.17 | convolution fusion | flops 3278080 | bytes 453120 | tf_op jit(solution)/shard_map/dot_general | solution.py:72
  46.1 1.2 %convolution_bitcast_fusion = f32[8,1,80]{2,0,1:T(8,128)S(1)} fusion(bf16[8,2560]{1,0:T(8,128)(2,1)S(1)} %multiply_convert_fusion, bf16[2560,80]{0,1:T(8,128)(2,1)} %param.13), kind=kOutput, calls=%fused_computation.15 | convolution fusion | flops 3276800 | bytes 453120 | tf_op jit(solution)/shard_map/dot_general | solution.py:71
  47.3 0.0 copy-done
  47.3 0.5 fusion.46
  47.9 0.1 fusion.39
  48.0 0.1 reshape.302
  48.1 0.1 maximum_bitcast_fusion
  48.2 0.1 subtract_convert_fusion
  48.2 0.2 fusion.36
  48.4 3.7 %fusion.43 = (f32[8,4]{1,0:T(8,128)S(1)}, f32[8,4,4096]{2,1,0:T(4,128)S(1)}) fusion(bf16[8,1,80,4096]{3,2,1,0:T(8,128)(2,1)} %param.15, f32[8,4]{1,0:T(8,128)S(1)} %broadcast_multiply_fusion, pred[8,4096]{1,0:T(8,128)(4,1)S(1)} %get-tuple-element.17, pred[8,4096]{1,0:T(8,128)(4,1)S(1)} %get-tuple-element.18, bf16[8,4,40]{2,1,0:T(4,128)(2,1)S(1)} %get-tuple-element.10, ...), kind=kOutput, calls=%fused_computation.68 | convolution fusion | flops 21641216 | bytes 5838080 | tf_op jit(solution)/shard_map/sub | solution.py:106
  52.1 0.4 convert_reduce_fusion.1
  52.5 4.0 %fusion.20 = bf16[8,4,80]{2,1,0:T(4,128)(2,1)S(1)} fusion(bf16[8,1,80,4096]{3,2,1,0:T(8,128)(2,1)} %param.16, bf16[8,4,4096]{2,1,0:T(4,128)(2,1)S(1)} %get-tuple-element.6, pred[8,4096]{1,0:T(8,128)(4,1)S(1)} %get-tuple-element.18, f32[8,80]{1,0:T(8,128)S(1)} %fusion.23, f32[8,4]{1,0:T(8,128)S(1)} %get-tuple-element.5), kind=kOutput, calls=%fused_computation.14 | convolution fusion | flops 21110272 | bytes 5545600 | tf_op jit(solution)/shard_map/rkgw,rkhw->rkgh/dot_general | solution.py:113
  56.4 0.1 convert_element_type.55
  56.5 0.3 fusion.16
  56.8 0.7 reduce.10
  57.5 0.2 copy.22
  57.7 0.8 %reshape.322 = bf16[256,2,160]{2,1,0:T(2,128)(2,1)} reshape(bf16[256,320]{1,0:T(8,128)(2,1)S(1)} %copy.22) | data formatting | bytes 327680
  58.5 6.2 %all-to-all-start.2 = ((bf16[256,2,160]{2,1,0:T(2,128)(2,1)}), bf16[256,2,160]{2,1,0:T(2,128)(2,1)S(1)}, u32[]{:S(2)}, u32[]{:S(2)}) async-start(bf16[256,2,160]{2,1,0:T(2,128)(2,1)} %reshape.322), calls=%async_computation.2 | async-start | bytes 524288 | tf_op jit(solution)/shard_map/all_to_all | solution.py:125
  64.7 15.6 %all-to-all-done.2 = bf16[256,2,160]{2,1,0:T(2,128)(2,1)S(1)} async-done(((bf16[256,2,160]{2,1,0:T(2,128)(2,1)}), bf16[256,2,160]{2,1,0:T(2,128)(2,1)S(1)}, u32[]{:S(2)}, u32[]{:S(2)}) %all-to-all-start.2) | async-done | bytes 163872 | tf_op jit(solution)/shard_map/all_to_all | solution.py:125
  80.3 0.3 reshape.323
  80.6 0.1 dynamic-slice_reduce_fusion
  80.6 0.7 reshape.306
  (8 shorter events, 0.1 us)
Async XLA Ops:
  0.0 47.3 %copy-start = (bf16[2560,320]{0,1:T(8,128)(2,1)S(1)}, bf16[2560,320]{0,1:T(8,128)(2,1)}, u32[]{:S(2)}) copy-start(bf16[2560,320]{0,1:T(8,128)(2,1)} %param.12) | copy-start | bytes 4915204
  7.9 21.2 %all-to-all-start = ((bf16[32,2,1280]{2,1,0:T(2,128)(2,1)}), bf16[32,2,1280]{2,1,0:T(2,128)(2,1)S(1)}, u32[]{:S(2)}, u32[]{:S(2)}) async-start(bf16[32,2,1280]{2,1,0:T(2,128)(2,1)} %reshape.320), calls=%async_computation | async-start | bytes 327680 | tf_op jit(solution)/shard_map/all_to_all | solution.py:54
  30.7 13.9 %all-to-all-start.1 = ((bf16[8,8,2560]{2,1,0:T(8,128)(2,1)}), bf16[8,8,2560]{2,1,0:T(8,128)(2,1)S(1)}, u32[]{:S(2)}, u32[]{:S(2)}) async-start(bf16[8,8,2560]{2,1,0:T(8,128)(2,1)} %broadcast_in_dim.122), calls=%async_computation.1 | async-start | bytes 655360 | tf_op jit(solution)/shard_map/all_to_all | solution.py:62
  58.5 21.8 %all-to-all-start.2 = ((bf16[256,2,160]{2,1,0:T(2,128)(2,1)}), bf16[256,2,160]{2,1,0:T(2,128)(2,1)S(1)}, u32[]{:S(2)}, u32[]{:S(2)}) async-start(bf16[256,2,160]{2,1,0:T(2,128)(2,1)} %reshape.322), calls=%async_computation.2 | async-start | bytes 524288 | tf_op jit(solution)/shard_map/all_to_all | solution.py:125

commit v13 on v6

--- a/solution.py
+++ b/solution.py
@@ -78,7 +78,7 @@
     recv_rows = lax.all_to_all(send_rows, "req", 0, 0, tiled=True)
     recv_flat = recv_rows.reshape(req_count * group_rows, packed.shape[1])
     dealt_ids = lax.dynamic_slice_in_dim(dealing, group_index * group_rows, group_rows)
-    mine = jnp.take(recv_flat, dealt_ids, axis=0)
+    mine = recv_flat.at[dealt_ids].get(mode="promise_in_bounds")
 
     query_vectors = mine[:, :query_width].reshape(group_rows, heads_dev * queries_per_group, head_size)
     query_vectors = (

time: 81.2 us -> 81.1 us (level)
  no operation moved by 1% of the time
where the time goes in v13:
time: 81.1 us; the launch traced here: 80.5 us
  waiting for transfers between devices  29.7 us (37%)
  starting transfers between devices  27 us (33%)
  matrix products  11.1 us (14%)
  other arithmetic  7.42 us (9%)
  local copies, waits for them, and re-layouts  4.54 us (6%)
    all_to_all x1, waiting for transfers between devices, local(): recv_out = lax.all_to_all(send_out, ('req', 'kv'), 0, 0, tiled=True)  14.2 us
    all_to_all x1, waiting for transfers between devices, local(): recv_rows = lax.all_to_all(send_rows, 'req', 0, 0, tiled=True)  13.9 us
    all_to_all x1, starting transfers between devices, local(): recv_rows = lax.all_to_all(send_rows, 'req', 0, 0, tiled=True)  10.5 us
    all_to_all x1, starting transfers between devices, local(): recv_out = lax.all_to_all(send_out, ('req', 'kv'), 0, 0, tiled=True)  9.98 us
    all_to_all x1, starting transfers between devices, local(): lax.all_to_all(jnp.broadcast_to(lane_rows[None], (kv_count,) + lane_rows....  6.45 us
    dot_general x1, matrix products, local(): jnp.einsum('rkgw,rkhw->rkgh', stale_weights, value_cache_slots, preferred...  3.96 us
    sub x1, matrix products, local(): expd = jnp.exp(scores - row_max)  3.66 us
  transfers between devices with their start and end apart: 3, of which 3 were waited for; matrix products, arithmetic and copies ran while one was open for 6% of the time, Pallas kernels for 0%

profile of v13, /device:TPU:1, one launch (start us, length us, event | category | flops | bytes accessed | tf_op | source)
XLA Modules:
  0.0 80.5 jit_solution(6306172427598048499)
XLA Ops:
  0.0 0.0 copy-start
  0.0 0.9 %reduce.7 = bf16[2560]{0:T(1024)(128)(2,1)S(1)} reduce(bf16[1,2560]{1,0:T(2,128)(2,1)} %param.10, bf16[]{:T(256)} %constant.60), dimensions={0}, to_apply=%param.10.reduce_sub_computation | reduce | bytes 10242 | tf_op args[0]
  0.9 0.6 broadcast_in_dim.123
  1.5 6.4 %all-to-all-start = ((bf16[8,20,128]{2,1,0:T(8,128)(2,1)}), bf16[8,20,128]{2,1,0:T(8,128)(2,1)S(1)}, u32[]{:S(2)}, u32[]{:S(2)}) async-start(bf16[8,20,128]{2,1,0:T(8,128)(2,1)} %broadcast_in_dim.123), calls=%async_computation | async-start | bytes 98304 | tf_op jit(solution)/shard_map/all_to_all | solution.py:50
  8.0 0.1 pad_add_fusion
  8.0 0.9 %select_reduce_fusion = s32[9]{0:T(128)S(1)} fusion(s32[256]{0:T(256)} %param.19, s32[9]{0:T(128)S(1)} %pad_add_fusion), kind=kLoop, calls=%fused_computation.37 | loop fusion | flops 6903 | bytes 1096 | tf_op jit(solution)/shard_map/reduce_sum | solution.py:72
  8.9 0.7 convert_element_type.63
  9.6 0.1 multiply_cosine_fusion.1
  9.7 0.8 compare_select_fusion
  10.5 0.7 convert_element_type.59
  11.2 1.6 %all-to-all-done = bf16[8,20,128]{2,1,0:T(8,128)(2,1)S(1)} async-done(((bf16[8,20,128]{2,1,0:T(8,128)(2,1)}), bf16[8,20,128]{2,1,0:T(8,128)(2,1)S(1)}, u32[]{:S(2)}, u32[]{:S(2)}) %all-to-all-start) | async-done | bytes 40992 | tf_op jit(solution)/shard_map/all_to_all | solution.py:50
  12.7 0.1 fusion.30
  12.9 0.0 copy-done
  12.9 0.5 fusion.49
  13.4 1.3 %fusion.23 = f32[8,80]{1,0:T(8,128)S(1)} fusion(bf16[2560,80]{0,1:T(8,128)(2,1)} %param.14, f32[2560]{0:T(1024)S(1)} %convert_element_type.59, f32[8]{0:T(128)S(1)} %add_rsqrt_fusion, bf16[8,20,128]{2,1,0:T(8,128)(2,1)S(1)} %all-to-all-done), kind=kOutput, calls=%fused_computation.16 | convolution fusion | flops 3360000 | bytes 463392 | tf_op jit(solution)/shard_map/dot_general | solution.py:61
  14.7 1.3 %fusion.47 = f32[8,80]{1,0:T(8,128)S(1)} fusion(bf16[2560,80]{0,1:T(8,128)(2,1)} %param.13, f32[2560]{0:T(1024)S(1)} %convert_element_type.59, f32[8]{0:T(128)S(1)} %add_rsqrt_fusion, bf16[8,20,128]{2,1,0:T(8,128)(2,1)S(1)} %all-to-all-done), kind=kOutput, calls=%fused_computation.72 | convolution fusion | flops 3358720 | bytes 463392 | tf_op jit(solution)/shard_map/dot_general | solution.py:59
  16.0 0.1 pad_maximum_fusion
  16.0 0.9 %broadcast_select_fusion = f32[32,8,480]{2,1,0:T(8,128)} fusion(f32[8,480]{1,0:T(8,128)S(1)} %pad_maximum_fusion, pred[32,8]{1,0:T(8,128)(4,1)S(1)} %iota_compare_fusion.4), kind=kLoop, calls=%fused_computation.20 | loop fusion | flops 122880 | bytes 507136 | tf_op jit(solution)/shard_map/jit(_where)/select_n | solution.py:77
  17.0 10.5 %all-to-all-start.1 = ((f32[32,8,480]{2,1,0:T(8,128)}), f32[32,8,480]{2,1,0:T(8,128)S(1)}, u32[]{:S(2)}, u32[]{:S(2)}) async-start(f32[32,8,480]{2,1,0:T(8,128)} %broadcast_select_fusion), calls=%async_computation.1 | async-start | bytes 1048576 | tf_op jit(solution)/shard_map/all_to_all | solution.py:78
  27.5 0.8 iota_compare_fusion
  28.3 13.9 %all-to-all-done.1 = f32[32,8,480]{2,1,0:T(8,128)S(1)} async-done(((f32[32,8,480]{2,1,0:T(8,128)}), f32[32,8,480]{2,1,0:T(8,128)S(1)}, u32[]{:S(2)}, u32[]{:S(2)}) %all-to-all-start.1) | async-done | bytes 491552 | tf_op jit(solution)/shard_map/all_to_all | solution.py:78
  42.2 0.6 gather_fusion
  42.7 0.1 slice_bitcast_fusion
  42.8 0.1 fusion.42
  42.9 0.1 fusion.44
  43.0 0.1 reshape.272
  43.1 0.1 maximum_bitcast_fusion
  43.1 0.1 subtract_convert_fusion
  43.2 0.2 fusion.40
  43.4 3.7 %fusion.51 = (f32[8,4]{1,0:T(8,128)S(1)}, f32[8,4,4096]{2,1,0:T(4,128)S(1)}) fusion(bf16[8,1,80,4096]{3,2,1,0:T(8,128)(2,1)} %param.15, f32[8,4]{1,0:T(8,128)S(1)} %broadcast_multiply_fusion, pred[8,4096]{1,0:T(8,128)(4,1)S(1)} %get-tuple-element.17, pred[8,4096]{1,0:T(8,128)(4,1)S(1)} %get-tuple-element.18, bf16[8,4,40]{2,1,0:T(4,128)(2,1)S(1)} %get-tuple-element.10, ...), kind=kOutput, calls=%fused_computation.74 | convolution fusion | flops 21641216 | bytes 5838080 | tf_op jit(solution)/shard_map/sub | solution.py:112
  47.1 0.4 convert_reduce_fusion
  47.5 4.0 %fusion.20 = bf16[8,4,80]{2,1,0:T(4,128)(2,1)S(1)} fusion(bf16[8,1,80,4096]{3,2,1,0:T(8,128)(2,1)} %param.16, bf16[8,4,4096]{2,1,0:T(4,128)(2,1)S(1)} %get-tuple-element.6, pred[8,4096]{1,0:T(8,128)(4,1)S(1)} %get-tuple-element.18, f32[8,80]{1,0:T(8,128)S(1)} %fusion.42, f32[8,4]{1,0:T(8,128)S(1)} %get-tuple-element.5), kind=kOutput, calls=%fused_computation.14 | convolution fusion | flops 21110272 | bytes 5545600 | tf_op jit(solution)/shard_map/rkgw,rkhw->rkgh/dot_general | solution.py:119
  51.4 0.1 convert_element_type.68
  51.5 0.3 fusion.16
  51.8 0.5 broadcast.195
  52.3 0.7 reduce.10
  53.0 0.2 copy.25
  53.2 0.8 %reshape.291 = bf16[256,2,160]{2,1,0:T(2,128)(2,1)} reshape(bf16[256,320]{1,0:T(8,128)(2,1)S(1)} %copy.25) | data formatting | bytes 327680
  54.0 10.0 %all-to-all-start.2 = ((bf16[256,2,160]{2,1,0:T(2,128)(2,1)}), bf16[256,2,160]{2,1,0:T(2,128)(2,1)S(1)}, u32[]{:S(2)}, u32[]{:S(2)}) async-start(bf16[256,2,160]{2,1,0:T(2,128)(2,1)} %reshape.291), calls=%async_computation.2 | async-start | bytes 524288 | tf_op jit(solution)/shard_map/all_to_all | solution.py:131
  64.0 0.6 slice.36
  65.2 14.2 %all-to-all-done.2 = bf16[256,2,160]{2,1,0:T(2,128)(2,1)S(1)} async-done(((bf16[256,2,160]{2,1,0:T(2,128)(2,1)}), bf16[256,2,160]{2,1,0:T(2,128)(2,1)S(1)}, u32[]{:S(2)}, u32[]{:S(2)}) %all-to-all-start.2) | async-done | bytes 163872 | tf_op jit(solution)/shard_map/all_to_all | solution.py:131
  79.5 0.3 reshape.292
  79.8 0.1 dynamic-slice_reduce_fusion
  79.8 0.7 reshape.276
  (8 shorter events, 0.1 us)
Async XLA Ops:
  0.0 12.9 %copy-start = (bf16[2560,320]{0,1:T(8,128)(2,1)S(1)}, bf16[2560,320]{0,1:T(8,128)(2,1)}, u32[]{:S(2)}) copy-start(bf16[2560,320]{0,1:T(8,128)(2,1)} %param.12) | copy-start | bytes 4915204
  1.5 11.3 %all-to-all-start = ((bf16[8,20,128]{2,1,0:T(8,128)(2,1)}), bf16[8,20,128]{2,1,0:T(8,128)(2,1)S(1)}, u32[]{:S(2)}, u32[]{:S(2)}) async-start(bf16[8,20,128]{2,1,0:T(8,128)(2,1)} %broadcast_in_dim.123), calls=%async_computation | async-start | bytes 98304 | tf_op jit(solution)/shard_map/all_to_all | solution.py:50
  17.0 25.2 %all-to-all-start.1 = ((f32[32,8,480]{2,1,0:T(8,128)}), f32[32,8,480]{2,1,0:T(8,128)S(1)}, u32[]{:S(2)}, u32[]{:S(2)}) async-start(f32[32,8,480]{2,1,0:T(8,128)} %broadcast_select_fusion), calls=%async_computation.1 | async-start | bytes 1048576 | tf_op jit(solution)/shard_map/all_to_all | solution.py:78
  54.0 25.5 %all-to-all-start.2 = ((bf16[256,2,160]{2,1,0:T(2,128)(2,1)}), bf16[256,2,160]{2,1,0:T(2,128)(2,1)S(1)}, u32[]{:S(2)}, u32[]{:S(2)}) async-start(bf16[256,2,160]{2,1,0:T(2,128)(2,1)} %reshape.291), calls=%async_computation.2 | async-start | bytes 524288 | tf_op jit(solution)/shard_map/all_to_all | solution.py:131

commit v14 on v11

--- a/solution.py
+++ b/solution.py
@@ -78,7 +78,7 @@
     recv_rows = lax.all_to_all(send_rows, "req", 0, 0, tiled=True)
     recv_flat = recv_rows.reshape(req_count * group_rows, packed.shape[1])
     dealt_ids = lax.dynamic_slice_in_dim(dealing, group_index * group_rows, group_rows)
-    mine = jnp.take(recv_flat, dealt_ids, axis=0)
+    mine = recv_flat.at[dealt_ids].get(mode="promise_in_bounds")
 
     query_vectors = mine[:, :query_width].reshape(group_rows, heads_dev * queries_per_group, head_size)
     query_vectors = (

time: 81.2 us -> 81.1 us (level)
  no operation moved by 1% of the time
where the time goes in v14:
time: 81.1 us; the launch traced here: 80.5 us
  waiting for transfers between devices  29.7 us (37%)
  starting transfers between devices  27 us (33%)
  matrix products  11.1 us (14%)
  other arithmetic  7.42 us (9%)
  local copies, waits for them, and re-layouts  4.54 us (6%)
    all_to_all x1, waiting for transfers between devices, local(): recv_out = lax.all_to_all(send_out, ('req', 'kv'), 0, 0, tiled=True)  14.2 us
    all_to_all x1, waiting for transfers between devices, local(): recv_rows = lax.all_to_all(send_rows, 'req', 0, 0, tiled=True)  13.9 us
    all_to_all x1, starting transfers between devices, local(): recv_rows = lax.all_to_all(send_rows, 'req', 0, 0, tiled=True)  10.5 us
    all_to_all x1, starting transfers between devices, local(): recv_out = lax.all_to_all(send_out, ('req', 'kv'), 0, 0, tiled=True)  9.98 us
    all_to_all x1, starting transfers between devices, local(): lax.all_to_all(jnp.broadcast_to(lane_rows[None], (kv_count,) + lane_rows....  6.45 us
    dot_general x1, matrix products, local(): jnp.einsum('rkwg,rkhw->rkgh', stale_weights, value_cache_slots, preferred...  3.96 us
    sub x1, matrix products, local(): expd = jnp.exp(scores - row_max)  3.66 us
  transfers between devices with their start and end apart: 3, of which 3 were waited for; matrix products, arithmetic and copies ran while one was open for 6% of the time, Pallas kernels for 0%

profile of v14, /device:TPU:1, one launch (start us, length us, event | category | flops | bytes accessed | tf_op | source)
XLA Modules:
  0.0 80.5 jit_solution(17512207563675206039)
XLA Ops:
  0.0 0.0 copy-start
  0.0 0.9 %reduce.7 = bf16[2560]{0:T(1024)(128)(2,1)S(1)} reduce(bf16[1,2560]{1,0:T(2,128)(2,1)} %param.10, bf16[]{:T(256)} %constant.60), dimensions={0}, to_apply=%param.10.reduce_sub_computation | reduce | bytes 10242 | tf_op args[0]
  0.9 0.6 broadcast_in_dim.126
  1.5 6.4 %all-to-all-start = ((bf16[8,20,128]{2,1,0:T(8,128)(2,1)}), bf16[8,20,128]{2,1,0:T(8,128)(2,1)S(1)}, u32[]{:S(2)}, u32[]{:S(2)}) async-start(bf16[8,20,128]{2,1,0:T(8,128)(2,1)} %broadcast_in_dim.126), calls=%async_computation | async-start | bytes 98304 | tf_op jit(solution)/shard_map/all_to_all | solution.py:50
  8.0 0.1 pad_add_fusion
  8.0 0.9 %select_reduce_fusion = s32[9]{0:T(128)S(1)} fusion(s32[256]{0:T(256)} %param.19, s32[9]{0:T(128)S(1)} %pad_add_fusion), kind=kLoop, calls=%fused_computation.38 | loop fusion | flops 6903 | bytes 1096 | tf_op jit(solution)/shard_map/reduce_sum | solution.py:72
  8.9 0.7 convert_element_type.63
  9.6 0.1 multiply_cosine_fusion.1
  9.7 0.8 compare_select_fusion
  10.5 0.7 convert_element_type.59
  11.2 1.6 %all-to-all-done = bf16[8,20,128]{2,1,0:T(8,128)(2,1)S(1)} async-done(((bf16[8,20,128]{2,1,0:T(8,128)(2,1)}), bf16[8,20,128]{2,1,0:T(8,128)(2,1)S(1)}, u32[]{:S(2)}, u32[]{:S(2)}) %all-to-all-start) | async-done | bytes 40992 | tf_op jit(solution)/shard_map/all_to_all | solution.py:50
  12.7 0.1 fusion.33
  12.9 0.0 copy-done
  12.9 0.5 fusion.52
  13.4 1.3 %fusion.26 = f32[8,80]{1,0:T(8,128)S(1)} fusion(bf16[2560,80]{0,1:T(8,128)(2,1)} %param.14, f32[2560]{0:T(1024)S(1)} %convert_element_type.59, f32[8]{0:T(128)S(1)} %add_rsqrt_fusion, bf16[8,20,128]{2,1,0:T(8,128)(2,1)S(1)} %all-to-all-done), kind=kOutput, calls=%fused_computation.17 | convolution fusion | flops 3360000 | bytes 463392 | tf_op jit(solution)/shard_map/dot_general | solution.py:61
  14.7 1.3 %fusion.50 = f32[8,80]{1,0:T(8,128)S(1)} fusion(bf16[2560,80]{0,1:T(8,128)(2,1)} %param.13, f32[2560]{0:T(1024)S(1)} %convert_element_type.59, f32[8]{0:T(128)S(1)} %add_rsqrt_fusion, bf16[8,20,128]{2,1,0:T(8,128)(2,1)S(1)} %all-to-all-done), kind=kOutput, calls=%fused_computation.73 | convolution fusion | flops 3358720 | bytes 463392 | tf_op jit(solution)/shard_map/dot_general | solution.py:59
  16.0 0.1 pad_maximum_fusion
  16.0 0.9 %broadcast_select_fusion = f32[32,8,480]{2,1,0:T(8,128)} fusion(f32[8,480]{1,0:T(8,128)S(1)} %pad_maximum_fusion, pred[32,8]{1,0:T(8,128)(4,1)S(1)} %iota_compare_fusion.4), kind=kLoop, calls=%fused_computation.21 | loop fusion | flops 122880 | bytes 507136 | tf_op jit(solution)/shard_map/jit(_where)/select_n | solution.py:77
  17.0 10.5 %all-to-all-start.1 = ((f32[32,8,480]{2,1,0:T(8,128)}), f32[32,8,480]{2,1,0:T(8,128)S(1)}, u32[]{:S(2)}, u32[]{:S(2)}) async-start(f32[32,8,480]{2,1,0:T(8,128)} %broadcast_select_fusion), calls=%async_computation.1 | async-start | bytes 1048576 | tf_op jit(solution)/shard_map/all_to_all | solution.py:78
  27.5 0.8 iota_compare_fusion
  28.3 13.9 %all-to-all-done.1 = f32[32,8,480]{2,1,0:T(8,128)S(1)} async-done(((f32[32,8,480]{2,1,0:T(8,128)}), f32[32,8,480]{2,1,0:T(8,128)S(1)}, u32[]{:S(2)}, u32[]{:S(2)}) %all-to-all-start.1) | async-done | bytes 491552 | tf_op jit(solution)/shard_map/all_to_all | solution.py:78
  42.2 0.6 gather_fusion
  42.7 0.1 slice_bitcast_fusion
  42.8 0.1 fusion.45
  42.9 0.1 fusion.47
  43.0 0.1 reshape.278
  43.1 0.1 maximum_bitcast_fusion
  43.1 0.1 subtract_convert_fusion
  43.2 0.2 fusion.43
  43.4 3.7 %fusion.54 = (f32[8,4]{1,0:T(8,128)S(1)}, f32[8,4096,4]{1,2,0:T(4,128)S(1)}) fusion(bf16[8,1,80,4096]{3,2,1,0:T(8,128)(2,1)} %param.15, f32[8,4]{1,0:T(8,128)S(1)} %broadcast_multiply_fusion, pred[8,4096]{1,0:T(8,128)(4,1)S(1)} %get-tuple-element.18, pred[8,4096]{1,0:T(8,128)(4,1)S(1)} %get-tuple-element.17, bf16[8,4,40]{2,1,0:T(4,128)(2,1)S(1)} %get-tuple-element.10, ...), kind=kOutput, calls=%fused_computation.75 | convolution fusion | flops 21641216 | bytes 5838080 | tf_op jit(solution)/shard_map/sub | solution.py:112
  47.1 0.4 convert_reduce_fusion
  47.5 4.0 %fusion.23 = bf16[8,4,80]{2,1,0:T(4,128)(2,1)S(1)} fusion(bf16[8,1,80,4096]{3,2,1,0:T(8,128)(2,1)} %param.16, bf16[8,4096,4]{1,2,0:T(4,128)(2,1)S(1)} %get-tuple-element.6, pred[8,4096]{1,0:T(8,128)(4,1)S(1)} %get-tuple-element.18, f32[8,80]{1,0:T(8,128)S(1)} %fusion.45, f32[8,4]{1,0:T(8,128)S(1)} %get-tuple-element.5), kind=kOutput, calls=%fused_computation.15 | convolution fusion | flops 21110272 | bytes 5545600 | tf_op jit(solution)/shard_map/rkwg,rkhw->rkgh/dot_general | solution.py:119
  51.4 0.1 convert_element_type.68
  51.5 0.3 fusion.19
  51.8 0.5 broadcast.210
  52.3 0.7 reduce.10
  53.0 0.2 copy.25
  53.2 0.8 %reshape.297 = bf16[256,2,160]{2,1,0:T(2,128)(2,1)} reshape(bf16[256,320]{1,0:T(8,128)(2,1)S(1)} %copy.25) | data formatting | bytes 327680
  54.0 10.0 %all-to-all-start.2 = ((bf16[256,2,160]{2,1,0:T(2,128)(2,1)}), bf16[256,2,160]{2,1,0:T(2,128)(2,1)S(1)}, u32[]{:S(2)}, u32[]{:S(2)}) async-start(bf16[256,2,160]{2,1,0:T(2,128)(2,1)} %reshape.297), calls=%async_computation.2 | async-start | bytes 524288 | tf_op jit(solution)/shard_map/all_to_all | solution.py:131
  64.0 0.6 slice.36
  65.2 14.2 %all-to-all-done.2 = bf16[256,2,160]{2,1,0:T(2,128)(2,1)S(1)} async-done(((bf16[256,2,160]{2,1,0:T(2,128)(2,1)}), bf16[256,2,160]{2,1,0:T(2,128)(2,1)S(1)}, u32[]{:S(2)}, u32[]{:S(2)}) %all-to-all-start.2) | async-done | bytes 163872 | tf_op jit(solution)/shard_map/all_to_all | solution.py:131
  79.5 0.3 reshape.298
  79.8 0.1 dynamic-slice_reduce_fusion
  79.8 0.7 reshape.282
  (8 shorter events, 0.1 us)
Async XLA Ops:
  0.0 12.9 %copy-start = (bf16[2560,320]{0,1:T(8,128)(2,1)S(1)}, bf16[2560,320]{0,1:T(8,128)(2,1)}, u32[]{:S(2)}) copy-start(bf16[2560,320]{0,1:T(8,128)(2,1)} %param.12) | copy-start | bytes 4915204
  1.5 11.3 %all-to-all-start = ((bf16[8,20,128]{2,1,0:T(8,128)(2,1)}), bf16[8,20,128]{2,1,0:T(8,128)(2,1)S(1)}, u32[]{:S(2)}, u32[]{:S(2)}) async-start(bf16[8,20,128]{2,1,0:T(8,128)(2,1)} %broadcast_in_dim.126), calls=%async_computation | async-start | bytes 98304 | tf_op jit(solution)/shard_map/all_to_all | solution.py:50
  17.0 25.2 %all-to-all-start.1 = ((f32[32,8,480]{2,1,0:T(8,128)}), f32[32,8,480]{2,1,0:T(8,128)S(1)}, u32[]{:S(2)}, u32[]{:S(2)}) async-start(f32[32,8,480]{2,1,0:T(8,128)} %broadcast_select_fusion), calls=%async_computation.1 | async-start | bytes 1048576 | tf_op jit(solution)/shard_map/all_to_all | solution.py:78
  54.0 25.5 %all-to-all-start.2 = ((bf16[256,2,160]{2,1,0:T(2,128)(2,1)}), bf16[256,2,160]{2,1,0:T(2,128)(2,1)S(1)}, u32[]{:S(2)}, u32[]{:S(2)}) async-start(bf16[256,2,160]{2,1,0:T(2,128)(2,1)} %reshape.297), calls=%async_computation.2 | async-start | bytes 524288 | tf_op jit(solution)/shard_map/all_to_all | solution.py:131
